TPU v7x, 256 devices: a whole 4x4x8 slice. The times are simulated.
256 devices in a mesh: scene: 16 (over y, z_hi), seq: 16 (over z_lo, x, core).
Axes of the slice: x: 4, y: 4, z: 8 (z_hi: 4, z_lo: 2; z = z_hi * 2 + z_lo), core: 2. Of those that a mesh axis runs over, the one named last changes fastest.
Arguments:
- scene_x: bfloat16 [16, 65536, 256], P('scene', 'seq'), may hold values from -6 to 6
- cotangent: bfloat16 [16, 65536, 256], P('scene', 'seq'), may hold values from -6 to 6
- gate_gain: float32 [256], replicated, may hold values from 0.3 to 3
- kernel: bfloat16 [256, 256, 256], P(None, 'seq'), may hold values from -6 to 6
- block_mix: bfloat16 [256, 256], replicated, may hold values from -0.375 to 0.375
- across_mix: bfloat16 [256, 256], replicated, may hold values from -0.375 to 0.375
- across_unmix: bfloat16 [256, 256], replicated, may hold values from -0.375 to 0.375
- block_unmix: bfloat16 [256, 256], replicated, may hold values from -0.375 to 0.375
Outputs:
- mixed: bfloat16 [16, 65536, 256], P('scene', 'seq')
- grad_x: bfloat16 [16, 65536, 256], P('scene', 'seq')
- grad_kernel: float32 [256, 256, 256], P('scene', 'seq')
- grad_gain: float32 [256], replicated
All inputs are finite; a program needn't handle non-finite values.
Results may differ from a plain program's by a relative error of at most 0.007.
Values may be sent and summed in bfloat16 or wider, within the bound.
No kernel may reach another device: no remote copies, remote signals or barrier semaphores. Data moves between devices by JAX's collectives and lax.ppermute only.
A program may use at most 128 MiB of HBM per device.

v0:
```python
import jax
import jax.numpy as jnp
from jax import lax
from jax.sharding import PartitionSpec as P


def on_device(
    scene_x, cotangent, gate_gain, kernel, block_mix, across_mix, across_unmix, block_unmix
):
    f32 = jnp.float32
    bf16 = jnp.bfloat16
    scenes_here, row_count, channels = scene_x.shape
    block_len = block_mix.shape[0]
    local_a = row_count // block_len
    kernel_f = kernel.astype(f32)
    inputs = scene_x.reshape(scenes_here, local_a, block_len, channels)
    first_mix = jnp.einsum("jb,sabc->sajc", block_mix, inputs, preferred_element_type=f32).astype(
        bf16
    )
    spread_mix = lax.all_to_all(first_mix, "seq", split_axis=2, concat_axis=1, tiled=True)
    second_mix = jnp.einsum(
        "ia,sajc->sijc", across_mix, spread_mix, preferred_element_type=f32
    ).astype(bf16)
    weighted = (second_mix.astype(f32) * kernel_f).astype(bf16)
    unmixed = jnp.einsum(
        "pi,sijc->spjc", across_unmix, weighted, preferred_element_type=f32
    ).astype(bf16)
    returned = lax.all_to_all(unmixed, "seq", split_axis=1, concat_axis=2, tiled=True)
    values = jnp.einsum("qj,spjc->spqc", block_unmix, returned, preferred_element_type=f32)
    gate_pre = inputs.astype(f32) * gate_gain
    gate_sig = jax.nn.sigmoid(gate_pre)
    mixed_out = (
        (values * gate_pre * gate_sig).astype(bf16).reshape(scenes_here, row_count, channels)
    )
    upstream = cotangent.reshape(scenes_here, local_a, block_len, channels).astype(f32)
    grad_values = (upstream * gate_pre * gate_sig).astype(bf16)
    grad_gate = upstream * values * gate_sig * (1.0 + gate_pre * (1.0 - gate_sig))
    grad_unmixed = jnp.einsum(
        "qj,spqc->spjc", block_unmix, grad_values, preferred_element_type=f32
    ).astype(bf16)
    spread_grad = lax.all_to_all(grad_unmixed, "seq", split_axis=2, concat_axis=1, tiled=True)
    grad_weighted = jnp.einsum(
        "pi,spjc->sijc", across_unmix, spread_grad, preferred_element_type=f32
    )
    kernel_term = jnp.sum(grad_weighted * second_mix.astype(f32), axis=0)
    kernel_grad = lax.psum_scatter(kernel_term, "scene", scatter_dimension=0, tiled=True)
    grad_second = (grad_weighted * kernel_f).astype(bf16)
    grad_first = jnp.einsum(
        "ia,sijc->sajc", across_mix, grad_second, preferred_element_type=f32
    ).astype(bf16)
    grad_back = lax.all_to_all(grad_first, "seq", split_axis=1, concat_axis=2, tiled=True)
    grad_input = (
        jnp.einsum("jb,sajc->sabc", block_mix, grad_back, preferred_element_type=f32)
        + grad_gate * gate_gain
    )
    grad_input = grad_input.astype(bf16).reshape(scenes_here, row_count, channels)
    gain_term = jnp.sum(inputs.astype(f32) * grad_gate, axis=(0, 1, 2))
    gain_total = lax.psum(gain_term, ("scene", "seq"))
    total_rows = scenes_here * lax.axis_size("scene") * local_a * lax.axis_size("seq") * block_len
    grad_scale = 1.0 / jnp.sqrt(jnp.float32(total_rows))
    return (mixed_out, grad_input, kernel_grad, gain_total * grad_scale)


def solution(mesh):
    return jax.shard_map(
        on_device,
        mesh=mesh,
        in_specs=(
            P("scene", "seq", None),
            P("scene", "seq", None),
            P(),
            P(None, "seq", None),
            P(),
            P(),
            P(),
            P(),
        ),
        out_specs=(P("scene", "seq", None), P("scene", "seq", None), P("scene", "seq", None), P()),
        check_vma=False,
    )
```

profile of v0, /device:TPU:1, one launch (start us, length us, event | category | flops | bytes accessed | tf_op | source)
XLA Modules:
  0.0 281.6 jit_solution(17763689708020302896)
XLA Ops:
  7.2 0.0 copy-start
  7.2 2.4 convert_bitcast_fusion.4
  9.6 3.1 %copy.39 = bf16[1,16,256,256]{3,1,0,2:T(8,128)(2,1)} copy(bf16[1,16,256,256]{2,3,1,0:T(8,128)(2,1)S(1)} %convert_bitcast_fusion.4) | data formatting | bytes 4194304 | tf_op jit(solution)/shard_map/convert_element_type | solution.py:17
  12.6 7.5 %all-to-all-start = ((bf16[1,16,256,256]{3,1,0,2:T(8,128)(2,1)}), bf16[1,16,256,256]{3,1,0,2:T(8,128)(2,1)}, u32[]{:S(2)}, u32[]{:S(2)}) async-start(bf16[1,16,256,256]{3,1,0,2:T(8,128)(2,1)} %copy.39), calls=%async_computation | async-start | bytes 4194304 | tf_op jit(solution)/shard_map/all_to_all | solution.py:20
  20.1 0.0 copy-done.2
  20.2 2.4 copy.46
  22.5 3.9 %convert_element_type.152 = f32[1,4096,256]{2,1,0:T(8,128)} convert(bf16[1,4096,256]{2,1,0:T(8,128)(2,1)} %param.9) | non-fusion elementwise | flops 1048576 | bytes 6291456 | tf_op jit(solution)/shard_map/convert_element_type | solution.py:35
  26.4 5.5 %copy.47 = f32[16,256,256]{1,2,0:T(8,128)} copy(f32[16,256,256]{2,1,0:T(8,128)} %bitcast.143) | data formatting | bytes 8388608 | tf_op jit(solution)/shard_map/convert_element_type | solution.py:35
  32.0 0.0 copy-done
  32.0 4.9 %convert_bitcast_fusion.2 = bf16[1,16,256,256]{2,3,1,0:T(8,128)(2,1)} fusion(f32[16,256,256]{1,2,0:T(8,128)} %copy.47, bf16[16,256,256]{1,2,0:T(8,128)(2,1)S(1)} %copy-done.10, f32[256]{0:T(256)S(1)} %copy-done.14, bf16[256,256]{1,0:T(8,128)(2,1)S(1)} %copy-done), kind=kOutput, calls=%fused_computation.37 | convolution fusion | flops 546308096 | bytes 8520704 | tf_op jit(solution)/shard_map/qj,spqc->spjc/dot_general | solution.py:38
  36.9 4.6 %copy.48 = bf16[1,16,256,256]{3,1,0,2:T(8,128)(2,1)} copy(bf16[1,16,256,256]{2,3,1,0:T(8,128)(2,1)} %convert_bitcast_fusion.2) | data formatting | bytes 4194304 | tf_op jit(solution)/shard_map/convert_element_type | solution.py:40
  41.5 6.5 %all-to-all-done = bf16[1,16,256,256]{3,1,0,2:T(8,128)(2,1)} async-done(((bf16[1,16,256,256]{3,1,0,2:T(8,128)(2,1)}), bf16[1,16,256,256]{3,1,0,2:T(8,128)(2,1)}, u32[]{:S(2)}, u32[]{:S(2)}) %all-to-all-start) | async-done | bytes 2097184 | tf_op jit(solution)/shard_map/all_to_all | solution.py:20
  48.0 6.0 %all-to-all-start.2 = ((bf16[1,16,256,256]{3,1,0,2:T(8,128)(2,1)}), bf16[1,16,256,256]{3,1,0,2:T(8,128)(2,1)}, u32[]{:S(2)}, u32[]{:S(2)}) async-start(bf16[1,16,256,256]{3,1,0,2:T(8,128)(2,1)} %copy.48), calls=%async_computation.2 | async-start | bytes 4194304 | tf_op jit(solution)/shard_map/all_to_all | solution.py:41
  54.0 2.7 copy.43
  56.7 2.3 copy.40
  59.0 0.0 copy-start.11
  59.1 0.2 copy.41
  59.3 0.7 copy-done.11
  60.0 1.7 fusion.31
  61.6 2.1 convert_bitcast_fusion.3
  63.8 4.6 %copy.44 = bf16[1,256,16,256]{3,2,0,1:T(8,128)(2,1)} copy(bf16[1,256,16,256]{1,3,2,0:T(8,128)(2,1)} %convert_bitcast_fusion.3) | data formatting | bytes 4194304 | tf_op jit(solution)/shard_map/convert_element_type | solution.py:27
  68.3 13.4 %all-to-all-done.2 = bf16[1,16,256,256]{3,1,0,2:T(8,128)(2,1)} async-done(((bf16[1,16,256,256]{3,1,0,2:T(8,128)(2,1)}), bf16[1,16,256,256]{3,1,0,2:T(8,128)(2,1)}, u32[]{:S(2)}, u32[]{:S(2)}) %all-to-all-start.2) | async-done | bytes 2097184 | tf_op jit(solution)/shard_map/all_to_all | solution.py:41
  81.7 6.3 %all-to-all-start.1 = ((bf16[1,256,16,256]{3,2,0,1:T(8,128)(2,1)}), bf16[1,256,16,256]{3,2,0,1:T(8,128)(2,1)}, u32[]{:S(2)}, u32[]{:S(2)}) async-start(bf16[1,256,16,256]{3,2,0,1:T(8,128)(2,1)} %copy.44), calls=%async_computation.1 | async-start | bytes 4194304 | tf_op jit(solution)/shard_map/all_to_all | solution.py:28
  88.0 0.2 reduce-scatter.2.cloned.1.call-start
  88.2 2.3 copy.49
  90.5 0.2 copy.50
  90.7 1.7 fusion.26
  92.4 2.0 copy-done.1
  94.4 2.5 fusion.15
  96.8 5.5 %copy.55 = f32[256,16,256]{2,1,0:T(8,128)} copy(f32[256,16,256]{0,2,1:T(8,128)} %fusion.15) | data formatting | bytes 8388608 | tf_op jit(solution)/shard_map/reduce_sum | solution.py:45
  102.3 0.0 reduce-scatter.2.cloned.1.call-update
  102.4 1.6 copy-done.5
  103.9 4.2 %convert_bitcast_fusion.1 = bf16[1,256,16,256]{1,3,2,0:T(8,128)(2,1)} fusion(f32[16,256,256]{2,1,0:T(8,128)} %copy-done.1, bf16[256,16,256]{0,2,1:T(8,128)(2,1)S(1)} %copy-done.5, bf16[256,256]{1,0:T(8,128)(2,1)S(1)} %copy-done.11), kind=kOutput, calls=%fused_computation.36 | convolution fusion | flops 541065216 | bytes 8519680 | tf_op jit(solution)/shard_map/ia,sijc->sajc/dot_general | solution.py:48
  108.1 4.5 %copy.52 = bf16[1,256,16,256]{3,2,0,1:T(8,128)(2,1)} copy(bf16[1,256,16,256]{1,3,2,0:T(8,128)(2,1)} %convert_bitcast_fusion.1) | data formatting | bytes 4194304 | tf_op jit(solution)/shard_map/convert_element_type | solution.py:50
  112.6 3.0 %all-to-all-done.1 = bf16[1,256,16,256]{3,2,0,1:T(8,128)(2,1)} async-done(((bf16[1,256,16,256]{3,2,0,1:T(8,128)(2,1)}), bf16[1,256,16,256]{3,2,0,1:T(8,128)(2,1)}, u32[]{:S(2)}, u32[]{:S(2)}) %all-to-all-start.1) | async-done | bytes 2097184 | tf_op jit(solution)/shard_map/all_to_all | solution.py:28
  115.7 6.3 %all-to-all-start.3 = ((bf16[1,256,16,256]{3,2,0,1:T(8,128)(2,1)}), bf16[1,256,16,256]{3,2,0,1:T(8,128)(2,1)S(1)}, u32[]{:S(2)}, u32[]{:S(2)}) async-start(bf16[1,256,16,256]{3,2,0,1:T(8,128)(2,1)} %copy.52), calls=%async_computation.3 | async-start | bytes 4194304 | tf_op jit(solution)/shard_map/all_to_all | solution.py:51
  121.9 3.2 %copy.45 = bf16[1,16,16,16,256]{4,3,2,1,0:T(8,128)(2,1)} copy(bf16[1,16,16,16,256]{4,3,1,2,0:T(8,128)(2,1)} %bitcast.16) | data formatting | bytes 4194304 | tf_op jit(solution)/shard_map/all_to_all | solution.py:28
  125.1 54.0 %all-to-all-done.3 = bf16[1,256,16,256]{3,2,0,1:T(8,128)(2,1)S(1)} async-done(((bf16[1,256,16,256]{3,2,0,1:T(8,128)(2,1)}), bf16[1,256,16,256]{3,2,0,1:T(8,128)(2,1)S(1)}, u32[]{:S(2)}, u32[]{:S(2)}) %all-to-all-start.3) | async-done | bytes 2097184 | tf_op jit(solution)/shard_map/all_to_all | solution.py:51
  179.1 1.3 copy-done.7
  180.4 2.0 copy.53
  182.4 0.3 copy-done.3
  182.6 0.6 copy-done.9
  183.3 5.0 %fusion.11 = (f32[1,16,256,256]{3,2,1,0:T(8,128)S(1)}, bf16[1,16,256,256]{3,2,1,0:T(8,128)(2,1)}) fusion(f32[1,16,256,256]{3,2,1,0:T(8,128)} %bitcast.144, f32[256]{0:T(256)S(1)} %copy-done.14, bf16[1,4096,256]{2,1,0:T(8,128)(2,1)S(1)} %copy-done.3, bf16[16,256,256]{2,1,0:T(8,128)(2,1)S(1)} %bitcast.152, bf16[256,256]{1,0:T(8,128)(2,1)S(1)} %copy-done), kind=kOutput, calls=%fused_computation.15 | convolution fusion | flops 551550976 | bytes 14812160 | tf_op jit(solution)/shard_map/qj,spjc->spqc/dot_general | solution.py:29
  188.3 2.0 copy-done.6
  190.2 0.7 fusion.12
  190.9 78.8 %psum.7 = f32[256]{0:T(256)S(1)} all-reduce(f32[256]{0:T(256)S(1)} %fusion.12), channel_id=1, replica_groups=mesh['scene'=16,'seq'=16] {'scene','seq'}, use_global_device_ids=true, to_apply=%region_2.0 | all-reduce | flops 256 | bytes 2048 | tf_op jit(solution)/shard_map/psum | solution.py:58
  269.7 0.6 broadcast_multiply_fusion
  270.3 4.5 %fusion.13 = bf16[1,16,256,256]{3,2,1,0:T(8,128)(2,1)} fusion(f32[1,16,256,256]{3,2,1,0:T(8,128)} %copy-done.6, bf16[16,256,256]{2,1,0:T(8,128)(2,1)S(1)} %bitcast.145, f32[256]{0:T(256)S(1)} %copy-done.14, bf16[256,256]{1,0:T(8,128)(2,1)S(1)} %copy-done.12), kind=kOutput, calls=%fused_computation.18 | convolution fusion | flops 540016640 | bytes 8520704 | tf_op jit(solution)/shard_map/jb,sajc->sabc/dot_general | solution.py:53
  (20 shorter events, 0.0 us)
Async XLA Ops:
  7.2 24.8 %copy-start = (bf16[256,256]{1,0:T(8,128)(2,1)S(1)}, bf16[256,256]{1,0:T(8,128)(2,1)}, u32[]{:S(2)}) copy-start(bf16[256,256]{1,0:T(8,128)(2,1)} %param.15) | copy-start | bytes 393220
  12.6 7.5 %copy-start.2 = (bf16[1,4096,256]{2,1,0:T(8,128)(2,1)S(1)}, bf16[1,4096,256]{2,1,0:T(8,128)(2,1)}, u32[]{:S(2)}) copy-start(bf16[1,4096,256]{2,1,0:T(8,128)(2,1)} %param.8) | copy-start | bytes 6291460
  12.6 35.3 %all-to-all-start = ((bf16[1,16,256,256]{3,1,0,2:T(8,128)(2,1)}), bf16[1,16,256,256]{3,1,0,2:T(8,128)(2,1)}, u32[]{:S(2)}, u32[]{:S(2)}) async-start(bf16[1,16,256,256]{3,1,0,2:T(8,128)(2,1)} %copy.39), calls=%async_computation | async-start | bytes 4194304 | tf_op jit(solution)/shard_map/all_to_all | solution.py:20
  26.4 5.6 %copy-start.10 = (bf16[16,256,256]{1,2,0:T(8,128)(2,1)S(1)}, bf16[16,256,256]{1,2,0:T(8,128)(2,1)}, u32[]{:S(2)}) copy-start(bf16[16,256,256]{1,2,0:T(8,128)(2,1)} %copy.46) | copy-start | bytes 6291460
  26.4 5.6 %copy-start.14 = (f32[256]{0:T(256)S(1)}, f32[256]{0:T(256)}, u32[]{:S(2)}) copy-start(f32[256]{0:T(256)} %param.10) | copy-start | bytes 3076
  41.5 12.5 %copy-start.8 = (bf16[256,16,256]{2,1,0:T(8,128)(2,1)S(1)}, bf16[256,16,256]{2,1,0:T(8,128)(2,1)}, u32[]{:S(2)}) copy-start(bf16[256,16,256]{2,1,0:T(8,128)(2,1)} %param.11) | copy-start | bytes 6291460
  48.0 33.7 %all-to-all-start.2 = ((bf16[1,16,256,256]{3,1,0,2:T(8,128)(2,1)}), bf16[1,16,256,256]{3,1,0,2:T(8,128)(2,1)}, u32[]{:S(2)}, u32[]{:S(2)}) async-start(bf16[1,16,256,256]{3,1,0,2:T(8,128)(2,1)} %copy.48), calls=%async_computation.2 | async-start | bytes 4194304 | tf_op jit(solution)/shard_map/all_to_all | solution.py:41
  59.0 0.9 copy-start.11
  59.9 1.7 copy-start.4
  60.0 1.7 copy-start.13
  81.7 34.0 %all-to-all-start.1 = ((bf16[1,256,16,256]{3,2,0,1:T(8,128)(2,1)}), bf16[1,256,16,256]{3,2,0,1:T(8,128)(2,1)}, u32[]{:S(2)}, u32[]{:S(2)}) async-start(bf16[1,256,16,256]{3,2,0,1:T(8,128)(2,1)} %copy.44), calls=%async_computation.1 | async-start | bytes 4194304 | tf_op jit(solution)/shard_map/all_to_all | solution.py:28
  88.0 186.8 %reduce-scatter.2.cloned.1.call-start = ((), (), s32[]{:S(2)}) async-start(), calls=%async_computation.5 | async-start | bytes 4456448 | tf_op jit(solution)/shard_map/reduce_scatter | solution.py:46
  92.4 2.0 copy-start.1
  102.3 1.6 copy-start.5
  115.7 63.4 %all-to-all-start.3 = ((bf16[1,256,16,256]{3,2,0,1:T(8,128)(2,1)}), bf16[1,256,16,256]{3,2,0,1:T(8,128)(2,1)S(1)}, u32[]{:S(2)}, u32[]{:S(2)}) async-start(bf16[1,256,16,256]{3,2,0,1:T(8,128)(2,1)} %copy.52), calls=%async_computation.3 | async-start | bytes 4194304 | tf_op jit(solution)/shard_map/all_to_all | solution.py:51
  179.1 1.3 copy-start.7
  180.4 2.2 copy-start.3
  180.4 2.9 %copy-start.9 = (bf16[1,16,16,16,256]{4,3,2,1,0:T(8,128)(2,1)S(1)}, bf16[1,16,16,16,256]{4,3,2,1,0:T(8,128)(2,1)}, u32[]{:S(2)}) copy-start(bf16[1,16,16,16,256]{4,3,2,1,0:T(8,128)(2,1)} %copy.45) | copy-start | bytes 6291460
  188.3 2.0 copy-start.6
  190.2 80.1 %copy-start.12 = (bf16[256,256]{1,0:T(8,128)(2,1)S(1)}, bf16[256,256]{1,0:T(8,128)(2,1)}, u32[]{:S(2)}) copy-start(bf16[256,256]{1,0:T(8,128)(2,1)} %param.12) | copy-start | bytes 393220
Sparse Core Ops, SparseCore 0:
  102.5 100.8 reduce-scatter.1
where the time goes:
time: 283 us; the launch traced here: 282 us
  blocking collectives  78.8 us (28%)
  waiting for transfers between devices  76.9 us (27%)
  local copies, waits for them, and re-layouts  51.5 us (18%)
  matrix products  26.4 us (9%)
  starting transfers between devices  26.2 us (9%)
  between operations  14.2 us (5%)
  other arithmetic  7.59 us (3%)
    psum x1, blocking collectives, on_device(): gain_total = lax.psum(gain_term, ('scene', 'seq'))  78.8 us
    all_to_all x1, waiting for transfers between devices, on_device(): lax.all_to_all(grad_first, 'seq', split_axis=1, concat_axis=2, tiled=True)  54 us
    all_to_all x1, waiting for transfers between devices, on_device(): lax.all_to_all(grad_unmixed, 'seq', split_axis=2, concat_axis=1, tiled=True)  13.4 us
    unnamed x31, local copies, waits for them, and re-layouts  11.2 us
    all_to_all x1, starting transfers between devices, on_device(): lax.all_to_all(first_mix, 'seq', split_axis=2, concat_axis=1, tiled=True)  7.5 us
    all_to_all x1, waiting for transfers between devices, on_device(): lax.all_to_all(first_mix, 'seq', split_axis=2, concat_axis=1, tiled=True)  6.49 us
    all_to_all x1, starting transfers between devices, on_device(): lax.all_to_all(grad_first, 'seq', split_axis=1, concat_axis=2, tiled=True)  6.26 us
    all_to_all x1, starting transfers between devices, on_device(): lax.all_to_all(unmixed, 'seq', split_axis=1, concat_axis=2, tiled=True)  6.26 us
  transfers between devices with their start and end apart: 5, of which 4 were waited for; matrix products, arithmetic and copies ran while one was open for 25% of the time, Pallas kernels for 0%

commit v1 on v0

v1 whole, which is shorter than its diff:
```python
import jax
import jax.numpy as jnp
from jax import lax
from jax.sharding import PartitionSpec as P


def on_device(
    scene_x, cotangent, gate_gain, kernel, block_mix, across_mix, across_unmix, block_unmix
):
    f32 = jnp.float32
    bf16 = jnp.bfloat16
    scenes_here, row_count, channels = scene_x.shape
    block_len = block_mix.shape[0]
    local_a = row_count // block_len
    parts = lax.axis_size("seq")
    chunk = block_len // parts
    kernel_f = kernel.astype(f32)

    inputs = scene_x.reshape(scenes_here, local_a, block_len, channels)
    upstream = cotangent.reshape(scenes_here, local_a, block_len, channels).astype(f32)
    gate_pre = inputs.astype(f32) * gate_gain
    gate_sig = jax.nn.sigmoid(gate_pre)
    gate = gate_pre * gate_sig
    grad_values = (upstream * gate).astype(bf16)
    mix_by_dest = block_mix.reshape(parts, chunk, block_len)
    unmix_by_dest = block_unmix.reshape(block_len, parts, chunk)
    first_mix = jnp.einsum(
        "Jjb,sabc->Jsajc", mix_by_dest, inputs, preferred_element_type=f32
    ).astype(bf16)
    grad_unmixed = jnp.einsum(
        "qJj,saqc->Jsajc", unmix_by_dest, grad_values, preferred_element_type=f32
    ).astype(bf16)
    outgoing = jnp.stack([first_mix, grad_unmixed], axis=1)
    incoming = lax.all_to_all(outgoing, "seq", split_axis=0, concat_axis=0, tiled=True)
    incoming = jnp.moveaxis(incoming, 2, 1)
    spread_mix = incoming[:, :, 0].reshape(parts, scenes_here, local_a, chunk, channels)
    spread_grad = incoming[:, :, 1].reshape(parts, scenes_here, local_a, chunk, channels)
    spread_mix = jnp.moveaxis(spread_mix, 1, 0).reshape(scenes_here, parts * local_a, chunk, channels)
    spread_grad = jnp.moveaxis(spread_grad, 1, 0).reshape(
        scenes_here, parts * local_a, chunk, channels
    )

    second_mix = jnp.einsum(
        "ia,sajc->sijc", across_mix, spread_mix, preferred_element_type=f32
    ).astype(bf16)
    weighted = (second_mix.astype(f32) * kernel_f).astype(bf16)
    unmixed = jnp.einsum(
        "pi,sijc->spjc", across_unmix, weighted, preferred_element_type=f32
    ).astype(bf16)
    grad_weighted = jnp.einsum(
        "pi,spjc->sijc", across_unmix, spread_grad, preferred_element_type=f32
    )
    kernel_term = jnp.sum(grad_weighted * second_mix.astype(f32), axis=0)
    kernel_grad = lax.psum_scatter(kernel_term, "scene", scatter_dimension=0, tiled=True)
    grad_second = (grad_weighted * kernel_f).astype(bf16)
    grad_first = jnp.einsum(
        "ia,sijc->sajc", across_mix, grad_second, preferred_element_type=f32
    ).astype(bf16)
    back = jnp.stack(
        [
            unmixed.reshape(scenes_here, parts, local_a, chunk, channels),
            grad_first.reshape(scenes_here, parts, local_a, chunk, channels),
        ],
        axis=2,
    )
    back = jnp.moveaxis(back, 1, 0)
    returned = lax.all_to_all(back, "seq", split_axis=0, concat_axis=0, tiled=True)
    values = jnp.einsum(
        "qJj,Jsajc->saqc",
        unmix_by_dest,
        returned[:, :, 0],
        preferred_element_type=f32,
    )
    mixed_out = (values * gate).astype(bf16).reshape(scenes_here, row_count, channels)
    grad_gate = upstream * values * gate_sig * (1.0 + gate_pre * (1.0 - gate_sig))
    grad_input = (
        jnp.einsum("Jjb,Jsajc->sabc", mix_by_dest, returned[:, :, 1], preferred_element_type=f32)
        + grad_gate * gate_gain
    )
    grad_input = grad_input.astype(bf16).reshape(scenes_here, row_count, channels)
    gain_term = jnp.sum(inputs.astype(f32) * grad_gate, axis=(0, 1, 2))
    gain_total = lax.psum(gain_term, ("scene", "seq"))
    total_rows = scenes_here * lax.axis_size("scene") * local_a * parts * block_len
    grad_scale = 1.0 / jnp.sqrt(jnp.float32(total_rows))
    return (mixed_out, grad_input, kernel_grad, gain_total * grad_scale)


def solution(mesh):
    return jax.shard_map(
        on_device,
        mesh=mesh,
        in_specs=(
            P("scene", "seq", None),
            P("scene", "seq", None),
            P(),
            P(None, "seq", None),
            P(),
            P(),
            P(),
            P(),
        ),
        out_specs=(P("scene", "seq", None), P("scene", "seq", None), P("scene", "seq", None), P()),
        check_vma=False,
    )
```

time: 283 us -> 297 us (1.049)
  waiting for transfers between devices: 76.9 us -> 125 us
  local copies, waits for them, and re-layouts: 51.5 us -> 25.3 us
  matrix products: 26.4 us -> 16.7 us
  blocking collectives: 78.8 us -> 86.4 us
  starting transfers between devices: 26.2 us -> 19.6 us
    all_to_all x4 -> x2, waiting for transfers between devices: 76.9 us -> 125 us  [the longest x1 73.7 us: on_device(): lax.all_to_all(back, 'seq', split_axis=0, concat_axis=0, tiled=True)]
    convert_element_type x5 -> x0, local copies, waits for them, and re-layouts: 22.3 us -> none  [the longest x1 5.55 us: on_device(): cotangent.reshape(scenes_here, local_a, block_len, channels).astype(f32)]
    psum x1, blocking collectives: 78.8 us -> 86.4 us  [on_device(): gain_total = lax.psum(gain_term, ('scene', 'seq'))]
    all_to_all x6 -> x1, local copies, waits for them, and re-layouts: 10.1 us -> 2.64 us  [on_device(): lax.all_to_all(outgoing, 'seq', split_axis=0, concat_axis=0, tiled=True)]
    all_to_all x4 -> x2, starting transfers between devices: 26 us -> 19.6 us  [the longest x1 12 us: on_device(): lax.all_to_all(back, 'seq', split_axis=0, concat_axis=0, tiled=True)]
    another operation x0 -> x3, local copies, waits for them, and re-layouts: none -> 4.9 us  [the longest x1 2.54 us: on_device(): outgoing = jnp.stack([first_mix, grad_unmixed], axis=1)]
    dot_general x4, matrix products: 16.8 us -> 11.9 us  [the longest x1 5.09 us: on_device(): jnp.einsum('Jjb,Jsajc->sabc', mix_by_dest, returned[:, :, 1], preferred_e...]
    slice x0 -> x2, local copies, waits for them, and re-layouts: none -> 4.38 us  [the longest x1 4.07 us: on_device(): returned[:, :, 1]]
  transfers between devices with their start and end apart: 5 -> 3, of which waited for: 4 -> 2; matrix products, arithmetic and copies ran while one was open for 25% -> 9% of each run, Pallas kernels for 0% -> 0%
where the time goes in v1:
time: 297 us
  waiting for transfers between devices  125 us (42%)
  blocking collectives  86.4 us (29%)
  local copies, waits for them, and re-layouts  25.3 us (9%)
  starting transfers between devices  19.6 us (7%)
  matrix products  16.7 us (6%)
  between operations  14.2 us (5%)
  other arithmetic  9.95 us (3%)
    psum x1, blocking collectives, on_device(): gain_total = lax.psum(gain_term, ('scene', 'seq'))  86.4 us
    all_to_all x1, waiting for transfers between devices, on_device(): lax.all_to_all(back, 'seq', split_axis=0, concat_axis=0, tiled=True)  73.7 us
    all_to_all x1, waiting for transfers between devices, on_device(): lax.all_to_all(outgoing, 'seq', split_axis=0, concat_axis=0, tiled=True)  50.9 us
    all_to_all x1, starting transfers between devices, on_device(): lax.all_to_all(back, 'seq', split_axis=0, concat_axis=0, tiled=True)  12 us
    unnamed x26, local copies, waits for them, and re-layouts  7.9 us
    all_to_all x1, starting transfers between devices, on_device(): lax.all_to_all(outgoing, 'seq', split_axis=0, concat_axis=0, tiled=True)  7.6 us
  transfers between devices with their start and end apart: 3, of which 2 were waited for; matrix products, arithmetic and copies ran while one was open for 9% of the time, Pallas kernels for 0%

profile of v1, /device:TPU:1, one launch (start us, length us, event | category | flops | bytes accessed | tf_op | source)
XLA Modules:
  0.0 296.9 jit_solution(17493549479198899965)
XLA Ops:
  7.2 0.0 copy-start
  7.2 1.0 copy.33
  8.2 0.0 copy-done
  8.2 0.0 copy-start.2
  8.2 0.0 copy-start.7
  8.3 0.0 copy-start.11
  8.3 2.5 convert_bitcast_fusion.2
  10.7 0.0 copy-done.2
  10.7 0.4 copy-done.7
  11.1 0.0 copy-done.11
  11.1 1.4 multiply_convert_fusion
  12.5 0.7 convert_bitcast_fusion.1
  13.2 0.4 pad_maximum_fusion
  13.6 2.5 copy.34
  16.1 7.6 %all-to-all-start = ((bf16[16,2,1,16,16,256]{5,4,3,2,1,0:T(8,128)(2,1)}), bf16[16,2,1,16,16,256]{5,4,3,2,1,0:T(8,128)(2,1)}, u32[]{:S(2)}, u32[]{:S(2)}) async-start(bf16[16,2,1,16,16,256]{5,4,3,2,1,0:T(8,128)(2,1)} %copy.34), calls=%async_computation | async-start | bytes 8388608 | tf_op jit(solution)/shard_map/all_to_all | solution.py:34
  23.7 0.0 copy-done.6
  23.7 2.7 copy.37
  26.5 50.9 %all-to-all-done = bf16[16,2,1,16,16,256]{5,4,3,2,1,0:T(8,128)(2,1)} async-done(((bf16[16,2,1,16,16,256]{5,4,3,2,1,0:T(8,128)(2,1)}), bf16[16,2,1,16,16,256]{5,4,3,2,1,0:T(8,128)(2,1)}, u32[]{:S(2)}, u32[]{:S(2)}) %all-to-all-start) | async-done | bytes 4194336 | tf_op jit(solution)/shard_map/all_to_all | solution.py:34
  77.4 2.6 copy.70
  80.0 0.0 copy-start.9
  80.0 0.3 fusion.36
  80.3 0.6 copy-done.9
  80.9 1.7 fusion.22
  82.6 0.0 copy-done.10
  82.6 0.0 copy-start.4
  82.6 1.7 fusion.18
  84.3 0.0 copy-done.4
  84.3 0.8 fusion.28
  85.1 1.2 copy-done.1
  86.2 0.8 fusion.25
  87.0 1.2 copy.42
  88.2 1.2 copy.43
  89.4 2.3 maximum_bitcast_fusion
  91.7 12.0 %all-to-all-start.1 = ((bf16[16,1,2,16,16,256]{5,4,3,2,1,0:T(8,128)(2,1)}), bf16[16,1,2,16,16,256]{5,4,3,2,1,0:T(8,128)(2,1)}, u32[]{:S(2)}, u32[]{:S(2)}) async-start(bf16[16,1,2,16,16,256]{5,4,3,2,1,0:T(8,128)(2,1)} %maximum_bitcast_fusion), calls=%async_computation.1 | async-start | bytes 8388608 | tf_op jit(solution)/shard_map/all_to_all | solution.py:67
  103.7 0.0 reduce-scatter.2.cloned.1.call-start
  103.7 4.6 %fusion.4 = f32[256,16,256]{0,2,1:T(8,128)} fusion(f32[16,256,256]{2,1,0:T(8,128)} %copy-done.1, bf16[16,256,256]{2,1,0:T(8,128)(2,1)S(1)} %fusion.22), kind=kLoop, calls=%fused_computation.10 | loop fusion | flops 2097152 | bytes 10485760 | tf_op jit(solution)/shard_map/reduce_sum | solution.py:53
  108.3 5.5 %copy.46 = f32[256,16,256]{2,1,0:T(8,128)} copy(f32[256,16,256]{0,2,1:T(8,128)} %fusion.4) | data formatting | bytes 8388608 | tf_op jit(solution)/shard_map/reduce_sum | solution.py:53
  113.8 0.0 reduce-scatter.2.cloned.1.call-update
  113.8 0.0 copy-start.3
  113.9 73.7 %all-to-all-done.1 = bf16[16,1,2,16,16,256]{5,4,3,2,1,0:T(8,128)(2,1)} async-done(((bf16[16,1,2,16,16,256]{5,4,3,2,1,0:T(8,128)(2,1)}), bf16[16,1,2,16,16,256]{5,4,3,2,1,0:T(8,128)(2,1)}, u32[]{:S(2)}, u32[]{:S(2)}) %all-to-all-start.1) | async-done | bytes 4194336 | tf_op jit(solution)/shard_map/all_to_all | solution.py:67
  187.6 4.1 %fusion.35 = (bf16[16,1,1,16,16,256]{5,4,3,2,1,0:T(8,128)(2,1)}, bf16[16,1,1,16,16,256]{5,4,3,2,1,0:T(8,128)(2,1)S(1)}) fusion(bf16[16,1,2,16,16,256]{5,4,3,2,1,0:T(8,128)(2,1)} %all-to-all-done.1), kind=kLoop, calls=%fused_computation.44 | loop fusion | bytes 8388608 | tf_op jit(solution)/shard_map/slice | solution.py:77
  191.6 0.0 copy-done.3
  191.6 3.6 %fusion.7 = (f32[1,16,256,256]{3,2,1,0:T(8,128)S(1)}, bf16[1,16,256,256]{3,2,1,0:T(8,128)(2,1)}) fusion(f32[256]{0:T(256)S(1)} %copy-done.11, bf16[1,4096,256]{2,1,0:T(8,128)(2,1)S(1)} %copy-done.3, bf16[256,16,16,1]{0,2,1,3:T(8,128)(2,1)S(1)} %bitcast.170, bf16[16,1,1,16,16,256]{5,4,3,2,1,0:T(8,128)(2,1)S(1)} %get-tuple-element.15, ...), kind=kOutput, calls=%fused_computation.15 | convolution fusion | flops 552599552 | bytes 12715008 | tf_op jit(solution)/shard_map/qJj,Jsajc->saqc/dot_general | solution.py:68
  195.3 2.0 copy-done.5
  197.2 0.7 multiply_reduce_fusion
  198.0 86.4 %psum.7 = f32[256]{0:T(256)S(1)} all-reduce(f32[256]{0:T(256)S(1)} %multiply_reduce_fusion), channel_id=1, replica_groups=mesh['scene'=16,'seq'=16] {'scene','seq'}, use_global_device_ids=true, to_apply=%region_2.0 | all-reduce | flops 256 | bytes 2048 | tf_op jit(solution)/shard_map/psum | solution.py:82
  284.4 0.6 broadcast_multiply_fusion
  285.0 5.1 %fusion.2 = bf16[1,16,256,256]{3,2,1,0:T(8,128)(2,1)} fusion(f32[1,16,256,256]{3,2,1,0:T(8,128)} %copy-done.5, bf16[16,16,256,1]{2,1,0,3:T(8,128)(2,1)S(1)} %bitcast.158, bf16[16,1,1,16,16,256]{5,4,3,2,1,0:T(8,128)(2,1)} %get-tuple-element.14, f32[256]{0:T(256)S(1)} %copy-done.11), kind=kOutput, calls=%fused_computation.7 | convolution fusion | flops 540016640 | bytes 8520704 | tf_op jit(solution)/shard_map/Jjb,Jsajc->sabc/dot_general | solution.py:77
  (7 shorter events, 0.0 us)
Async XLA Ops:
  7.2 1.1 copy-start
  8.2 2.5 copy-start.2
  8.2 2.8 copy-start.7
  8.3 2.8 copy-start.11
  16.1 7.6 %copy-start.6 = (bf16[256,16,256]{2,1,0:T(8,128)(2,1)S(1)}, bf16[256,16,256]{2,1,0:T(8,128)(2,1)}, u32[]{:S(2)}) copy-start(bf16[256,16,256]{2,1,0:T(8,128)(2,1)} %param.11) | copy-start | bytes 6291460
  16.1 61.2 %all-to-all-start = ((bf16[16,2,1,16,16,256]{5,4,3,2,1,0:T(8,128)(2,1)}), bf16[16,2,1,16,16,256]{5,4,3,2,1,0:T(8,128)(2,1)}, u32[]{:S(2)}, u32[]{:S(2)}) async-start(bf16[16,2,1,16,16,256]{5,4,3,2,1,0:T(8,128)(2,1)} %copy.34), calls=%async_computation | async-start | bytes 8388608 | tf_op jit(solution)/shard_map/all_to_all | solution.py:34
  80.0 0.9 copy-start.9
  80.9 1.7 copy-start.10
  82.6 1.7 copy-start.4
  84.3 1.9 copy-start.1
  91.7 95.9 %all-to-all-start.1 = ((bf16[16,1,2,16,16,256]{5,4,3,2,1,0:T(8,128)(2,1)}), bf16[16,1,2,16,16,256]{5,4,3,2,1,0:T(8,128)(2,1)}, u32[]{:S(2)}, u32[]{:S(2)}) async-start(bf16[16,1,2,16,16,256]{5,4,3,2,1,0:T(8,128)(2,1)} %maximum_bitcast_fusion), calls=%async_computation.1 | async-start | bytes 8388608 | tf_op jit(solution)/shard_map/all_to_all | solution.py:67
  103.7 186.4 %reduce-scatter.2.cloned.1.call-start = ((), (), s32[]{:S(2)}) async-start(), calls=%async_computation.3 | async-start | bytes 4456448 | tf_op jit(solution)/shard_map/reduce_scatter | solution.py:54
  113.8 77.8 %copy-start.3 = (bf16[1,4096,256]{2,1,0:T(8,128)(2,1)S(1)}, bf16[1,4096,256]{2,1,0:T(8,128)(2,1)}, u32[]{:S(2)}) copy-start(bf16[1,4096,256]{2,1,0:T(8,128)(2,1)} %param.8) | copy-start | bytes 6291460
  187.6 4.1 %copy-start.8 = (bf16[1,4096,256]{2,1,0:T(8,128)(2,1)S(1)}, bf16[1,4096,256]{2,1,0:T(8,128)(2,1)}, u32[]{:S(2)}) copy-start(bf16[1,4096,256]{2,1,0:T(8,128)(2,1)} %param.9) | copy-start | bytes 6291460
  195.3 2.0 copy-start.5
Sparse Core Ops, SparseCore 0:
  114.0 102.4 reduce-scatter.1

commit v2 on v1

--- a/solution.py
+++ b/solution.py
@@ -51,7 +51,12 @@
         "pi,spjc->sijc", across_unmix, spread_grad, preferred_element_type=f32
     )
     kernel_term = jnp.sum(grad_weighted * second_mix.astype(f32), axis=0)
-    kernel_grad = lax.psum_scatter(kernel_term, "scene", scatter_dimension=0, tiled=True)
+    scene_parts = lax.axis_size("scene")
+    term_by_dest = kernel_term.reshape(scene_parts, block_len // scene_parts, chunk, channels)
+    term_spread = lax.all_to_all(
+        term_by_dest.astype(bf16), "scene", split_axis=0, concat_axis=0, tiled=True
+    )
+    kernel_grad = jnp.sum(term_spread.astype(f32), axis=0)
     grad_second = (grad_weighted * kernel_f).astype(bf16)
     grad_first = jnp.einsum(
         "ia,sijc->sajc", across_mix, grad_second, preferred_element_type=f32
@@ -79,7 +84,15 @@
     )
     grad_input = grad_input.astype(bf16).reshape(scenes_here, row_count, channels)
     gain_term = jnp.sum(inputs.astype(f32) * grad_gate, axis=(0, 1, 2))
-    gain_total = lax.psum(gain_term, ("scene", "seq"))
+    devices = lax.axis_size(("scene", "seq"))
+    gain_spread = lax.all_to_all(
+        jnp.broadcast_to(gain_term, (devices, channels)),
+        ("scene", "seq"),
+        split_axis=0,
+        concat_axis=0,
+        tiled=True,
+    )
+    gain_total = jnp.sum(gain_spread, axis=0)
     total_rows = scenes_here * lax.axis_size("scene") * local_a * parts * block_len
     grad_scale = 1.0 / jnp.sqrt(jnp.float32(total_rows))
     return (mixed_out, grad_input, kernel_grad, gain_total * grad_scale)

time: 297 us -> 233 us (0.78)
  blocking collectives: 86.4 us -> 55.9 us
  waiting for transfers between devices: 125 us -> 100 us
  starting transfers between devices: 19.6 us -> 33.9 us
  between operations: 14.2 us -> 0.82 us
  local copies, waits for them, and re-layouts: 25.3 us -> 17.1 us
    psum x1 -> x0, blocking collectives: 86.4 us -> none  [on_device(): gain_total = lax.psum(gain_term, ('scene', 'seq'))]
    all_to_all x0 -> x1, blocking collectives: none -> 55.9 us  [on_device(): lax.all_to_all(outgoing, 'seq', split_axis=0, concat_axis=0, tiled=True)]
    all_to_all x1, waiting for transfers between devices: 73.7 us -> 52 us  [on_device(): lax.all_to_all(back, 'seq', split_axis=0, concat_axis=0, tiled=True)]
    all_to_all x1 -> x2, starting transfers between devices: 7.6 us -> 28.2 us  [the longest x1 18.1 us: on_device(): lax.all_to_all(jnp.broadcast_to(gain_term, (devices, channels)), ('scene'...]
    all_to_all x1, starting transfers between devices: 12 us -> 5.71 us  [on_device(): lax.all_to_all(back, 'seq', split_axis=0, concat_axis=0, tiled=True)]
    reduce_sum x1 -> x0, local copies, waits for them, and re-layouts: 5.48 us -> none  [on_device(): kernel_term = jnp.sum(grad_weighted * second_mix.astype(f32), axis=0)]
    convert_element_type x0 -> x1, local copies, waits for them, and re-layouts: none -> 3.18 us  [on_device(): term_by_dest.astype(bf16)]
    all_to_all x1 -> x2, waiting for transfers between devices: 50.9 us -> 48.1 us  [the longest x1 40 us: on_device(): lax.all_to_all(term_by_dest.astype(bf16), 'scene', split_axis=0, concat_a...]
  transfers between devices with their start and end apart: 3 -> 3, of which waited for: 2 -> 3; matrix products, arithmetic and copies ran while one was open for 9% -> 8% of each run, Pallas kernels for 0% -> 0%
where the time goes in v2:
time: 233 us
  waiting for transfers between devices  100 us (43%)
  blocking collectives  55.9 us (24%)
  starting transfers between devices  33.9 us (15%)
  matrix products  17.5 us (8%)
  local copies, waits for them, and re-layouts  17.1 us (7%)
  other arithmetic  7.53 us (3%)
    all_to_all x1, blocking collectives, on_device(): lax.all_to_all(outgoing, 'seq', split_axis=0, concat_axis=0, tiled=True)  55.9 us
    all_to_all x1, waiting for transfers between devices, on_device(): lax.all_to_all(back, 'seq', split_axis=0, concat_axis=0, tiled=True)  52 us
    all_to_all x1, waiting for transfers between devices, on_device(): lax.all_to_all(term_by_dest.astype(bf16), 'scene', split_axis=0, concat_a...  40 us
    all_to_all x1, starting transfers between devices, on_device(): lax.all_to_all(jnp.broadcast_to(gain_term, (devices, channels)), ('scene'...  18.1 us
    all_to_all x1, starting transfers between devices, on_device(): lax.all_to_all(term_by_dest.astype(bf16), 'scene', split_axis=0, concat_a...  10.1 us
    all_to_all x1, waiting for transfers between devices, on_device(): lax.all_to_all(jnp.broadcast_to(gain_term, (devices, channels)), ('scene'...  8.15 us
    all_to_all x1, starting transfers between devices, on_device(): lax.all_to_all(back, 'seq', split_axis=0, concat_axis=0, tiled=True)  5.71 us
    unnamed x24, local copies, waits for them, and re-layouts  5.42 us
  transfers between devices with their start and end apart: 3, of which 3 were waited for; matrix products, arithmetic and copies ran while one was open for 8% of the time, Pallas kernels for 0%

profile of v2, /device:TPU:1, one launch (start us, length us, event | category | flops | bytes accessed | tf_op | source)
XLA Modules:
  0.0 233.0 jit_solution(3830661353342950202)
XLA Ops:
  0.6 0.0 copy-start
  0.6 1.0 copy.59
  1.7 0.0 copy-start.2
  1.7 0.0 copy-start.6
  1.7 0.0 copy-start.10
  1.7 2.5 %convert_bitcast_fusion.2 = bf16[16,1,1,16,16,256]{5,4,0,3,2,1:T(8,128)(2,1)S(1)} fusion(bf16[16,256,256,1]{2,1,3,0:T(8,128)(2,1)} %bitcast.159, bf16[16,16,256,1]{2,1,0,3:T(8,128)(2,1)} %bitcast.170), kind=kOutput, calls=%fused_computation.36 | convolution fusion | flops 537919488 | bytes 4325376 | tf_op jit(solution)/shard_map/Jjb,sabc->Jsajc/dot_general | solution.py:27
  4.2 0.0 copy-done.2
  4.2 0.4 copy-done.6
  4.6 0.0 copy-done.10
  4.6 1.4 multiply_convert_fusion
  6.0 0.7 convert_bitcast_fusion.1
  6.7 0.4 pad_maximum_fusion
  7.1 0.5 copy.60
  7.6 55.9 %all_to_all.21 = bf16[16,2,1,16,16,256]{5,4,3,2,1,0:T(8,128)(2,1)S(1)} all-to-all(bf16[16,2,1,16,16,256]{5,4,3,2,1,0:T(8,128)(2,1)S(1)} %copy.60), channel_id=1, replica_groups=mesh['scene'=16,'seq'=16] {'seq'}, dimensions={0} | all-to-all | bytes 8388608 | tf_op jit(solution)/shard_map/all_to_all | solution.py:34
  63.6 0.4 copy.110
  64.0 0.0 copy-start.8
  64.0 0.3 fusion.38
  64.3 0.6 copy-done.8
  64.9 1.0 fusion.22
  65.9 0.0 copy-done
  65.9 0.6 copy-done.4
  66.5 1.2 fusion.25
  67.7 1.2 copy.67
  68.9 2.8 %fusion.4 = (bf16[1,256,16,256]{3,1,2,0:T(8,128)(2,1)}, f32[16,256,256]{1,2,0:T(8,128)S(1)}) fusion(bf16[16,256,256]{1,2,0:T(8,128)(2,1)S(1)} %fusion.22, bf16[256,256]{1,0:T(8,128)(2,1)S(1)} %copy-done, bf16[256,16,256]{2,1,0:T(8,128)(2,1)S(1)} %bitcast.167), kind=kOutput, calls=%fused_computation.10 | convolution fusion | flops 540016640 | bytes 10616832 | tf_op jit(solution)/shard_map/pi,spjc->sijc/dot_general | solution.py:50
  71.7 1.3 fusion.28
  72.9 1.2 copy.68
  74.1 2.3 maximum_bitcast_fusion
  76.5 5.7 %all-to-all-start.1 = ((bf16[16,1,2,16,16,256]{5,4,3,2,1,0:T(8,128)(2,1)}), bf16[16,1,2,16,16,256]{5,4,3,2,1,0:T(8,128)(2,1)}, u32[]{:S(2)}, u32[]{:S(2)}) async-start(bf16[16,1,2,16,16,256]{5,4,3,2,1,0:T(8,128)(2,1)} %maximum_bitcast_fusion), calls=%async_computation.1 | async-start | bytes 8388608 | tf_op jit(solution)/shard_map/all_to_all | solution.py:72
  82.2 3.2 %copy.71 = bf16[16,16,16,256]{3,1,2,0:T(8,128)(2,1)} copy(bf16[16,16,16,256]{3,1,0,2:T(8,128)(2,1)} %bitcast.164) | data formatting | bytes 4194304 | tf_op jit(solution)/shard_map/convert_element_type | solution.py:57
  85.4 52.0 %all-to-all-done.1 = bf16[16,1,2,16,16,256]{5,4,3,2,1,0:T(8,128)(2,1)} async-done(((bf16[16,1,2,16,16,256]{5,4,3,2,1,0:T(8,128)(2,1)}), bf16[16,1,2,16,16,256]{5,4,3,2,1,0:T(8,128)(2,1)}, u32[]{:S(2)}, u32[]{:S(2)}) %all-to-all-start.1) | async-done | bytes 4194336 | tf_op jit(solution)/shard_map/all_to_all | solution.py:72
  137.4 10.1 %all-to-all-start.2 = ((bf16[16,16,16,256]{3,1,2,0:T(8,128)(2,1)}), bf16[16,16,16,256]{3,1,2,0:T(8,128)(2,1)}, u32[]{:S(2)}, u32[]{:S(2)}) async-start(bf16[16,16,16,256]{3,1,2,0:T(8,128)(2,1)} %copy.71), calls=%async_computation.2 | async-start | bytes 4194304 | tf_op jit(solution)/shard_map/all_to_all | solution.py:56
  147.4 0.0 copy-start.7
  147.5 4.0 %fusion.37 = (bf16[16,1,1,16,16,256]{5,4,3,2,1,0:T(8,128)(2,1)}, bf16[16,1,1,16,16,256]{5,4,3,2,1,0:T(8,128)(2,1)S(1)}) fusion(bf16[16,1,2,16,16,256]{5,4,3,2,1,0:T(8,128)(2,1)} %all-to-all-done.1), kind=kLoop, calls=%fused_computation.47 | loop fusion | bytes 8388608 | tf_op jit(solution)/shard_map/slice | solution.py:82
  151.5 0.0 copy-done.7
  151.5 3.6 %fusion.7 = (f32[1,16,256,256]{3,2,1,0:T(8,128)S(1)}, bf16[1,16,256,256]{3,2,1,0:T(8,128)(2,1)}) fusion(f32[256]{0:T(256)S(1)} %copy-done.10, bf16[1,4096,256]{2,1,0:T(8,128)(2,1)S(1)} %copy-done.2, bf16[256,16,16,1]{0,2,1,3:T(8,128)(2,1)S(1)} %bitcast.173, bf16[16,1,1,16,16,256]{5,4,3,2,1,0:T(8,128)(2,1)S(1)} %get-tuple-element.19, ...), kind=kOutput, calls=%fused_computation.15 | convolution fusion | flops 552599552 | bytes 12715008 | tf_op jit(solution)/shard_map/qJj,Jsajc->saqc/dot_general | solution.py:73
  155.1 1.9 copy-done.3
  157.1 0.7 multiply_reduce_fusion
  157.8 0.0 copy-start.9
  157.8 40.0 %all-to-all-done.2 = bf16[16,16,16,256]{3,1,2,0:T(8,128)(2,1)} async-done(((bf16[16,16,16,256]{3,1,2,0:T(8,128)(2,1)}), bf16[16,16,16,256]{3,1,2,0:T(8,128)(2,1)}, u32[]{:S(2)}, u32[]{:S(2)}) %all-to-all-start.2) | async-done | bytes 2097184 | tf_op jit(solution)/shard_map/all_to_all | solution.py:56
  197.7 0.8 broadcast_in_dim.14
  198.6 18.1 %all-to-all-start.3 = ((f32[256,1,256]{2,1,0:T(1,128)}), f32[256,1,256]{2,1,0:T(1,128)S(1)}, u32[]{:S(2)}, u32[]{:S(2)}) async-start(f32[256,1,256]{2,1,0:T(1,128)} %broadcast_in_dim.14), calls=%async_computation.3 | async-start | bytes 524288 | tf_op jit(solution)/shard_map/all_to_all | solution.py:88
  216.7 1.9 convert_reduce_fusion
  218.6 0.9 copy.74
  219.5 0.0 copy-done.9
  219.5 4.5 %fusion.2 = bf16[1,16,256,256]{3,2,1,0:T(8,128)(2,1)} fusion(f32[1,16,256,256]{3,2,1,0:T(8,128)} %copy-done.3, bf16[16,16,256,1]{2,1,0,3:T(8,128)(2,1)S(1)} %bitcast.171, bf16[16,1,1,16,16,256]{5,4,3,2,1,0:T(8,128)(2,1)S(1)} %copy-done.5, f32[256]{0:T(256)S(1)} %copy-done.10), kind=kOutput, calls=%fused_computation.7 | convolution fusion | flops 540016640 | bytes 8520704 | tf_op jit(solution)/shard_map/Jjb,Jsajc->sabc/dot_general | solution.py:82
  224.0 8.2 %all-to-all-done.3 = f32[256,1,256]{2,1,0:T(1,128)S(1)} async-done(((f32[256,1,256]{2,1,0:T(1,128)}), f32[256,1,256]{2,1,0:T(1,128)S(1)}, u32[]{:S(2)}, u32[]{:S(2)}) %all-to-all-start.3) | async-done | bytes 262176 | tf_op jit(solution)/shard_map/all_to_all | solution.py:88
  232.1 0.3 reduce_sum.33
  232.4 0.6 broadcast_multiply_fusion
  (6 shorter events, 0.0 us)
Async XLA Ops:
  0.6 65.3 %copy-start = (bf16[256,256]{1,0:T(8,128)(2,1)S(1)}, bf16[256,256]{1,0:T(8,128)(2,1)}, u32[]{:S(2)}) copy-start(bf16[256,256]{1,0:T(8,128)(2,1)} %param.14) | copy-start | bytes 393220
  1.7 2.5 %copy-start.2 = (bf16[1,4096,256]{2,1,0:T(8,128)(2,1)S(1)}, bf16[1,4096,256]{2,1,0:T(8,128)(2,1)}, u32[]{:S(2)}) copy-start(bf16[1,4096,256]{2,1,0:T(8,128)(2,1)} %param.8) | copy-start | bytes 6291460
  1.7 2.9 %copy-start.6 = (bf16[1,4096,256]{2,1,0:T(8,128)(2,1)S(1)}, bf16[1,4096,256]{2,1,0:T(8,128)(2,1)}, u32[]{:S(2)}) copy-start(bf16[1,4096,256]{2,1,0:T(8,128)(2,1)} %param.9) | copy-start | bytes 6291460
  1.7 2.9 %copy-start.10 = (f32[256]{0:T(256)S(1)}, f32[256]{0:T(256)}, u32[]{:S(2)}) copy-start(f32[256]{0:T(256)} %param.10) | copy-start | bytes 3076
  64.0 0.9 copy-start.8
  64.9 1.6 copy-start.4
  76.5 60.9 %all-to-all-start.1 = ((bf16[16,1,2,16,16,256]{5,4,3,2,1,0:T(8,128)(2,1)}), bf16[16,1,2,16,16,256]{5,4,3,2,1,0:T(8,128)(2,1)}, u32[]{:S(2)}, u32[]{:S(2)}) async-start(bf16[16,1,2,16,16,256]{5,4,3,2,1,0:T(8,128)(2,1)} %maximum_bitcast_fusion), calls=%async_computation.1 | async-start | bytes 8388608 | tf_op jit(solution)/shard_map/all_to_all | solution.py:72
  137.4 60.4 %all-to-all-start.2 = ((bf16[16,16,16,256]{3,1,2,0:T(8,128)(2,1)}), bf16[16,16,16,256]{3,1,2,0:T(8,128)(2,1)}, u32[]{:S(2)}, u32[]{:S(2)}) async-start(bf16[16,16,16,256]{3,1,2,0:T(8,128)(2,1)} %copy.71), calls=%async_computation.2 | async-start | bytes 4194304 | tf_op jit(solution)/shard_map/all_to_all | solution.py:56
  147.4 4.0 %copy-start.7 = (bf16[1,4096,256]{2,1,0:T(8,128)(2,1)S(1)}, bf16[1,4096,256]{2,1,0:T(8,128)(2,1)}, u32[]{:S(2)}) copy-start(bf16[1,4096,256]{2,1,0:T(8,128)(2,1)} %param.9) | copy-start | bytes 6291460
  155.1 2.0 copy-start.3
  157.8 61.7 %copy-start.5 = (bf16[16,1,1,16,16,256]{5,4,3,2,1,0:T(8,128)(2,1)S(1)}, bf16[16,1,1,16,16,256]{5,4,3,2,1,0:T(8,128)(2,1)}, u32[]{:S(2)}) copy-start(bf16[16,1,1,16,16,256]{5,4,3,2,1,0:T(8,128)(2,1)} %get-tuple-element.18) | copy-start | bytes 6291460
  157.8 61.7 %copy-start.9 = (bf16[256,256]{1,0:T(8,128)(2,1)S(1)}, bf16[256,256]{1,0:T(8,128)(2,1)}, u32[]{:S(2)}) copy-start(bf16[256,256]{1,0:T(8,128)(2,1)} %param.12) | copy-start | bytes 393220
  198.6 33.6 %all-to-all-start.3 = ((f32[256,1,256]{2,1,0:T(1,128)}), f32[256,1,256]{2,1,0:T(1,128)S(1)}, u32[]{:S(2)}, u32[]{:S(2)}) async-start(f32[256,1,256]{2,1,0:T(1,128)} %broadcast_in_dim.14), calls=%async_computation.3 | async-start | bytes 524288 | tf_op jit(solution)/shard_map/all_to_all | solution.py:88
  219.5 13.5 %copy-start.1 = (bf16[256,256]{1,0:T(8,128)(2,1)S(1)}, bf16[256,256]{1,0:T(8,128)(2,1)}, u32[]{:S(2)}) copy-start(bf16[256,256]{1,0:T(8,128)(2,1)} %param.14) | copy-start | bytes 393220

commit v3 on v2

--- a/solution.py
+++ b/solution.py
@@ -53,10 +53,15 @@
     kernel_term = jnp.sum(grad_weighted * second_mix.astype(f32), axis=0)
     scene_parts = lax.axis_size("scene")
     term_by_dest = kernel_term.reshape(scene_parts, block_len // scene_parts, chunk, channels)
-    term_spread = lax.all_to_all(
-        term_by_dest.astype(bf16), "scene", split_axis=0, concat_axis=0, tiled=True
-    )
-    kernel_grad = jnp.sum(term_spread.astype(f32), axis=0)
+    term_by_dest = term_by_dest.astype(bf16)
+    scene_index = lax.axis_index("scene")
+    kernel_grad = lax.dynamic_index_in_dim(term_by_dest, scene_index, 0, False).astype(f32)
+    for shift in range(1, scene_parts):
+        outgoing_term = lax.dynamic_index_in_dim(
+            term_by_dest, (scene_index + shift) % scene_parts, 0, False
+        )
+        pairs = [(src, (src + shift) % scene_parts) for src in range(scene_parts)]
+        kernel_grad = kernel_grad + lax.ppermute(outgoing_term, "scene", pairs).astype(f32)
     grad_second = (grad_weighted * kernel_f).astype(bf16)
     grad_first = jnp.einsum(
         "ia,sijc->sajc", across_mix, grad_second, preferred_element_type=f32

time: 233 us -> 213 us (0.914)
  waiting for transfers between devices: 100 us -> 52.3 us
  starting transfers between devices: 33.9 us -> 57.6 us
  local copies, waits for them, and re-layouts: 17.1 us -> 20.6 us
    all_to_all x1 -> x0, waiting for transfers between devices: 40 us -> none  [on_device(): lax.all_to_all(term_by_dest.astype(bf16), 'scene', split_axis=0, concat_a...]
    ppermute x0 -> x15, starting transfers between devices: none -> 38 us  [on_device(): lax.ppermute(outgoing_term, 'scene', pairs).astype(f32)]
    all_to_all x1, waiting for transfers between devices: 52 us -> 33.9 us  [on_device(): lax.all_to_all(back, 'seq', split_axis=0, concat_axis=0, tiled=True)]
    all_to_all x1 -> x0, starting transfers between devices: 10.1 us -> none  [on_device(): lax.all_to_all(term_by_dest.astype(bf16), 'scene', split_axis=0, concat_a...]
    ppermute x0 -> x15, waiting for transfers between devices: none -> 9.83 us  [on_device(): lax.ppermute(outgoing_term, 'scene', pairs).astype(f32)]
    dynamic_slice x0 -> x16, local copies, waits for them, and re-layouts: none -> 9.61 us  [the longest x15 7.84 us: on_device(): lax.dynamic_index_in_dim(term_by_dest, (scene_index + shift) % scene_part...]
    all_to_all x1, starting transfers between devices: 18.1 us -> 13.9 us  [on_device(): lax.all_to_all(jnp.broadcast_to(gain_term, (devices, channels)), ('scene'...]
    convert_element_type x1 -> x0, local copies, waits for them, and re-layouts: 3.18 us -> none  [on_device(): term_by_dest.astype(bf16)]
  transfers between devices with their start and end apart: 3 -> 17, of which waited for: 3 -> 5; matrix products, arithmetic and copies ran while one was open for 8% -> 12% of each run, Pallas kernels for 0% -> 0%
where the time goes in v3:
time: 213 us
  starting transfers between devices  57.6 us (27%)
  blocking collectives  55.9 us (26%)
  waiting for transfers between devices  52.3 us (25%)
  local copies, waits for them, and re-layouts  20.6 us (10%)
  matrix products  17.8 us (8%)
  other arithmetic  7.94 us (4%)
    all_to_all x1, blocking collectives, on_device(): lax.all_to_all(outgoing, 'seq', split_axis=0, concat_axis=0, tiled=True)  55.9 us
    ppermute x15, starting transfers between devices, on_device(): lax.ppermute(outgoing_term, 'scene', pairs).astype(f32)  38 us
    all_to_all x1, waiting for transfers between devices, on_device(): lax.all_to_all(back, 'seq', split_axis=0, concat_axis=0, tiled=True)  33.9 us
    all_to_all x1, starting transfers between devices, on_device(): lax.all_to_all(jnp.broadcast_to(gain_term, (devices, channels)), ('scene'...  13.9 us
    ppermute x15, waiting for transfers between devices, on_device(): lax.ppermute(outgoing_term, 'scene', pairs).astype(f32)  9.83 us
    all_to_all x1, waiting for transfers between devices, on_device(): lax.all_to_all(jnp.broadcast_to(gain_term, (devices, channels)), ('scene'...  8.6 us
    dynamic_slice x15, local copies, waits for them, and re-layouts, on_device(): lax.dynamic_index_in_dim(term_by_dest, (scene_index + shift) % scene_part...  7.84 us
    all_to_all x1, starting transfers between devices, on_device(): lax.all_to_all(back, 'seq', split_axis=0, concat_axis=0, tiled=True)  5.72 us
  transfers between devices with their start and end apart: 17, of which 5 were waited for; matrix products, arithmetic and copies ran while one was open for 12% of the time, Pallas kernels for 0%

profile of v3, /device:TPU:1, one launch (start us, length us, event | category | flops | bytes accessed | tf_op | source)
XLA Modules:
  0.0 213.1 jit_solution(10372289200764059109)
XLA Ops:
  0.6 1.0 copy.117
  1.7 2.5 %convert_bitcast_fusion.2 = bf16[16,1,1,16,16,256]{5,4,0,3,2,1:T(8,128)(2,1)S(1)} fusion(bf16[16,256,256,1]{2,1,3,0:T(8,128)(2,1)} %bitcast.209, bf16[16,16,256,1]{2,1,0,3:T(8,128)(2,1)} %bitcast.220), kind=kOutput, calls=%fused_computation.35 | convolution fusion | flops 537919488 | bytes 4325376 | tf_op jit(solution)/shard_map/Jjb,sabc->Jsajc/dot_general | solution.py:27
  4.6 1.4 multiply_convert_fusion
  6.0 0.7 convert_bitcast_fusion.1
  7.6 55.9 %all_to_all.16 = bf16[16,2,1,16,16,256]{5,4,3,2,1,0:T(8,128)(2,1)S(1)} all-to-all(bf16[16,2,1,16,16,256]{5,4,3,2,1,0:T(8,128)(2,1)S(1)} %copy.118), channel_id=1, replica_groups=mesh['scene'=16,'seq'=16] {'seq'}, dimensions={0} | all-to-all | bytes 8388608 | tf_op jit(solution)/shard_map/all_to_all | solution.py:34
  64.7 1.0 fusion.22
  66.3 1.2 fusion.25
  67.5 1.2 copy.125
  68.7 2.8 %fusion.4 = (bf16[1,256,16,256]{3,1,2,0:T(8,128)(2,1)}, f32[16,256,256]{1,2,0:T(8,128)S(1)}) fusion(bf16[16,256,256]{1,2,0:T(8,128)(2,1)S(1)} %fusion.22, bf16[256,256]{1,0:T(8,128)(2,1)S(1)} %copy-done, bf16[256,16,256]{2,1,0:T(8,128)(2,1)S(1)} %bitcast.217), kind=kOutput, calls=%fused_computation.10 | convolution fusion | flops 540016640 | bytes 10616832 | tf_op jit(solution)/shard_map/pi,spjc->sijc/dot_general | solution.py:50
  71.5 1.5 fusion.28
  73.0 1.2 copy.126
  74.2 2.4 %maximum_bitcast_fusion = bf16[16,1,2,16,16,256]{5,4,3,2,1,0:T(8,128)(2,1)} fusion(bf16[1,16,1,16,16,256]{5,4,3,2,1,0:T(8,128)(2,1)S(1)} %copy.126, bf16[1,16,1,16,16,256]{5,4,3,2,1,0:T(8,128)(2,1)S(1)} %copy.125), kind=kLoop, calls=%fused_computation.5 | loop fusion | flops 2097152 | bytes 8388608 | tf_op jit(solution)/shard_map/transpose | solution.py:76
  76.6 5.7 %all-to-all-start.1 = ((bf16[16,1,2,16,16,256]{5,4,3,2,1,0:T(8,128)(2,1)}), bf16[16,1,2,16,16,256]{5,4,3,2,1,0:T(8,128)(2,1)}, u32[]{:S(2)}, u32[]{:S(2)}) async-start(bf16[16,1,2,16,16,256]{5,4,3,2,1,0:T(8,128)(2,1)} %maximum_bitcast_fusion), calls=%async_computation.1 | async-start | bytes 8388608 | tf_op jit(solution)/shard_map/all_to_all | solution.py:77
  82.3 1.8 constant_dynamic-slice_fusion.15
  84.0 0.7 copy.200
  86.1 0.7 copy.203
  86.8 0.7 copy.204
  87.6 0.7 copy.207
  88.3 0.7 copy.208
  89.0 0.7 copy.209
  89.7 0.7 copy.210
  90.4 0.7 copy.211
  91.1 0.7 copy.212
  91.9 3.1 %collective-permute-start = (bf16[16,16,256]{2,1,0:T(8,128)(2,1)S(1)}, bf16[16,16,256]{2,1,0:T(8,128)(2,1)S(1)}, u32[]{:S(2)}, u32[]{:S(2)}) collective-permute-start(bf16[16,16,256]{2,1,0:T(8,128)(2,1)S(1)} %bitcast.229), channel_id=1, source_target_pairs={{0,16},{16,32},{32,48},{48,64},{64,80},{80,96},{96,112},{112,128},... | collective-permute-start | bytes 393224 | tf_op jit(solution)/shard_map/ppermute | solution.py:64
  95.0 4.2 %collective-permute-start.1 = (bf16[16,16,256]{2,1,0:T(8,128)(2,1)S(1)}, bf16[16,16,256]{2,1,0:T(8,128)(2,1)S(1)}, u32[]{:S(2)}, u32[]{:S(2)}) collective-permute-start(bf16[16,16,256]{2,1,0:T(8,128)(2,1)S(1)} %bitcast.228), channel_id=1, source_target_pairs={{0,32},{16,48},{32,64},{48,80},{64,96},{80,112},{96,128},{112,144}... | collective-permute-start | bytes 393224 | tf_op jit(solution)/shard_map/ppermute | solution.py:64
  99.2 3.4 %collective-permute-start.2 = (bf16[16,16,256]{2,1,0:T(8,128)(2,1)}, bf16[16,16,256]{2,1,0:T(8,128)(2,1)S(1)}, u32[]{:S(2)}, u32[]{:S(2)}) collective-permute-start(bf16[16,16,256]{2,1,0:T(8,128)(2,1)} %bitcast.206), channel_id=1, source_target_pairs={{0,48},{16,64},{32,80},{48,96},{64,112},{80,128},{96,144},{112,160... | collective-permute-start | bytes 393224 | tf_op jit(solution)/shard_map/ppermute | solution.py:64
  102.6 1.3 collective-permute-start.3
  103.9 0.7 collective-permute-start.4
  104.6 33.9 %all-to-all-done.1 = bf16[16,1,2,16,16,256]{5,4,3,2,1,0:T(8,128)(2,1)} async-done(((bf16[16,1,2,16,16,256]{5,4,3,2,1,0:T(8,128)(2,1)}), bf16[16,1,2,16,16,256]{5,4,3,2,1,0:T(8,128)(2,1)}, u32[]{:S(2)}, u32[]{:S(2)}) %all-to-all-start.1) | async-done | bytes 4194336 | tf_op jit(solution)/shard_map/all_to_all | solution.py:77
  138.5 4.0 %fusion.51 = (bf16[16,1,1,16,16,256]{5,4,3,2,1,0:T(8,128)(2,1)}, bf16[16,1,1,16,16,256]{5,4,3,2,1,0:T(8,128)(2,1)S(1)}) fusion(bf16[16,1,2,16,16,256]{5,4,3,2,1,0:T(8,128)(2,1)} %all-to-all-done.1), kind=kLoop, calls=%fused_computation.93 | loop fusion | bytes 8388608 | tf_op jit(solution)/shard_map/slice | solution.py:87
  142.5 6.2 %collective-permute-done = bf16[16,16,256]{2,1,0:T(8,128)(2,1)S(1)} collective-permute-done((bf16[16,16,256]{2,1,0:T(8,128)(2,1)S(1)}, bf16[16,16,256]{2,1,0:T(8,128)(2,1)S(1)}, u32[]{:S(2)}, u32[]{:S(2)}) %collective-permute-start) | collective-permute-done | bytes 131104 | tf_op jit(solution)/shard_map/ppermute | solution.py:64
  148.7 4.7 %collective-permute-start.5 = (bf16[16,16,256]{2,1,0:T(8,128)(2,1)}, bf16[16,16,256]{2,1,0:T(8,128)(2,1)S(1)}, u32[]{:S(2)}, u32[]{:S(2)}) collective-permute-start(bf16[16,16,256]{2,1,0:T(8,128)(2,1)} %bitcast.203), channel_id=1, source_target_pairs={{0,96},{16,112},{32,128},{48,144},{64,160},{80,176},{96,192},{112,... | collective-permute-start | bytes 393224 | tf_op jit(solution)/shard_map/ppermute | solution.py:64
  153.4 1.7 collective-permute-done.1
  155.1 1.1 collective-permute-start.6
  156.2 3.1 %collective-permute-start.7 = (bf16[16,16,256]{2,1,0:T(8,128)(2,1)}, bf16[16,16,256]{2,1,0:T(8,128)(2,1)S(1)}, u32[]{:S(2)}, u32[]{:S(2)}) collective-permute-start(bf16[16,16,256]{2,1,0:T(8,128)(2,1)} %bitcast.226), channel_id=1, source_target_pairs={{0,128},{16,144},{32,160},{48,176},{64,192},{80,208},{96,224},{112... | collective-permute-start | bytes 393224 | tf_op jit(solution)/shard_map/ppermute | solution.py:64
  159.3 3.8 %collective-permute-start.8 = (bf16[16,16,256]{2,1,0:T(8,128)(2,1)S(1)}, bf16[16,16,256]{2,1,0:T(8,128)(2,1)S(1)}, u32[]{:S(2)}, u32[]{:S(2)}) collective-permute-start(bf16[16,16,256]{2,1,0:T(8,128)(2,1)S(1)} %bitcast.225), channel_id=1, source_target_pairs={{0,144},{16,160},{32,176},{48,192},{64,208},{80,224},{96,240},{112... | collective-permute-start | bytes 393224 | tf_op jit(solution)/shard_map/ppermute | solution.py:64
  163.1 3.6 %fusion.7 = (f32[1,16,256,256]{3,2,1,0:T(8,128)S(1)}, bf16[1,16,256,256]{3,2,1,0:T(8,128)(2,1)}) fusion(f32[256]{0:T(256)S(1)} %copy-done.13, bf16[1,4096,256]{2,1,0:T(8,128)(2,1)S(1)} %copy-done.2, bf16[256,16,16,1]{0,2,1,3:T(8,128)(2,1)S(1)} %bitcast.223, bf16[16,1,1,16,16,256]{5,4,3,2,1,0:T(8,128)(2,1)S(1)} %get-tuple-element.7, ...), kind=kOutput, calls=%fused_computation.15 | convolution fusion | flops 552599552 | bytes 12715008 | tf_op jit(solution)/shard_map/qJj,Jsajc->saqc/dot_general | solution.py:78
  166.7 1.9 collective-permute-done.5
  168.6 1.2 collective-permute-start.10
  169.8 2.0 collective-permute-start.11
  172.3 5.2 %collective-permute-start.13 = (bf16[16,16,256]{2,1,0:T(8,128)(2,1)}, bf16[16,16,256]{2,1,0:T(8,128)(2,1)}, u32[]{:S(2)}, u32[]{:S(2)}) collective-permute-start(bf16[16,16,256]{2,1,0:T(8,128)(2,1)} %bitcast.195), channel_id=1, source_target_pairs={{0,224},{16,240},{32,0},{48,16},{64,32},{80,48},{96,64},{112,80},{... | collective-permute-start | bytes 393224 | tf_op jit(solution)/shard_map/ppermute | solution.py:64
  177.5 3.9 %collective-permute-start.14 = (bf16[16,16,256]{2,1,0:T(8,128)(2,1)}, bf16[16,16,256]{2,1,0:T(8,128)(2,1)}, u32[]{:S(2)}, u32[]{:S(2)}) collective-permute-start(bf16[16,16,256]{2,1,0:T(8,128)(2,1)} %bitcast.194), channel_id=1, source_target_pairs={{0,240},{16,0},{32,16},{48,32},{64,48},{80,64},{96,80},{112,96},{1... | collective-permute-start | bytes 393224 | tf_op jit(solution)/shard_map/ppermute | solution.py:64
  181.3 0.7 multiply_reduce_fusion
  182.1 0.8 broadcast_in_dim.14
  182.9 13.9 %all-to-all-start.2 = ((f32[256,1,256]{2,1,0:T(1,128)}), f32[256,1,256]{2,1,0:T(1,128)S(1)}, u32[]{:S(2)}, u32[]{:S(2)}) async-start(f32[256,1,256]{2,1,0:T(1,128)} %broadcast_in_dim.14), calls=%async_computation.2 | async-start | bytes 524288 | tf_op jit(solution)/shard_map/all_to_all | solution.py:93
  196.9 2.3 %fusion.46 = f32[16,16,256]{2,1,0:T(8,128)} fusion(bf16[16,16,256]{2,1,0:T(8,128)(2,1)} %collective-permute-done.14, bf16[16,16,256]{2,1,0:T(8,128)(2,1)} %collective-permute-done.13, bf16[16,16,256]{2,1,0:T(8,128)(2,1)} %collective-permute-done.12, bf16[16,16,256]{2,1,0:T(8,128)(2,1)} %collective-permute-done.11, ...), kind=kLoop, calls=%fused_computation.55 | loop fusion | flops 2031616 | bytes 2359296 | tf_op jit(solution)/shard_map/add | solution.py:64
  199.2 4.5 %fusion.2 = bf16[1,16,256,256]{3,2,1,0:T(8,128)(2,1)} fusion(f32[1,16,256,256]{3,2,1,0:T(8,128)} %copy-done.3, bf16[16,16,256,1]{2,1,0,3:T(8,128)(2,1)S(1)} %bitcast.221, bf16[16,1,1,16,16,256]{5,4,3,2,1,0:T(8,128)(2,1)S(1)} %copy-done.5, f32[256]{0:T(256)S(1)} %copy-done.13), kind=kOutput, calls=%fused_computation.7 | convolution fusion | flops 540016640 | bytes 8520704 | tf_op jit(solution)/shard_map/Jjb,Jsajc->sabc/dot_general | solution.py:87
  203.7 8.6 %all-to-all-done.2 = f32[256,1,256]{2,1,0:T(1,128)S(1)} async-done(((f32[256,1,256]{2,1,0:T(1,128)}), f32[256,1,256]{2,1,0:T(1,128)S(1)}, u32[]{:S(2)}, u32[]{:S(2)}) %all-to-all-start.2) | async-done | bytes 262176 | tf_op jit(solution)/shard_map/all_to_all | solution.py:93
  (54 shorter events, 6.0 us)
Async XLA Ops:
  0.6 65.1 %copy-start = (bf16[256,256]{1,0:T(8,128)(2,1)S(1)}, bf16[256,256]{1,0:T(8,128)(2,1)}, u32[]{:S(2)}) copy-start(bf16[256,256]{1,0:T(8,128)(2,1)} %param.14) | copy-start | bytes 393220
  1.7 2.5 %copy-start.2 = (bf16[1,4096,256]{2,1,0:T(8,128)(2,1)S(1)}, bf16[1,4096,256]{2,1,0:T(8,128)(2,1)}, u32[]{:S(2)}) copy-start(bf16[1,4096,256]{2,1,0:T(8,128)(2,1)} %param.8) | copy-start | bytes 6291460
  1.7 2.9 %copy-start.6 = (bf16[1,4096,256]{2,1,0:T(8,128)(2,1)S(1)}, bf16[1,4096,256]{2,1,0:T(8,128)(2,1)}, u32[]{:S(2)}) copy-start(bf16[1,4096,256]{2,1,0:T(8,128)(2,1)} %param.9) | copy-start | bytes 6291460
  1.7 2.9 %copy-start.13 = (f32[256]{0:T(256)S(1)}, f32[256]{0:T(256)}, u32[]{:S(2)}) copy-start(f32[256]{0:T(256)} %param.10) | copy-start | bytes 3076
  63.8 0.9 copy-start.8
  64.7 1.6 copy-start.4
  76.6 61.9 %all-to-all-start.1 = ((bf16[16,1,2,16,16,256]{5,4,3,2,1,0:T(8,128)(2,1)}), bf16[16,1,2,16,16,256]{5,4,3,2,1,0:T(8,128)(2,1)}, u32[]{:S(2)}, u32[]{:S(2)}) async-start(bf16[16,1,2,16,16,256]{5,4,3,2,1,0:T(8,128)(2,1)} %maximum_bitcast_fusion), calls=%async_computation.1 | async-start | bytes 8388608 | tf_op jit(solution)/shard_map/all_to_all | solution.py:77
  91.9 56.8 %collective-permute-start = (bf16[16,16,256]{2,1,0:T(8,128)(2,1)S(1)}, bf16[16,16,256]{2,1,0:T(8,128)(2,1)S(1)}, u32[]{:S(2)}, u32[]{:S(2)}) collective-permute-start(bf16[16,16,256]{2,1,0:T(8,128)(2,1)S(1)} %bitcast.229), channel_id=1, source_target_pairs={{0,16},{16,32},{32,48},{48,64},{64,80},{80,96},{96,112},{112,128},... | collective-permute-start | bytes 393224 | tf_op jit(solution)/shard_map/ppermute | solution.py:64
  95.0 60.1 %collective-permute-start.1 = (bf16[16,16,256]{2,1,0:T(8,128)(2,1)S(1)}, bf16[16,16,256]{2,1,0:T(8,128)(2,1)S(1)}, u32[]{:S(2)}, u32[]{:S(2)}) collective-permute-start(bf16[16,16,256]{2,1,0:T(8,128)(2,1)S(1)} %bitcast.228), channel_id=1, source_target_pairs={{0,32},{16,48},{32,64},{48,80},{64,96},{80,112},{96,128},{112,144}... | collective-permute-start | bytes 393224 | tf_op jit(solution)/shard_map/ppermute | solution.py:64
  99.2 57.0 %collective-permute-start.2 = (bf16[16,16,256]{2,1,0:T(8,128)(2,1)}, bf16[16,16,256]{2,1,0:T(8,128)(2,1)S(1)}, u32[]{:S(2)}, u32[]{:S(2)}) collective-permute-start(bf16[16,16,256]{2,1,0:T(8,128)(2,1)} %bitcast.206), channel_id=1, source_target_pairs={{0,48},{16,64},{32,80},{48,96},{64,112},{80,128},{96,144},{112,160... | collective-permute-start | bytes 393224 | tf_op jit(solution)/shard_map/ppermute | solution.py:64
  102.6 56.7 %collective-permute-start.3 = (bf16[16,16,256]{2,1,0:T(8,128)(2,1)}, bf16[16,16,256]{2,1,0:T(8,128)(2,1)S(1)}, u32[]{:S(2)}, u32[]{:S(2)}) collective-permute-start(bf16[16,16,256]{2,1,0:T(8,128)(2,1)} %bitcast.205), channel_id=1, source_target_pairs={{0,64},{16,80},{32,96},{48,112},{64,128},{80,144},{96,160},{112,17... | collective-permute-start | bytes 393224 | tf_op jit(solution)/shard_map/ppermute | solution.py:64
  103.9 59.2 %collective-permute-start.4 = (bf16[16,16,256]{2,1,0:T(8,128)(2,1)}, bf16[16,16,256]{2,1,0:T(8,128)(2,1)S(1)}, u32[]{:S(2)}, u32[]{:S(2)}) collective-permute-start(bf16[16,16,256]{2,1,0:T(8,128)(2,1)} %bitcast.204), channel_id=1, source_target_pairs={{0,80},{16,96},{32,112},{48,128},{64,144},{80,160},{96,176},{112,1... | collective-permute-start | bytes 393224 | tf_op jit(solution)/shard_map/ppermute | solution.py:64
  138.5 24.6 %copy-start.7 = (bf16[1,4096,256]{2,1,0:T(8,128)(2,1)S(1)}, bf16[1,4096,256]{2,1,0:T(8,128)(2,1)}, u32[]{:S(2)}) copy-start(bf16[1,4096,256]{2,1,0:T(8,128)(2,1)} %param.9) | copy-start | bytes 6291460
  148.7 20.0 %collective-permute-start.5 = (bf16[16,16,256]{2,1,0:T(8,128)(2,1)}, bf16[16,16,256]{2,1,0:T(8,128)(2,1)S(1)}, u32[]{:S(2)}, u32[]{:S(2)}) collective-permute-start(bf16[16,16,256]{2,1,0:T(8,128)(2,1)} %bitcast.203), channel_id=1, source_target_pairs={{0,96},{16,112},{32,128},{48,144},{64,160},{80,176},{96,192},{112,... | collective-permute-start | bytes 393224 | tf_op jit(solution)/shard_map/ppermute | solution.py:64
  155.1 14.7 %collective-permute-start.6 = (bf16[16,16,256]{2,1,0:T(8,128)(2,1)}, bf16[16,16,256]{2,1,0:T(8,128)(2,1)S(1)}, u32[]{:S(2)}, u32[]{:S(2)}) collective-permute-start(bf16[16,16,256]{2,1,0:T(8,128)(2,1)} %bitcast.227), channel_id=1, source_target_pairs={{0,112},{16,128},{32,144},{48,160},{64,176},{80,192},{96,208},{112... | collective-permute-start | bytes 393224 | tf_op jit(solution)/shard_map/ppermute | solution.py:64
  156.2 15.7 %collective-permute-start.7 = (bf16[16,16,256]{2,1,0:T(8,128)(2,1)}, bf16[16,16,256]{2,1,0:T(8,128)(2,1)S(1)}, u32[]{:S(2)}, u32[]{:S(2)}) collective-permute-start(bf16[16,16,256]{2,1,0:T(8,128)(2,1)} %bitcast.226), channel_id=1, source_target_pairs={{0,128},{16,144},{32,160},{48,176},{64,192},{80,208},{96,224},{112... | collective-permute-start | bytes 393224 | tf_op jit(solution)/shard_map/ppermute | solution.py:64
  159.3 13.0 %collective-permute-start.8 = (bf16[16,16,256]{2,1,0:T(8,128)(2,1)S(1)}, bf16[16,16,256]{2,1,0:T(8,128)(2,1)S(1)}, u32[]{:S(2)}, u32[]{:S(2)}) collective-permute-start(bf16[16,16,256]{2,1,0:T(8,128)(2,1)S(1)} %bitcast.225), channel_id=1, source_target_pairs={{0,144},{16,160},{32,176},{48,192},{64,208},{80,224},{96,240},{112... | collective-permute-start | bytes 393224 | tf_op jit(solution)/shard_map/ppermute | solution.py:64
  163.1 14.4 %collective-permute-start.9 = (bf16[16,16,256]{2,1,0:T(8,128)(2,1)S(1)}, bf16[16,16,256]{2,1,0:T(8,128)(2,1)S(1)}, u32[]{:S(2)}, u32[]{:S(2)}) collective-permute-start(bf16[16,16,256]{2,1,0:T(8,128)(2,1)S(1)} %bitcast.224), channel_id=1, source_target_pairs={{0,160},{16,176},{32,192},{48,208},{64,224},{80,240},{96,0},{112,1... | collective-permute-start | bytes 393224 | tf_op jit(solution)/shard_map/ppermute | solution.py:64
  166.7 15.3 %copy-start.3 = (f32[1,16,256,256]{3,2,1,0:T(8,128)}, f32[1,16,256,256]{3,2,1,0:T(8,128)S(1)}, u32[]{:S(2)}) copy-start(f32[1,16,256,256]{3,2,1,0:T(8,128)S(1)} %get-tuple-element.4) | copy-start | bytes 12582916
  168.6 28.2 %collective-permute-start.10 = (bf16[16,16,256]{2,1,0:T(8,128)(2,1)}, bf16[16,16,256]{2,1,0:T(8,128)(2,1)}, u32[]{:S(2)}, u32[]{:S(2)}) collective-permute-start(bf16[16,16,256]{2,1,0:T(8,128)(2,1)} %bitcast.198), channel_id=1, source_target_pairs={{0,176},{16,192},{32,208},{48,224},{64,240},{80,0},{96,16},{112,32... | collective-permute-start | bytes 393224 | tf_op jit(solution)/shard_map/ppermute | solution.py:64
  169.8 27.1 %collective-permute-start.11 = (bf16[16,16,256]{2,1,0:T(8,128)(2,1)}, bf16[16,16,256]{2,1,0:T(8,128)(2,1)}, u32[]{:S(2)}, u32[]{:S(2)}) collective-permute-start(bf16[16,16,256]{2,1,0:T(8,128)(2,1)} %bitcast.197), channel_id=1, source_target_pairs={{0,192},{16,208},{32,224},{48,240},{64,0},{80,16},{96,32},{112,48}... | collective-permute-start | bytes 393224 | tf_op jit(solution)/shard_map/ppermute | solution.py:64
  171.8 10.2 %copy-start.10 = (bf16[16,16,256]{2,1,0:T(8,128)(2,1)}, bf16[16,16,256]{2,1,0:T(8,128)(2,1)S(1)}, u32[]{:S(2)}) copy-start(bf16[16,16,256]{2,1,0:T(8,128)(2,1)S(1)} %collective-permute-done.7) | copy-start | bytes 393220
  171.8 25.0 %collective-permute-start.12 = (bf16[16,16,256]{2,1,0:T(8,128)(2,1)}, bf16[16,16,256]{2,1,0:T(8,128)(2,1)}, u32[]{:S(2)}, u32[]{:S(2)}) collective-permute-start(bf16[16,16,256]{2,1,0:T(8,128)(2,1)} %bitcast.196), channel_id=1, source_target_pairs={{0,208},{16,224},{32,240},{48,0},{64,16},{80,32},{96,48},{112,64},... | collective-permute-start | bytes 393224 | tf_op jit(solution)/shard_map/ppermute | solution.py:64
  172.3 9.8 %copy-start.11 = (bf16[16,16,256]{2,1,0:T(8,128)(2,1)}, bf16[16,16,256]{2,1,0:T(8,128)(2,1)S(1)}, u32[]{:S(2)}) copy-start(bf16[16,16,256]{2,1,0:T(8,128)(2,1)S(1)} %collective-permute-done.8) | copy-start | bytes 393220
  172.3 24.6 %collective-permute-start.13 = (bf16[16,16,256]{2,1,0:T(8,128)(2,1)}, bf16[16,16,256]{2,1,0:T(8,128)(2,1)}, u32[]{:S(2)}, u32[]{:S(2)}) collective-permute-start(bf16[16,16,256]{2,1,0:T(8,128)(2,1)} %bitcast.195), channel_id=1, source_target_pairs={{0,224},{16,240},{32,0},{48,16},{64,32},{80,48},{96,64},{112,80},{... | collective-permute-start | bytes 393224 | tf_op jit(solution)/shard_map/ppermute | solution.py:64
  177.5 4.6 %copy-start.12 = (bf16[16,16,256]{2,1,0:T(8,128)(2,1)}, bf16[16,16,256]{2,1,0:T(8,128)(2,1)S(1)}, u32[]{:S(2)}) copy-start(bf16[16,16,256]{2,1,0:T(8,128)(2,1)S(1)} %collective-permute-done.9) | copy-start | bytes 393220
  177.5 19.4 %collective-permute-start.14 = (bf16[16,16,256]{2,1,0:T(8,128)(2,1)}, bf16[16,16,256]{2,1,0:T(8,128)(2,1)}, u32[]{:S(2)}, u32[]{:S(2)}) collective-permute-start(bf16[16,16,256]{2,1,0:T(8,128)(2,1)} %bitcast.194), channel_id=1, source_target_pairs={{0,240},{16,0},{32,16},{48,32},{64,48},{80,64},{96,80},{112,96},{1... | collective-permute-start | bytes 393224 | tf_op jit(solution)/shard_map/ppermute | solution.py:64
  182.1 17.1 %copy-start.5 = (bf16[16,1,1,16,16,256]{5,4,3,2,1,0:T(8,128)(2,1)S(1)}, bf16[16,1,1,16,16,256]{5,4,3,2,1,0:T(8,128)(2,1)}, u32[]{:S(2)}) copy-start(bf16[16,1,1,16,16,256]{5,4,3,2,1,0:T(8,128)(2,1)} %get-tuple-element.6) | copy-start | bytes 6291460
  182.1 17.1 %copy-start.9 = (bf16[256,256]{1,0:T(8,128)(2,1)S(1)}, bf16[256,256]{1,0:T(8,128)(2,1)}, u32[]{:S(2)}) copy-start(bf16[256,256]{1,0:T(8,128)(2,1)} %param.12) | copy-start | bytes 393220
  182.9 29.3 %all-to-all-start.2 = ((f32[256,1,256]{2,1,0:T(1,128)}), f32[256,1,256]{2,1,0:T(1,128)S(1)}, u32[]{:S(2)}, u32[]{:S(2)}) async-start(f32[256,1,256]{2,1,0:T(1,128)} %broadcast_in_dim.14), calls=%async_computation.2 | async-start | bytes 524288 | tf_op jit(solution)/shard_map/all_to_all | solution.py:93
  199.2 14.0 %copy-start.1 = (bf16[256,256]{1,0:T(8,128)(2,1)S(1)}, bf16[256,256]{1,0:T(8,128)(2,1)}, u32[]{:S(2)}) copy-start(bf16[256,256]{1,0:T(8,128)(2,1)} %param.14) | copy-start | bytes 393220

commit v4 on v2

--- a/solution.py
+++ b/solution.py
@@ -52,11 +52,31 @@
     )
     kernel_term = jnp.sum(grad_weighted * second_mix.astype(f32), axis=0)
     scene_parts = lax.axis_size("scene")
-    term_by_dest = kernel_term.reshape(scene_parts, block_len // scene_parts, chunk, channels)
-    term_spread = lax.all_to_all(
-        term_by_dest.astype(bf16), "scene", split_axis=0, concat_axis=0, tiled=True
-    )
-    kernel_grad = jnp.sum(term_spread.astype(f32), axis=0)
+    inner = 4 if scene_parts % 4 == 0 else 1
+    outer = scene_parts // inner
+    scene_index = lax.axis_index("scene")
+    outer_index = scene_index // inner
+    inner_index = scene_index % inner
+    term_by_dest = kernel_term.reshape(outer, inner, block_len // scene_parts, chunk, channels)
+    term_sent = term_by_dest.astype(bf16)
+    partial = lax.dynamic_index_in_dim(term_by_dest, outer_index, 0, False)
+    for shift in range(1, outer):
+        piece = lax.dynamic_index_in_dim(term_sent, (outer_index + shift) % outer, 0, False)
+        pairs = [
+            (o * inner + k, ((o + shift) % outer) * inner + k)
+            for o in range(outer)
+            for k in range(inner)
+        ]
+        partial = partial + lax.ppermute(piece, "scene", pairs).astype(f32)
+    kernel_grad = lax.dynamic_index_in_dim(partial, inner_index, 0, False)
+    for shift in range(1, inner):
+        piece = lax.dynamic_index_in_dim(partial, (inner_index + shift) % inner, 0, False)
+        pairs = [
+            (o * inner + k, o * inner + (k + shift) % inner)
+            for o in range(outer)
+            for k in range(inner)
+        ]
+        kernel_grad = kernel_grad + lax.ppermute(piece, "scene", pairs)
     grad_second = (grad_weighted * kernel_f).astype(bf16)
     grad_first = jnp.einsum(
         "ia,sijc->sajc", across_mix, grad_second, preferred_element_type=f32

time: 233 us -> 193 us (0.83)
  waiting for transfers between devices: 100 us -> 40.1 us
  starting transfers between devices: 33.9 us -> 44 us
  local copies, waits for them, and re-layouts: 17.1 us -> 23.9 us
  other arithmetic: 7.53 us -> 11.4 us
    all_to_all x1 -> x0, waiting for transfers between devices: 40 us -> none  [on_device(): lax.all_to_all(term_by_dest.astype(bf16), 'scene', split_axis=0, concat_a...]
    all_to_all x1, waiting for transfers between devices: 52 us -> 14.7 us  [on_device(): lax.all_to_all(back, 'seq', split_axis=0, concat_axis=0, tiled=True)]
    ppermute x0 -> x6, waiting for transfers between devices: none -> 16.5 us  [the longest x3 16.5 us: on_device(): partial = partial + lax.ppermute(piece, 'scene', pairs).astype(f32)]
    ppermute x0 -> x6, starting transfers between devices: none -> 14.6 us  [the longest x3 9.58 us: on_device(): kernel_grad = kernel_grad + lax.ppermute(piece, 'scene', pairs)]
    all_to_all x1 -> x0, starting transfers between devices: 10.1 us -> none  [on_device(): lax.all_to_all(term_by_dest.astype(bf16), 'scene', split_axis=0, concat_a...]
    reshape x0 -> x2, local copies, waits for them, and re-layouts: none -> 9.86 us  [on_device(): kernel_term.reshape(outer, inner, block_len // scene_parts, chunk, channels)]
    all_to_all x1, starting transfers between devices: 18.1 us -> 23.9 us  [on_device(): lax.all_to_all(jnp.broadcast_to(gain_term, (devices, channels)), ('scene'...]
    add x0 -> x2, other arithmetic: none -> 3.53 us  [the longest x1 1.9 us: on_device(): kernel_grad = kernel_grad + lax.ppermute(piece, 'scene', pairs)]
  transfers between devices with their start and end apart: 3 -> 8, of which waited for: 3 -> 4; matrix products, arithmetic and copies ran while one was open for 8% -> 15% of each run, Pallas kernels for 0% -> 0%
where the time goes in v4:
time: 193 us; the launch traced here: 192 us
  blocking collectives  55.9 us (29%)
  starting transfers between devices  44 us (23%)
  waiting for transfers between devices  40.1 us (21%)
  local copies, waits for them, and re-layouts  23.9 us (12%)
  matrix products  16.3 us (8%)
  other arithmetic  11.4 us (6%)
    all_to_all x1, blocking collectives, on_device(): lax.all_to_all(outgoing, 'seq', split_axis=0, concat_axis=0, tiled=True)  55.9 us
    all_to_all x1, starting transfers between devices, on_device(): lax.all_to_all(jnp.broadcast_to(gain_term, (devices, channels)), ('scene'...  23.9 us
    ppermute x3, waiting for transfers between devices, on_device(): partial = partial + lax.ppermute(piece, 'scene', pairs).astype(f32)  16.5 us
    all_to_all x1, waiting for transfers between devices, on_device(): lax.all_to_all(back, 'seq', split_axis=0, concat_axis=0, tiled=True)  14.7 us
    reshape x2, local copies, waits for them, and re-layouts, on_device(): kernel_term.reshape(outer, inner, block_len // scene_parts, chunk, channels)  9.86 us
    ppermute x3, starting transfers between devices, on_device(): kernel_grad = kernel_grad + lax.ppermute(piece, 'scene', pairs)  9.58 us
    all_to_all x1, waiting for transfers between devices, on_device(): lax.all_to_all(jnp.broadcast_to(gain_term, (devices, channels)), ('scene'...  8.92 us
    all_to_all x1, starting transfers between devices, on_device(): lax.all_to_all(back, 'seq', split_axis=0, concat_axis=0, tiled=True)  5.55 us
  transfers between devices with their start and end apart: 8, of which 4 were waited for; matrix products, arithmetic and copies ran while one was open for 15% of the time, Pallas kernels for 0%

profile of v4, /device:TPU:1, one launch (start us, length us, event | category | flops | bytes accessed | tf_op | source)
XLA Modules:
  0.0 192.4 jit_solution(7938115967004199320)
XLA Ops:
  0.6 0.0 copy-start
  0.6 1.0 copy.59
  1.7 3.5 %multiply_convert_fusion = bf16[1,4096,256]{2,1,0:T(8,128)(2,1)S(1)} fusion(f32[256]{0:T(256)} %param.10, bf16[1,4096,256]{2,1,0:T(8,128)(2,1)} %param.8, bf16[1,4096,256]{2,1,0:T(8,128)(2,1)} %param.9), kind=kLoop, calls=%fused_computation.18 | loop fusion | flops 9437184 | bytes 6292480 | tf_op jit(solution)/shard_map/convert_element_type | solution.py:24
  5.2 0.0 copy-start.2
  5.2 0.0 copy-start.8
  5.3 0.7 convert_bitcast_fusion.1
  6.0 0.8 copy-done.2
  6.8 0.7 convert_bitcast_fusion.2
  7.6 0.4 pad_maximum_fusion
  7.9 0.5 copy.60
  8.5 55.9 %all_to_all.16 = bf16[16,2,1,16,16,256]{5,4,3,2,1,0:T(8,128)(2,1)S(1)} all-to-all(bf16[16,2,1,16,16,256]{5,4,3,2,1,0:T(8,128)(2,1)S(1)} %copy.60), channel_id=1, replica_groups=mesh['scene'=16,'seq'=16] {'seq'}, dimensions={0} | all-to-all | bytes 8388608 | tf_op jit(solution)/shard_map/all_to_all | solution.py:34
  64.4 0.3 copy.110
  64.7 0.0 copy-start.7
  64.7 0.4 fusion.41
  65.2 0.5 copy-done.7
  65.6 1.0 fusion.21
  66.7 3.2 %fusion.3 = (f32[1,256,16,256]{3,1,2,0:T(8,128)}, f32[16,256,256]{1,2,0:T(8,128)S(1)}) fusion(bf16[16,256,256]{1,2,0:T(8,128)(2,1)S(1)} %fusion.21, bf16[256,256]{1,0:T(8,128)(2,1)S(1)} %copy-done, bf16[256,16,256]{2,1,0:T(8,128)(2,1)S(1)} %bitcast.187), kind=kOutput, calls=%fused_computation.9 | convolution fusion | flops 538968064 | bytes 12713984 | tf_op jit(solution)/shard_map/pi,spjc->sijc/dot_general | solution.py:50
  69.9 1.2 fusion.24
  71.1 1.3 fusion.27
  72.3 1.2 copy.68
  73.5 1.2 copy.67
  74.7 2.3 %maximum_bitcast_fusion = bf16[16,1,2,16,16,256]{5,4,3,2,1,0:T(8,128)(2,1)} fusion(bf16[1,16,1,16,16,256]{5,4,3,2,1,0:T(8,128)(2,1)S(1)} %copy.68, bf16[1,16,1,16,16,256]{5,4,3,2,1,0:T(8,128)(2,1)S(1)} %copy.67), kind=kLoop, calls=%fused_computation.5 | loop fusion | flops 2097152 | bytes 8388608 | tf_op jit(solution)/shard_map/transpose | solution.py:91
  77.1 5.5 %all-to-all-start.1 = ((bf16[16,1,2,16,16,256]{5,4,3,2,1,0:T(8,128)(2,1)}), bf16[16,1,2,16,16,256]{5,4,3,2,1,0:T(8,128)(2,1)}, u32[]{:S(2)}, u32[]{:S(2)}) async-start(bf16[16,1,2,16,16,256]{5,4,3,2,1,0:T(8,128)(2,1)} %maximum_bitcast_fusion), calls=%async_computation.1 | async-start | bytes 8388608 | tf_op jit(solution)/shard_map/all_to_all | solution.py:92
  82.6 4.4 %copy.105 = bf16[4,4,16,16,256]{4,3,2,1,0:T(8,128)(2,1)S(1)} copy(f32[4,4,16,16,256]{4,2,1,0,3:T(8,128)} %bitcast.181) | data formatting | bytes 6291456 | tf_op jit(solution)/shard_map/reshape | solution.py:60
  87.0 0.9 dynamic-slice_bitcast_fusion.2
  88.0 1.3 collective-permute-start
  89.3 2.6 %collective-permute-start.1 = (bf16[4,16,16,256]{3,2,1,0:T(8,128)(2,1)S(1)}, bf16[4,16,16,256]{3,2,1,0:T(8,128)(2,1)}, u32[]{:S(2)}, u32[]{:S(2)}) collective-permute-start(bf16[4,16,16,256]{3,2,1,0:T(8,128)(2,1)S(1)} %get-tuple-element.12), channel_id=1, source_target_pairs={{0,128},{16,144},{32,160},{48,176},{64,192},{80,208},{96,224},{112... | collective-permute-start | bytes 1572872 | tf_op jit(solution)/shard_map/ppermute | solution.py:70
  91.9 1.1 collective-permute-start.2
  93.0 5.4 %copy.71 = f32[4,4,16,16,256]{4,3,2,1,0:T(8,128)S(1)} copy(f32[4,4,16,16,256]{4,2,1,0,3:T(8,128)} %bitcast.182) | data formatting | bytes 8388608 | tf_op jit(solution)/shard_map/reshape | solution.py:60
  98.4 4.2 %collective-permute-done = bf16[4,16,16,256]{3,2,1,0:T(8,128)(2,1)} collective-permute-done((bf16[4,16,16,256]{3,2,1,0:T(8,128)(2,1)}, bf16[4,16,16,256]{3,2,1,0:T(8,128)(2,1)}, u32[]{:S(2)}, u32[]{:S(2)}) %collective-permute-start) | collective-permute-done | bytes 524320 | tf_op jit(solution)/shard_map/ppermute | solution.py:70
  102.6 12.3 %collective-permute-done.1 = bf16[4,16,16,256]{3,2,1,0:T(8,128)(2,1)} collective-permute-done((bf16[4,16,16,256]{3,2,1,0:T(8,128)(2,1)S(1)}, bf16[4,16,16,256]{3,2,1,0:T(8,128)(2,1)}, u32[]{:S(2)}, u32[]{:S(2)}) %collective-permute-start.1) | collective-permute-done | bytes 524320 | tf_op jit(solution)/shard_map/ppermute | solution.py:70
  114.9 1.6 fusion.33
  116.6 0.9 dynamic-slice_bitcast_fusion.5
  117.5 3.0 %collective-permute-start.3 = (f32[16,16,256]{2,1,0:T(8,128)}, f32[16,16,256]{2,1,0:T(8,128)}, u32[]{:S(2)}, u32[]{:S(2)}) collective-permute-start(f32[16,16,256]{2,1,0:T(8,128)} %get-tuple-element.13), channel_id=1, source_target_pairs={{0,16},{16,32},{32,48},{48,0},{64,80},{80,96},{96,112},{112,64},{1... | collective-permute-start | bytes 786440 | tf_op jit(solution)/shard_map/ppermute | solution.py:79
  120.5 4.2 %collective-permute-start.4 = (f32[16,16,256]{2,1,0:T(8,128)}, f32[16,16,256]{2,1,0:T(8,128)}, u32[]{:S(2)}, u32[]{:S(2)}) collective-permute-start(f32[16,16,256]{2,1,0:T(8,128)} %get-tuple-element.15), channel_id=1, source_target_pairs={{0,32},{16,48},{32,0},{48,16},{64,96},{80,112},{96,64},{112,80},{1... | collective-permute-start | bytes 786440 | tf_op jit(solution)/shard_map/ppermute | solution.py:79
  124.7 2.4 %collective-permute-start.5 = (f32[16,16,256]{2,1,0:T(8,128)}, f32[16,16,256]{2,1,0:T(8,128)}, u32[]{:S(2)}, u32[]{:S(2)}) collective-permute-start(f32[16,16,256]{2,1,0:T(8,128)} %get-tuple-element.14), channel_id=1, source_target_pairs={{0,48},{16,0},{32,16},{48,32},{64,112},{80,64},{96,80},{112,96},{1... | collective-permute-start | bytes 786440 | tf_op jit(solution)/shard_map/ppermute | solution.py:79
  127.1 14.7 %all-to-all-done.1 = bf16[16,1,2,16,16,256]{5,4,3,2,1,0:T(8,128)(2,1)} async-done(((bf16[16,1,2,16,16,256]{5,4,3,2,1,0:T(8,128)(2,1)}), bf16[16,1,2,16,16,256]{5,4,3,2,1,0:T(8,128)(2,1)}, u32[]{:S(2)}, u32[]{:S(2)}) %all-to-all-start.1) | async-done | bytes 4194336 | tf_op jit(solution)/shard_map/all_to_all | solution.py:92
  141.8 4.0 %fusion.40 = (bf16[16,1,1,16,16,256]{5,4,3,2,1,0:T(8,128)(2,1)}, bf16[16,1,1,16,16,256]{5,4,3,2,1,0:T(8,128)(2,1)S(1)}) fusion(bf16[16,1,2,16,16,256]{5,4,3,2,1,0:T(8,128)(2,1)} %all-to-all-done.1), kind=kLoop, calls=%fused_computation.58 | loop fusion | bytes 8388608 | tf_op jit(solution)/shard_map/slice | solution.py:102
  145.8 3.6 %fusion.6 = (f32[1,16,256,256]{3,2,1,0:T(8,128)S(1)}, bf16[1,16,256,256]{3,2,1,0:T(8,128)(2,1)}) fusion(f32[256]{0:T(256)S(1)} %copy-done.9, bf16[1,4096,256]{2,1,0:T(8,128)(2,1)S(1)} %copy-done.2, bf16[256,16,16,1]{0,2,1,3:T(8,128)(2,1)S(1)} %bitcast.196, bf16[16,1,1,16,16,256]{5,4,3,2,1,0:T(8,128)(2,1)S(1)} %get-tuple-element.7, ...), kind=kOutput, calls=%fused_computation.14 | convolution fusion | flops 552599552 | bytes 12715008 | tf_op jit(solution)/shard_map/qJj,Jsajc->saqc/dot_general | solution.py:93
  149.5 0.7 multiply_reduce_fusion
  150.2 1.2 copy-done.3
  151.4 0.9 broadcast_in_dim.14
  152.3 23.9 %all-to-all-start.2 = ((f32[256,1,256]{2,1,0:T(1,128)}), f32[256,1,256]{2,1,0:T(1,128)S(1)}, u32[]{:S(2)}, u32[]{:S(2)}) async-start(f32[256,1,256]{2,1,0:T(1,128)} %broadcast_in_dim.14), calls=%async_computation.2 | async-start | bytes 524288 | tf_op jit(solution)/shard_map/all_to_all | solution.py:108
  176.2 1.9 fusion.35
  178.1 4.6 %fusion.2 = bf16[1,16,256,256]{3,2,1,0:T(8,128)(2,1)} fusion(f32[1,16,256,256]{3,2,1,0:T(8,128)} %copy-done.3, bf16[16,16,256,1]{2,1,0,3:T(8,128)(2,1)} %bitcast.193, bf16[16,1,1,16,16,256]{5,4,3,2,1,0:T(8,128)(2,1)S(1)} %copy-done.5, f32[256]{0:T(256)S(1)} %copy-done.9), kind=kOutput, calls=%fused_computation.7 | convolution fusion | flops 540016640 | bytes 8520704 | tf_op jit(solution)/shard_map/Jjb,Jsajc->sabc/dot_general | solution.py:102
  182.7 8.9 %all-to-all-done.2 = f32[256,1,256]{2,1,0:T(1,128)S(1)} async-done(((f32[256,1,256]{2,1,0:T(1,128)}), f32[256,1,256]{2,1,0:T(1,128)S(1)}, u32[]{:S(2)}, u32[]{:S(2)}) %all-to-all-start.2) | async-done | bytes 262176 | tf_op jit(solution)/shard_map/all_to_all | solution.py:108
  191.6 0.3 reduce_sum.20
  191.9 0.6 broadcast_multiply_fusion
  (17 shorter events, 0.0 us)
Async XLA Ops:
  0.6 66.0 %copy-start = (bf16[256,256]{1,0:T(8,128)(2,1)S(1)}, bf16[256,256]{1,0:T(8,128)(2,1)}, u32[]{:S(2)}) copy-start(bf16[256,256]{1,0:T(8,128)(2,1)} %param.14) | copy-start | bytes 393220
  5.2 1.6 copy-start.2
  5.2 1.6 copy-start.8
  64.7 0.9 copy-start.7
  66.6 3.2 %copy-start.4 = (bf16[256,16,256]{2,1,0:T(8,128)(2,1)S(1)}, bf16[256,16,256]{2,1,0:T(8,128)(2,1)}, u32[]{:S(2)}) copy-start(bf16[256,16,256]{2,1,0:T(8,128)(2,1)} %param.11) | copy-start | bytes 6291460
  77.1 64.7 %all-to-all-start.1 = ((bf16[16,1,2,16,16,256]{5,4,3,2,1,0:T(8,128)(2,1)}), bf16[16,1,2,16,16,256]{5,4,3,2,1,0:T(8,128)(2,1)}, u32[]{:S(2)}, u32[]{:S(2)}) async-start(bf16[16,1,2,16,16,256]{5,4,3,2,1,0:T(8,128)(2,1)} %maximum_bitcast_fusion), calls=%async_computation.1 | async-start | bytes 8388608 | tf_op jit(solution)/shard_map/all_to_all | solution.py:92
  88.0 14.6 %collective-permute-start = (bf16[4,16,16,256]{3,2,1,0:T(8,128)(2,1)}, bf16[4,16,16,256]{3,2,1,0:T(8,128)(2,1)}, u32[]{:S(2)}, u32[]{:S(2)}) collective-permute-start(bf16[4,16,16,256]{3,2,1,0:T(8,128)(2,1)} %get-tuple-element.10), channel_id=1, source_target_pairs={{0,64},{16,80},{32,96},{48,112},{64,128},{80,144},{96,160},{112,17... | collective-permute-start | bytes 1572872 | tf_op jit(solution)/shard_map/ppermute | solution.py:70
  89.3 25.7 %collective-permute-start.1 = (bf16[4,16,16,256]{3,2,1,0:T(8,128)(2,1)S(1)}, bf16[4,16,16,256]{3,2,1,0:T(8,128)(2,1)}, u32[]{:S(2)}, u32[]{:S(2)}) collective-permute-start(bf16[4,16,16,256]{3,2,1,0:T(8,128)(2,1)S(1)} %get-tuple-element.12), channel_id=1, source_target_pairs={{0,128},{16,144},{32,160},{48,176},{64,192},{80,208},{96,224},{112... | collective-permute-start | bytes 1572872 | tf_op jit(solution)/shard_map/ppermute | solution.py:70
  91.9 23.0 %collective-permute-start.2 = (bf16[4,16,16,256]{3,2,1,0:T(8,128)(2,1)S(1)}, bf16[4,16,16,256]{3,2,1,0:T(8,128)(2,1)}, u32[]{:S(2)}, u32[]{:S(2)}) collective-permute-start(bf16[4,16,16,256]{3,2,1,0:T(8,128)(2,1)S(1)} %get-tuple-element.11), channel_id=1, source_target_pairs={{0,192},{16,208},{32,224},{48,240},{64,0},{80,16},{96,32},{112,48}... | collective-permute-start | bytes 1572872 | tf_op jit(solution)/shard_map/ppermute | solution.py:70
  117.5 58.6 %collective-permute-start.3 = (f32[16,16,256]{2,1,0:T(8,128)}, f32[16,16,256]{2,1,0:T(8,128)}, u32[]{:S(2)}, u32[]{:S(2)}) collective-permute-start(f32[16,16,256]{2,1,0:T(8,128)} %get-tuple-element.13), channel_id=1, source_target_pairs={{0,16},{16,32},{32,48},{48,0},{64,80},{80,96},{96,112},{112,64},{1... | collective-permute-start | bytes 786440 | tf_op jit(solution)/shard_map/ppermute | solution.py:79
  120.5 55.7 %collective-permute-start.4 = (f32[16,16,256]{2,1,0:T(8,128)}, f32[16,16,256]{2,1,0:T(8,128)}, u32[]{:S(2)}, u32[]{:S(2)}) collective-permute-start(f32[16,16,256]{2,1,0:T(8,128)} %get-tuple-element.15), channel_id=1, source_target_pairs={{0,32},{16,48},{32,0},{48,16},{64,96},{80,112},{96,64},{112,80},{1... | collective-permute-start | bytes 786440 | tf_op jit(solution)/shard_map/ppermute | solution.py:79
  124.7 21.1 %copy-start.9 = (f32[256]{0:T(256)S(1)}, f32[256]{0:T(256)}, u32[]{:S(2)}) copy-start(f32[256]{0:T(256)} %param.10) | copy-start | bytes 3076
  124.7 51.5 %collective-permute-start.5 = (f32[16,16,256]{2,1,0:T(8,128)}, f32[16,16,256]{2,1,0:T(8,128)}, u32[]{:S(2)}, u32[]{:S(2)}) collective-permute-start(f32[16,16,256]{2,1,0:T(8,128)} %get-tuple-element.14), channel_id=1, source_target_pairs={{0,48},{16,0},{32,16},{48,32},{64,112},{80,64},{96,80},{112,96},{1... | collective-permute-start | bytes 786440 | tf_op jit(solution)/shard_map/ppermute | solution.py:79
  141.8 4.0 %copy-start.6 = (bf16[1,4096,256]{2,1,0:T(8,128)(2,1)S(1)}, bf16[1,4096,256]{2,1,0:T(8,128)(2,1)}, u32[]{:S(2)}) copy-start(bf16[1,4096,256]{2,1,0:T(8,128)(2,1)} %param.9) | copy-start | bytes 6291460
  149.5 1.9 %copy-start.3 = (f32[1,16,256,256]{3,2,1,0:T(8,128)}, f32[1,16,256,256]{3,2,1,0:T(8,128)S(1)}, u32[]{:S(2)}) copy-start(f32[1,16,256,256]{3,2,1,0:T(8,128)S(1)} %get-tuple-element.4) | copy-start | bytes 12582916
  151.4 26.7 %copy-start.5 = (bf16[16,1,1,16,16,256]{5,4,3,2,1,0:T(8,128)(2,1)S(1)}, bf16[16,1,1,16,16,256]{5,4,3,2,1,0:T(8,128)(2,1)}, u32[]{:S(2)}) copy-start(bf16[16,1,1,16,16,256]{5,4,3,2,1,0:T(8,128)(2,1)} %get-tuple-element.6) | copy-start | bytes 6291460
  152.3 39.3 %all-to-all-start.2 = ((f32[256,1,256]{2,1,0:T(1,128)}), f32[256,1,256]{2,1,0:T(1,128)S(1)}, u32[]{:S(2)}, u32[]{:S(2)}) async-start(f32[256,1,256]{2,1,0:T(1,128)} %broadcast_in_dim.14), calls=%async_computation.2 | async-start | bytes 524288 | tf_op jit(solution)/shard_map/all_to_all | solution.py:108
  178.1 14.4 %copy-start.1 = (bf16[256,256]{1,0:T(8,128)(2,1)S(1)}, bf16[256,256]{1,0:T(8,128)(2,1)}, u32[]{:S(2)}) copy-start(bf16[256,256]{1,0:T(8,128)(2,1)} %param.14) | copy-start | bytes 393220

commit v5 on v4

--- a/solution.py
+++ b/solution.py
@@ -69,14 +69,15 @@
         ]
         partial = partial + lax.ppermute(piece, "scene", pairs).astype(f32)
     kernel_grad = lax.dynamic_index_in_dim(partial, inner_index, 0, False)
+    partial_sent = partial.astype(bf16)
     for shift in range(1, inner):
-        piece = lax.dynamic_index_in_dim(partial, (inner_index + shift) % inner, 0, False)
+        piece = lax.dynamic_index_in_dim(partial_sent, (inner_index + shift) % inner, 0, False)
         pairs = [
             (o * inner + k, o * inner + (k + shift) % inner)
             for o in range(outer)
             for k in range(inner)
         ]
-        kernel_grad = kernel_grad + lax.ppermute(piece, "scene", pairs)
+        kernel_grad = kernel_grad + lax.ppermute(piece, "scene", pairs).astype(f32)
     grad_second = (grad_weighted * kernel_f).astype(bf16)
     grad_first = jnp.einsum(
         "ia,sijc->sajc", across_mix, grad_second, preferred_element_type=f32

time: 193 us -> 189 us (0.979)
  waiting for transfers between devices: 40.1 us -> 36.9 us
    all_to_all x1, waiting for transfers between devices: 14.7 us -> 11.8 us  [on_device(): lax.all_to_all(back, 'seq', split_axis=0, concat_axis=0, tiled=True)]
  transfers between devices with their start and end apart: 8 -> 8, of which waited for: 4 -> 4; matrix products, arithmetic and copies ran while one was open for 15% -> 16% of each run, Pallas kernels for 0% -> 0%
where the time goes in v5:
time: 189 us; the launch traced here: 188 us
  blocking collectives  55.9 us (30%)
  starting transfers between devices  42.5 us (22%)
  waiting for transfers between devices  36.9 us (20%)
  local copies, waits for them, and re-layouts  24.1 us (13%)
  matrix products  16.8 us (9%)
  other arithmetic  11.2 us (6%)
    all_to_all x1, blocking collectives, on_device(): lax.all_to_all(outgoing, 'seq', split_axis=0, concat_axis=0, tiled=True)  55.9 us
    all_to_all x1, starting transfers between devices, on_device(): lax.all_to_all(jnp.broadcast_to(gain_term, (devices, channels)), ('scene'...  22.4 us
    ppermute x3, waiting for transfers between devices, on_device(): partial = partial + lax.ppermute(piece, 'scene', pairs).astype(f32)  16.5 us
    all_to_all x1, waiting for transfers between devices, on_device(): lax.all_to_all(back, 'seq', split_axis=0, concat_axis=0, tiled=True)  11.8 us
    reshape x2, local copies, waits for them, and re-layouts, on_device(): kernel_term.reshape(outer, inner, block_len // scene_parts, chunk, channels)  9.86 us
    ppermute x3, starting transfers between devices, on_device(): kernel_grad = kernel_grad + lax.ppermute(piece, 'scene', pairs).astype(f32)  9.58 us
    all_to_all x1, waiting for transfers between devices, on_device(): lax.all_to_all(jnp.broadcast_to(gain_term, (devices, channels)), ('scene'...  8.54 us
    all_to_all x1, starting transfers between devices, on_device(): lax.all_to_all(back, 'seq', split_axis=0, concat_axis=0, tiled=True)  5.52 us
  transfers between devices with their start and end apart: 8, of which 4 were waited for; matrix products, arithmetic and copies ran while one was open for 16% of the time, Pallas kernels for 0%

profile of v5, /device:TPU:1, one launch (start us, length us, event | category | flops | bytes accessed | tf_op | source)
XLA Modules:
  0.0 188.3 jit_solution(1316267982988902602)
XLA Ops:
  0.6 0.0 copy-start
  0.6 1.0 copy.59
  1.7 3.5 %multiply_convert_fusion = bf16[1,4096,256]{2,1,0:T(8,128)(2,1)S(1)} fusion(f32[256]{0:T(256)} %param.10, bf16[1,4096,256]{2,1,0:T(8,128)(2,1)} %param.8, bf16[1,4096,256]{2,1,0:T(8,128)(2,1)} %param.9), kind=kLoop, calls=%fused_computation.18 | loop fusion | flops 9437184 | bytes 6292480 | tf_op jit(solution)/shard_map/convert_element_type | solution.py:24
  5.2 0.0 copy-start.2
  5.3 0.7 convert_bitcast_fusion.1
  6.0 0.8 copy-done.2
  6.8 0.7 convert_bitcast_fusion.2
  7.6 0.4 pad_maximum_fusion
  7.9 0.5 copy.60
  8.5 55.9 %all_to_all.16 = bf16[16,2,1,16,16,256]{5,4,3,2,1,0:T(8,128)(2,1)S(1)} all-to-all(bf16[16,2,1,16,16,256]{5,4,3,2,1,0:T(8,128)(2,1)S(1)} %copy.60), channel_id=1, replica_groups=mesh['scene'=16,'seq'=16] {'seq'}, dimensions={0} | all-to-all | bytes 8388608 | tf_op jit(solution)/shard_map/all_to_all | solution.py:34
  64.4 0.4 copy.110
  64.9 0.0 copy-start.6
  64.9 0.3 fusion.43
  65.2 0.6 copy-done.6
  65.8 1.0 fusion.21
  66.8 0.0 copy-start.4
  66.8 3.2 %fusion.3 = (f32[1,256,16,256]{3,1,2,0:T(8,128)}, f32[16,256,256]{1,2,0:T(8,128)S(1)}) fusion(bf16[16,256,256]{1,2,0:T(8,128)(2,1)S(1)} %fusion.21, bf16[256,256]{1,0:T(8,128)(2,1)S(1)} %copy-done, bf16[256,16,256]{2,1,0:T(8,128)(2,1)S(1)} %bitcast.188), kind=kOutput, calls=%fused_computation.9 | convolution fusion | flops 538968064 | bytes 12713984 | tf_op jit(solution)/shard_map/pi,spjc->sijc/dot_general | solution.py:50
  70.0 1.2 fusion.24
  71.2 1.3 fusion.27
  72.5 1.2 copy.68
  73.7 1.2 copy.67
  74.9 2.4 %maximum_bitcast_fusion = bf16[16,1,2,16,16,256]{5,4,3,2,1,0:T(8,128)(2,1)} fusion(bf16[1,16,1,16,16,256]{5,4,3,2,1,0:T(8,128)(2,1)S(1)} %copy.68, bf16[1,16,1,16,16,256]{5,4,3,2,1,0:T(8,128)(2,1)S(1)} %copy.67), kind=kLoop, calls=%fused_computation.5 | loop fusion | flops 2097152 | bytes 8388608 | tf_op jit(solution)/shard_map/transpose | solution.py:92
  77.2 5.5 %all-to-all-start.1 = ((bf16[16,1,2,16,16,256]{5,4,3,2,1,0:T(8,128)(2,1)}), bf16[16,1,2,16,16,256]{5,4,3,2,1,0:T(8,128)(2,1)}, u32[]{:S(2)}, u32[]{:S(2)}) async-start(bf16[16,1,2,16,16,256]{5,4,3,2,1,0:T(8,128)(2,1)} %maximum_bitcast_fusion), calls=%async_computation.1 | async-start | bytes 8388608 | tf_op jit(solution)/shard_map/all_to_all | solution.py:93
  82.8 4.4 %copy.105 = bf16[4,4,16,16,256]{4,3,2,1,0:T(8,128)(2,1)S(1)} copy(f32[4,4,16,16,256]{4,2,1,0,3:T(8,128)} %bitcast.182) | data formatting | bytes 6291456 | tf_op jit(solution)/shard_map/reshape | solution.py:60
  87.2 1.1 dynamic-slice_bitcast_fusion.2
  88.3 1.3 collective-permute-start
  89.6 2.6 %collective-permute-start.1 = (bf16[4,16,16,256]{3,2,1,0:T(8,128)(2,1)}, bf16[4,16,16,256]{3,2,1,0:T(8,128)(2,1)}, u32[]{:S(2)}, u32[]{:S(2)}) collective-permute-start(bf16[4,16,16,256]{3,2,1,0:T(8,128)(2,1)} %get-tuple-element.14), channel_id=1, source_target_pairs={{0,128},{16,144},{32,160},{48,176},{64,192},{80,208},{96,224},{112... | collective-permute-start | bytes 1572872 | tf_op jit(solution)/shard_map/ppermute | solution.py:70
  92.2 1.1 collective-permute-start.2
  93.3 5.4 %copy.71 = f32[4,4,16,16,256]{4,3,2,1,0:T(8,128)S(1)} copy(f32[4,4,16,16,256]{4,2,1,0,3:T(8,128)} %bitcast.183) | data formatting | bytes 8388608 | tf_op jit(solution)/shard_map/reshape | solution.py:60
  98.8 4.2 %collective-permute-done = bf16[4,16,16,256]{3,2,1,0:T(8,128)(2,1)S(1)} collective-permute-done((bf16[4,16,16,256]{3,2,1,0:T(8,128)(2,1)}, bf16[4,16,16,256]{3,2,1,0:T(8,128)(2,1)S(1)}, u32[]{:S(2)}, u32[]{:S(2)}) %collective-permute-start) | collective-permute-done | bytes 524320 | tf_op jit(solution)/shard_map/ppermute | solution.py:70
  102.9 12.3 %collective-permute-done.1 = bf16[4,16,16,256]{3,2,1,0:T(8,128)(2,1)} collective-permute-done((bf16[4,16,16,256]{3,2,1,0:T(8,128)(2,1)}, bf16[4,16,16,256]{3,2,1,0:T(8,128)(2,1)}, u32[]{:S(2)}, u32[]{:S(2)}) %collective-permute-start.1) | collective-permute-done | bytes 524320 | tf_op jit(solution)/shard_map/ppermute | solution.py:70
  115.3 1.7 fusion.40
  116.9 0.8 dynamic-slice_bitcast_fusion.5
  117.7 3.0 %collective-permute-start.3 = (bf16[16,16,256]{2,1,0:T(8,128)(2,1)}, bf16[16,16,256]{2,1,0:T(8,128)(2,1)S(1)}, u32[]{:S(2)}, u32[]{:S(2)}) collective-permute-start(bf16[16,16,256]{2,1,0:T(8,128)(2,1)} %get-tuple-element.15), channel_id=1, source_target_pairs={{0,16},{16,32},{32,48},{48,0},{64,80},{80,96},{96,112},{112,64},{1... | collective-permute-start | bytes 393224 | tf_op jit(solution)/shard_map/ppermute | solution.py:80
  120.7 4.2 %collective-permute-start.4 = (bf16[16,16,256]{2,1,0:T(8,128)(2,1)}, bf16[16,16,256]{2,1,0:T(8,128)(2,1)}, u32[]{:S(2)}, u32[]{:S(2)}) collective-permute-start(bf16[16,16,256]{2,1,0:T(8,128)(2,1)} %get-tuple-element.17), channel_id=1, source_target_pairs={{0,32},{16,48},{32,0},{48,16},{64,96},{80,112},{96,64},{112,80},{1... | collective-permute-start | bytes 393224 | tf_op jit(solution)/shard_map/ppermute | solution.py:80
  124.9 2.4 %collective-permute-start.5 = (bf16[16,16,256]{2,1,0:T(8,128)(2,1)}, bf16[16,16,256]{2,1,0:T(8,128)(2,1)}, u32[]{:S(2)}, u32[]{:S(2)}) collective-permute-start(bf16[16,16,256]{2,1,0:T(8,128)(2,1)} %get-tuple-element.16), channel_id=1, source_target_pairs={{0,48},{16,0},{32,16},{48,32},{64,112},{80,64},{96,80},{112,96},{1... | collective-permute-start | bytes 393224 | tf_op jit(solution)/shard_map/ppermute | solution.py:80
  127.3 11.8 %all-to-all-done.1 = bf16[16,1,2,16,16,256]{5,4,3,2,1,0:T(8,128)(2,1)} async-done(((bf16[16,1,2,16,16,256]{5,4,3,2,1,0:T(8,128)(2,1)}), bf16[16,1,2,16,16,256]{5,4,3,2,1,0:T(8,128)(2,1)}, u32[]{:S(2)}, u32[]{:S(2)}) %all-to-all-start.1) | async-done | bytes 4194336 | tf_op jit(solution)/shard_map/all_to_all | solution.py:93
  139.1 4.1 %fusion.42 = (bf16[16,1,1,16,16,256]{5,4,3,2,1,0:T(8,128)(2,1)}, bf16[16,1,1,16,16,256]{5,4,3,2,1,0:T(8,128)(2,1)S(1)}) fusion(bf16[16,1,2,16,16,256]{5,4,3,2,1,0:T(8,128)(2,1)} %all-to-all-done.1), kind=kLoop, calls=%fused_computation.59 | loop fusion | bytes 8388608 | tf_op jit(solution)/shard_map/slice | solution.py:103
  143.2 3.6 %fusion.6 = (f32[1,16,256,256]{3,2,1,0:T(8,128)S(1)}, bf16[1,16,256,256]{3,2,1,0:T(8,128)(2,1)}) fusion(f32[256]{0:T(256)S(1)} %copy-done.9, bf16[1,4096,256]{2,1,0:T(8,128)(2,1)S(1)} %copy-done.2, bf16[256,16,16,1]{0,2,1,3:T(8,128)(2,1)S(1)} %bitcast.197, bf16[16,1,1,16,16,256]{5,4,3,2,1,0:T(8,128)(2,1)S(1)} %get-tuple-element.9, ...), kind=kOutput, calls=%fused_computation.14 | convolution fusion | flops 552599552 | bytes 12715008 | tf_op jit(solution)/shard_map/qJj,Jsajc->saqc/dot_general | solution.py:94
  146.8 0.7 multiply_reduce_fusion
  147.5 1.2 copy-done.3
  148.8 0.8 broadcast_in_dim.14
  149.6 22.4 %all-to-all-start.2 = ((f32[256,1,256]{2,1,0:T(1,128)}), f32[256,1,256]{2,1,0:T(1,128)S(1)}, u32[]{:S(2)}, u32[]{:S(2)}) async-start(f32[256,1,256]{2,1,0:T(1,128)} %broadcast_in_dim.14), calls=%async_computation.2 | async-start | bytes 524288 | tf_op jit(solution)/shard_map/all_to_all | solution.py:109
  172.1 1.7 fusion.35
  173.8 5.1 %fusion.2 = bf16[1,16,256,256]{3,2,1,0:T(8,128)(2,1)} fusion(f32[1,16,256,256]{3,2,1,0:T(8,128)} %copy-done.3, bf16[16,16,256,1]{2,1,0,3:T(8,128)(2,1)S(1)} %bitcast.195, bf16[16,1,1,16,16,256]{5,4,3,2,1,0:T(8,128)(2,1)} %get-tuple-element.8, f32[256]{0:T(256)S(1)} %copy-done.9), kind=kOutput, calls=%fused_computation.7 | convolution fusion | flops 540016640 | bytes 8520704 | tf_op jit(solution)/shard_map/Jjb,Jsajc->sabc/dot_general | solution.py:103
  178.9 8.5 %all-to-all-done.2 = f32[256,1,256]{2,1,0:T(1,128)S(1)} async-done(((f32[256,1,256]{2,1,0:T(1,128)}), f32[256,1,256]{2,1,0:T(1,128)S(1)}, u32[]{:S(2)}, u32[]{:S(2)}) %all-to-all-start.2) | async-done | bytes 262176 | tf_op jit(solution)/shard_map/all_to_all | solution.py:109
  187.5 0.3 reduce_sum.20
  187.8 0.6 broadcast_multiply_fusion
  (17 shorter events, 0.0 us)
Async XLA Ops:
  0.6 66.2 %copy-start = (bf16[256,256]{1,0:T(8,128)(2,1)S(1)}, bf16[256,256]{1,0:T(8,128)(2,1)}, u32[]{:S(2)}) copy-start(bf16[256,256]{1,0:T(8,128)(2,1)} %param.14) | copy-start | bytes 393220
  5.2 1.6 copy-start.2
  5.2 1.6 copy-start.7
  64.9 0.9 copy-start.6
  66.8 3.2 %copy-start.4 = (bf16[256,16,256]{2,1,0:T(8,128)(2,1)S(1)}, bf16[256,16,256]{2,1,0:T(8,128)(2,1)}, u32[]{:S(2)}) copy-start(bf16[256,16,256]{2,1,0:T(8,128)(2,1)} %param.11) | copy-start | bytes 6291460
  77.2 61.9 %all-to-all-start.1 = ((bf16[16,1,2,16,16,256]{5,4,3,2,1,0:T(8,128)(2,1)}), bf16[16,1,2,16,16,256]{5,4,3,2,1,0:T(8,128)(2,1)}, u32[]{:S(2)}, u32[]{:S(2)}) async-start(bf16[16,1,2,16,16,256]{5,4,3,2,1,0:T(8,128)(2,1)} %maximum_bitcast_fusion), calls=%async_computation.1 | async-start | bytes 8388608 | tf_op jit(solution)/shard_map/all_to_all | solution.py:93
  88.3 14.6 %collective-permute-start = (bf16[4,16,16,256]{3,2,1,0:T(8,128)(2,1)}, bf16[4,16,16,256]{3,2,1,0:T(8,128)(2,1)S(1)}, u32[]{:S(2)}, u32[]{:S(2)}) collective-permute-start(bf16[4,16,16,256]{3,2,1,0:T(8,128)(2,1)} %get-tuple-element.12), channel_id=1, source_target_pairs={{0,64},{16,80},{32,96},{48,112},{64,128},{80,144},{96,160},{112,17... | collective-permute-start | bytes 1572872 | tf_op jit(solution)/shard_map/ppermute | solution.py:70
  89.6 25.7 %collective-permute-start.1 = (bf16[4,16,16,256]{3,2,1,0:T(8,128)(2,1)}, bf16[4,16,16,256]{3,2,1,0:T(8,128)(2,1)}, u32[]{:S(2)}, u32[]{:S(2)}) collective-permute-start(bf16[4,16,16,256]{3,2,1,0:T(8,128)(2,1)} %get-tuple-element.14), channel_id=1, source_target_pairs={{0,128},{16,144},{32,160},{48,176},{64,192},{80,208},{96,224},{112... | collective-permute-start | bytes 1572872 | tf_op jit(solution)/shard_map/ppermute | solution.py:70
  92.2 23.0 %collective-permute-start.2 = (bf16[4,16,16,256]{3,2,1,0:T(8,128)(2,1)S(1)}, bf16[4,16,16,256]{3,2,1,0:T(8,128)(2,1)}, u32[]{:S(2)}, u32[]{:S(2)}) collective-permute-start(bf16[4,16,16,256]{3,2,1,0:T(8,128)(2,1)S(1)} %get-tuple-element.13), channel_id=1, source_target_pairs={{0,192},{16,208},{32,224},{48,240},{64,0},{80,16},{96,32},{112,48}... | collective-permute-start | bytes 1572872 | tf_op jit(solution)/shard_map/ppermute | solution.py:70
  102.9 12.3 %copy-start.8 = (bf16[4,16,16,256]{3,2,1,0:T(8,128)(2,1)}, bf16[4,16,16,256]{3,2,1,0:T(8,128)(2,1)S(1)}, u32[]{:S(2)}) copy-start(bf16[4,16,16,256]{3,2,1,0:T(8,128)(2,1)S(1)} %collective-permute-done) | copy-start | bytes 1572868
  117.7 54.3 %collective-permute-start.3 = (bf16[16,16,256]{2,1,0:T(8,128)(2,1)}, bf16[16,16,256]{2,1,0:T(8,128)(2,1)S(1)}, u32[]{:S(2)}, u32[]{:S(2)}) collective-permute-start(bf16[16,16,256]{2,1,0:T(8,128)(2,1)} %get-tuple-element.15), channel_id=1, source_target_pairs={{0,16},{16,32},{32,48},{48,0},{64,80},{80,96},{96,112},{112,64},{1... | collective-permute-start | bytes 393224 | tf_op jit(solution)/shard_map/ppermute | solution.py:80
  120.7 51.4 %collective-permute-start.4 = (bf16[16,16,256]{2,1,0:T(8,128)(2,1)}, bf16[16,16,256]{2,1,0:T(8,128)(2,1)}, u32[]{:S(2)}, u32[]{:S(2)}) collective-permute-start(bf16[16,16,256]{2,1,0:T(8,128)(2,1)} %get-tuple-element.17), channel_id=1, source_target_pairs={{0,32},{16,48},{32,0},{48,16},{64,96},{80,112},{96,64},{112,80},{1... | collective-permute-start | bytes 393224 | tf_op jit(solution)/shard_map/ppermute | solution.py:80
  124.9 18.3 %copy-start.9 = (f32[256]{0:T(256)S(1)}, f32[256]{0:T(256)}, u32[]{:S(2)}) copy-start(f32[256]{0:T(256)} %param.10) | copy-start | bytes 3076
  124.9 47.1 %collective-permute-start.5 = (bf16[16,16,256]{2,1,0:T(8,128)(2,1)}, bf16[16,16,256]{2,1,0:T(8,128)(2,1)}, u32[]{:S(2)}, u32[]{:S(2)}) collective-permute-start(bf16[16,16,256]{2,1,0:T(8,128)(2,1)} %get-tuple-element.16), channel_id=1, source_target_pairs={{0,48},{16,0},{32,16},{48,32},{64,112},{80,64},{96,80},{112,96},{1... | collective-permute-start | bytes 393224 | tf_op jit(solution)/shard_map/ppermute | solution.py:80
  139.1 4.1 %copy-start.5 = (bf16[1,4096,256]{2,1,0:T(8,128)(2,1)S(1)}, bf16[1,4096,256]{2,1,0:T(8,128)(2,1)}, u32[]{:S(2)}) copy-start(bf16[1,4096,256]{2,1,0:T(8,128)(2,1)} %param.9) | copy-start | bytes 6291460
  146.8 1.9 %copy-start.3 = (f32[1,16,256,256]{3,2,1,0:T(8,128)}, f32[1,16,256,256]{3,2,1,0:T(8,128)S(1)}, u32[]{:S(2)}) copy-start(f32[1,16,256,256]{3,2,1,0:T(8,128)S(1)} %get-tuple-element.6) | copy-start | bytes 12582916
  149.6 37.9 %all-to-all-start.2 = ((f32[256,1,256]{2,1,0:T(1,128)}), f32[256,1,256]{2,1,0:T(1,128)S(1)}, u32[]{:S(2)}, u32[]{:S(2)}) async-start(f32[256,1,256]{2,1,0:T(1,128)} %broadcast_in_dim.14), calls=%async_computation.2 | async-start | bytes 524288 | tf_op jit(solution)/shard_map/all_to_all | solution.py:109
  173.8 14.5 %copy-start.1 = (bf16[256,256]{1,0:T(8,128)(2,1)S(1)}, bf16[256,256]{1,0:T(8,128)(2,1)}, u32[]{:S(2)}) copy-start(bf16[256,256]{1,0:T(8,128)(2,1)} %param.14) | copy-start | bytes 393220

commit v6 on v5

v6 whole, which is shorter than its diff:
```python
import jax
import jax.numpy as jnp
from jax import lax
from jax.sharding import PartitionSpec as P

CHANNEL_GROUPS = 2


def on_device(
    scene_x, cotangent, gate_gain, kernel, block_mix, across_mix, across_unmix, block_unmix
):
    f32 = jnp.float32
    bf16 = jnp.bfloat16
    scenes_here, row_count, channels = scene_x.shape
    block_len = block_mix.shape[0]
    local_a = row_count // block_len
    parts = lax.axis_size("seq")
    chunk = block_len // parts
    width = channels // CHANNEL_GROUPS
    mix_by_dest = block_mix.reshape(parts, chunk, block_len)
    unmix_by_dest = block_unmix.reshape(block_len, parts, chunk)

    def first_phase(g):
        cols = slice(g * width, (g + 1) * width)
        inputs = scene_x[:, :, cols].reshape(scenes_here, local_a, block_len, width)
        upstream = cotangent[:, :, cols].reshape(scenes_here, local_a, block_len, width)
        gain_g = gate_gain[cols]
        gate_pre = inputs.astype(f32) * gain_g
        gate_sig = jax.nn.sigmoid(gate_pre)
        grad_values = (upstream.astype(f32) * gate_pre * gate_sig).astype(bf16)
        first_mix = jnp.einsum(
            "Jjb,sabc->Jsajc", mix_by_dest, inputs, preferred_element_type=f32
        ).astype(bf16)
        grad_unmixed = jnp.einsum(
            "qJj,saqc->Jsajc", unmix_by_dest, grad_values, preferred_element_type=f32
        ).astype(bf16)
        return jnp.stack([first_mix, grad_unmixed], axis=1)

    def middle_phase(g, incoming):
        cols = slice(g * width, (g + 1) * width)
        kernel_f = kernel[:, :, cols].astype(f32)
        incoming = jnp.moveaxis(incoming, 2, 1)
        spread_mix = incoming[:, :, 0]
        spread_grad = incoming[:, :, 1]
        spread_mix = jnp.moveaxis(spread_mix, 1, 0).reshape(
            scenes_here, parts * local_a, chunk, width
        )
        spread_grad = jnp.moveaxis(spread_grad, 1, 0).reshape(
            scenes_here, parts * local_a, chunk, width
        )
        second_mix = jnp.einsum(
            "ia,sajc->sijc", across_mix, spread_mix, preferred_element_type=f32
        ).astype(bf16)
        weighted = (second_mix.astype(f32) * kernel_f).astype(bf16)
        unmixed = jnp.einsum(
            "pi,sijc->spjc", across_unmix, weighted, preferred_element_type=f32
        ).astype(bf16)
        grad_weighted = jnp.einsum(
            "pi,spjc->sijc", across_unmix, spread_grad, preferred_element_type=f32
        )
        kernel_term = jnp.sum(grad_weighted * second_mix.astype(f32), axis=0)
        grad_second = (grad_weighted * kernel_f).astype(bf16)
        grad_first = jnp.einsum(
            "ia,sijc->sajc", across_mix, grad_second, preferred_element_type=f32
        ).astype(bf16)
        back = jnp.stack(
            [
                unmixed.reshape(scenes_here, parts, local_a, chunk, width),
                grad_first.reshape(scenes_here, parts, local_a, chunk, width),
            ],
            axis=2,
        )
        return jnp.moveaxis(back, 1, 0), kernel_term

    def last_phase(g, returned):
        cols = slice(g * width, (g + 1) * width)
        inputs = scene_x[:, :, cols].reshape(scenes_here, local_a, block_len, width).astype(f32)
        upstream = cotangent[:, :, cols].reshape(scenes_here, local_a, block_len, width)
        upstream = upstream.astype(f32)
        gain_g = gate_gain[cols]
        gate_pre = inputs * gain_g
        gate_sig = jax.nn.sigmoid(gate_pre)
        values = jnp.einsum(
            "qJj,Jsajc->saqc", unmix_by_dest, returned[:, :, 0], preferred_element_type=f32
        )
        mixed_out = (values * gate_pre * gate_sig).astype(bf16)
        grad_gate = upstream * values * gate_sig * (1.0 + gate_pre * (1.0 - gate_sig))
        grad_input = (
            jnp.einsum(
                "Jjb,Jsajc->sabc", mix_by_dest, returned[:, :, 1], preferred_element_type=f32
            )
            + grad_gate * gain_g
        ).astype(bf16)
        gain_term = jnp.sum(inputs * grad_gate, axis=(0, 1, 2))
        return mixed_out, grad_input, gain_term

    outgoing = [first_phase(g) for g in range(CHANNEL_GROUPS)]
    incoming = [
        lax.all_to_all(o, "seq", split_axis=0, concat_axis=0, tiled=True) for o in outgoing
    ]
    middles = [middle_phase(g, incoming[g]) for g in range(CHANNEL_GROUPS)]
    returned = [
        lax.all_to_all(m[0], "seq", split_axis=0, concat_axis=0, tiled=True) for m in middles
    ]
    lasts = [last_phase(g, returned[g]) for g in range(CHANNEL_GROUPS)]
    mixed_out = jnp.concatenate([l[0] for l in lasts], axis=-1)
    grad_input = jnp.concatenate([l[1] for l in lasts], axis=-1)
    mixed_out = mixed_out.reshape(scenes_here, row_count, channels)
    grad_input = grad_input.reshape(scenes_here, row_count, channels)
    gain_term = jnp.concatenate([l[2] for l in lasts], axis=-1)
    kernel_term = jnp.concatenate([m[1] for m in middles], axis=-1)

    scene_parts = lax.axis_size("scene")
    inner = 4 if scene_parts % 4 == 0 else 1
    outer = scene_parts // inner
    scene_index = lax.axis_index("scene")
    outer_index = scene_index // inner
    inner_index = scene_index % inner
    term_by_dest = kernel_term.reshape(outer, inner, block_len // scene_parts, chunk, channels)
    term_sent = term_by_dest.astype(bf16)
    partial = lax.dynamic_index_in_dim(term_by_dest, outer_index, 0, False)
    for shift in range(1, outer):
        piece = lax.dynamic_index_in_dim(term_sent, (outer_index + shift) % outer, 0, False)
        pairs = [
            (o * inner + k, ((o + shift) % outer) * inner + k)
            for o in range(outer)
            for k in range(inner)
        ]
        partial = partial + lax.ppermute(piece, "scene", pairs).astype(f32)
    kernel_grad = lax.dynamic_index_in_dim(partial, inner_index, 0, False)
    partial_sent = partial.astype(bf16)
    for shift in range(1, inner):
        piece = lax.dynamic_index_in_dim(partial_sent, (inner_index + shift) % inner, 0, False)
        pairs = [
            (o * inner + k, o * inner + (k + shift) % inner)
            for o in range(outer)
            for k in range(inner)
        ]
        kernel_grad = kernel_grad + lax.ppermute(piece, "scene", pairs).astype(f32)

    devices = lax.axis_size(("scene", "seq"))
    gain_spread = lax.all_to_all(
        jnp.broadcast_to(gain_term, (devices, channels)),
        ("scene", "seq"),
        split_axis=0,
        concat_axis=0,
        tiled=True,
    )
    gain_total = jnp.sum(gain_spread, axis=0)
    total_rows = scenes_here * scene_parts * local_a * parts * block_len
    grad_scale = 1.0 / jnp.sqrt(jnp.float32(total_rows))
    return (mixed_out, grad_input, kernel_grad, gain_total * grad_scale)


def solution(mesh):
    return jax.shard_map(
        on_device,
        mesh=mesh,
        in_specs=(
            P("scene", "seq", None),
            P("scene", "seq", None),
            P(),
            P(None, "seq", None),
            P(),
            P(),
            P(),
            P(),
        ),
        out_specs=(P("scene", "seq", None), P("scene", "seq", None), P("scene", "seq", None), P()),
        check_vma=False,
    )
```

time: 189 us -> 226 us (1.20)
  blocking collectives: 55.9 us -> 0 us
  waiting for transfers between devices: 36.9 us -> 75.5 us
  local copies, waits for them, and re-layouts: 24.1 us -> 56.4 us
  matrix products: 16.8 us -> 24.9 us
  other arithmetic: 11.2 us -> 18.4 us
  starting transfers between devices: 42.5 us -> 48.7 us
    all_to_all x1 -> x0, blocking collectives: 55.9 us -> none  [on_device(): lax.all_to_all(outgoing, 'seq', split_axis=0, concat_axis=0, tiled=True)]
    all_to_all x1 -> x4, waiting for transfers between devices: 11.8 us -> 45.9 us  [the longest x2 33.5 us: on_device(): lax.all_to_all(o, 'seq', split_axis=0, concat_axis=0, tiled=True)]
    all_to_all x1 -> x4, starting transfers between devices: 5.52 us -> 26.1 us  [the longest x2 13.6 us: on_device(): lax.all_to_all(o, 'seq', split_axis=0, concat_axis=0, tiled=True)]
    convert_element_type x0 -> x8, local copies, waits for them, and re-layouts: none -> 18.1 us  [the longest x2 5.92 us: first_phase(): gate_pre = inputs.astype(f32) * gain_g]
    all_to_all x1, starting transfers between devices: 22.4 us -> 10.4 us  [on_device(): lax.all_to_all(jnp.broadcast_to(gain_term, (devices, channels)), ('scene'...]
    reshape x2 -> x0, local copies, waits for them, and re-layouts: 9.86 us -> none  [on_device(): kernel_term.reshape(outer, inner, block_len // scene_parts, chunk, channels)]
    ppermute x3, waiting for transfers between devices: 16.5 us -> 25.6 us  [on_device(): partial = partial + lax.ppermute(piece, 'scene', pairs).astype(f32)]
    convert_element_type x1 -> x4, other arithmetic: 3.54 us -> 11.8 us  [the longest x2 5.58 us: first_phase(): grad_values = (upstream.astype(f32) * gate_pre * gate_sig).astype(bf16)]
  transfers between devices with their start and end apart: 8 -> 11, of which waited for: 4 -> 6; matrix products, arithmetic and copies ran while one was open for 16% -> 34% of each run, Pallas kernels for 0% -> 0%
where the time goes in v6:
time: 226 us; the launch traced here: 225 us
  waiting for transfers between devices  75.5 us (33%)
  local copies, waits for them, and re-layouts  56.4 us (25%)
  starting transfers between devices  48.7 us (22%)
  matrix products  24.9 us (11%)
  other arithmetic  18.4 us (8%)
    all_to_all x2, waiting for transfers between devices, on_device(): lax.all_to_all(o, 'seq', split_axis=0, concat_axis=0, tiled=True)  33.5 us
    ppermute x3, waiting for transfers between devices, on_device(): partial = partial + lax.ppermute(piece, 'scene', pairs).astype(f32)  25.6 us
    all_to_all x2, starting transfers between devices, on_device(): lax.all_to_all(o, 'seq', split_axis=0, concat_axis=0, tiled=True)  13.6 us
    all_to_all x2, starting transfers between devices, on_device(): lax.all_to_all(m[0], 'seq', split_axis=0, concat_axis=0, tiled=True)  12.5 us
    all_to_all x2, waiting for transfers between devices, on_device(): lax.all_to_all(m[0], 'seq', split_axis=0, concat_axis=0, tiled=True)  12.4 us
    all_to_all x1, starting transfers between devices, on_device(): lax.all_to_all(jnp.broadcast_to(gain_term, (devices, channels)), ('scene'...  10.4 us
    ppermute x3, starting transfers between devices, on_device(): kernel_grad = kernel_grad + lax.ppermute(piece, 'scene', pairs).astype(f32)  8.38 us
    dot_general x2, matrix products, last_phase(): jnp.einsum('qJj,Jsajc->saqc', unmix_by_dest, returned[:, :, 0], preferred...  6.43 us
  transfers between devices with their start and end apart: 11, of which 6 were waited for; matrix products, arithmetic and copies ran while one was open for 34% of the time, Pallas kernels for 0%

profile of v6, /device:TPU:1, one launch (start us, length us, event | category | flops | bytes accessed | tf_op | source)
XLA Modules:
  0.0 224.9 jit_solution(8452067909105541745)
XLA Ops:
  0.7 4.3 %slice_convert_fusion.3 = (f32[1,4096,128]{2,1,0:T(8,128)}, f32[1,4096,128]{2,1,0:T(8,128)}, bf16[1,4096,128]{2,1,0:T(8,128)(2,1)S(1)}, bf16[1,4096,128]{2,1,0:T(8,128)(2,1)}) fusion(bf16[1,4096,256]{2,1,0:T(8,128)(2,1)} %param.8), kind=kLoop, calls=%fused_computation.113 | loop fusion | flops 1048576 | bytes 8388608 | tf_op jit(solution)/shard_map/convert_element_type | solution.py:28
  5.1 3.9 %multiply_convert_fusion.1 = (bf16[1,4096,128]{2,1,0:T(8,128)(2,1)}, bf16[1,4096,128]{2,1,0:T(8,128)(2,1)S(1)}) fusion(f32[128]{0:T(128)S(1)} %get-tuple-element.36, bf16[1,4096,256]{2,1,0:T(8,128)(2,1)S(1)} %copy-done.2, bf16[1,4096,256]{2,1,0:T(8,128)(2,1)} %param.8, f32[128]{0:T(128)S(1)} %get-tuple-element.37), kind=kLoop, calls=%fused_computation.45 | loop fusion | flops 9437184 | bytes 6292480 | tf_op jit(solution)/shard_map/convert_element_type | solution.py:30
  10.6 1.9 copy.124
  12.5 7.3 %all-to-all-start.2 = ((bf16[16,2,1,16,16,128]{5,4,3,2,1,0:T(8,128)(2,1)}), bf16[16,2,1,16,16,128]{5,4,3,2,1,0:T(8,128)(2,1)S(1)}, u32[]{:S(2)}, u32[]{:S(2)}) async-start(bf16[16,2,1,16,16,128]{5,4,3,2,1,0:T(8,128)(2,1)} %copy.124), calls=%async_computation.2 | async-start | bytes 4194304 | tf_op jit(solution)/shard_map/all_to_all | solution.py:99
  21.7 1.9 copy.114
  23.6 23.8 %all-to-all-done.2 = bf16[16,2,1,16,16,128]{5,4,3,2,1,0:T(8,128)(2,1)S(1)} async-done(((bf16[16,2,1,16,16,128]{5,4,3,2,1,0:T(8,128)(2,1)}), bf16[16,2,1,16,16,128]{5,4,3,2,1,0:T(8,128)(2,1)S(1)}, u32[]{:S(2)}, u32[]{:S(2)}) %all-to-all-start.2) | async-done | bytes 2097184 | tf_op jit(solution)/shard_map/all_to_all | solution.py:99
  47.4 6.3 %all-to-all-start = ((bf16[16,2,1,16,16,128]{5,4,3,2,1,0:T(8,128)(2,1)}), bf16[16,2,1,16,16,128]{5,4,3,2,1,0:T(8,128)(2,1)}, u32[]{:S(2)}, u32[]{:S(2)}) async-start(bf16[16,2,1,16,16,128]{5,4,3,2,1,0:T(8,128)(2,1)} %copy.114), calls=%async_computation | async-start | bytes 4194304 | tf_op jit(solution)/shard_map/all_to_all | solution.py:99
  53.7 3.3 %fusion.69 = (bf16[256,16,128]{2,1,0:T(8,128)(2,1)}, bf16[256,16,128]{2,1,0:T(8,128)(2,1)}) fusion(bf16[256,16,256]{2,1,0:T(8,128)(2,1)} %param.11), kind=kLoop, calls=%fused_computation.118 | loop fusion | bytes 4194304 | tf_op jit(solution)/shard_map/slice | solution.py:41
  57.0 1.6 copy.156
  59.0 1.4 fusion.70
  60.9 1.4 fusion.26
  62.3 2.6 %copy.130 = bf16[1,256,16,128]{3,2,1,0:T(8,128)(2,1)} copy(bf16[1,256,16,128]{1,3,2,0:T(8,128)(2,1)} %fusion.26) | data formatting | bytes 2097152 | tf_op jit(solution)/shard_map/convert_element_type | solution.py:65
  65.0 3.2 %fusion.7 = (f32[1,256,16,128]{1,3,2,0:T(8,128)}, bf16[1,16,128,256]{3,2,1,0:T(8,128)(2,1)S(1)}) fusion(f32[16,128,256]{2,1,0:T(8,128)S(1)} %fusion.46, bf16[256,256]{1,0:T(8,128)(2,1)S(1)} %copy-done, bf16[256,16,128]{2,1,0:T(8,128)(2,1)} %bitcast.299), kind=kOutput, calls=%fused_computation.23 | convolution fusion | flops 270008320 | bytes 6422528 | tf_op jit(solution)/shard_map/ia,sajc->sijc/dot_general | solution.py:51
  69.9 1.7 copy.131
  71.7 9.7 %all-to-all-done = bf16[16,2,1,16,16,128]{5,4,3,2,1,0:T(8,128)(2,1)} async-done(((bf16[16,2,1,16,16,128]{5,4,3,2,1,0:T(8,128)(2,1)}), bf16[16,2,1,16,16,128]{5,4,3,2,1,0:T(8,128)(2,1)}, u32[]{:S(2)}, u32[]{:S(2)}) %all-to-all-start) | async-done | bytes 2097184 | tf_op jit(solution)/shard_map/all_to_all | solution.py:99
  81.4 6.3 %all-to-all-start.3 = ((bf16[16,1,2,16,16,128]{5,4,3,2,1,0:T(8,128)(2,1)}), bf16[16,1,2,16,16,128]{5,4,3,2,1,0:T(8,128)(2,1)}, u32[]{:S(2)}, u32[]{:S(2)}) async-start(bf16[16,1,2,16,16,128]{5,4,3,2,1,0:T(8,128)(2,1)} %copy.131), calls=%async_computation.3 | async-start | bytes 4194304 | tf_op jit(solution)/shard_map/all_to_all | solution.py:103
  88.4 2.0 copy.187
  92.3 1.4 fusion.21
  93.7 2.6 %copy.120 = bf16[1,256,16,128]{3,2,1,0:T(8,128)(2,1)} copy(bf16[1,256,16,128]{1,3,2,0:T(8,128)(2,1)} %fusion.21) | data formatting | bytes 2097152 | tf_op jit(solution)/shard_map/convert_element_type | solution.py:65
  96.4 3.1 %fusion.8 = (f32[1,256,16,128]{1,3,2,0:T(8,128)}, bf16[1,16,128,256]{3,2,1,0:T(8,128)(2,1)S(1)}) fusion(f32[16,128,256]{2,1,0:T(8,128)S(1)} %fusion.49, bf16[256,256]{1,0:T(8,128)(2,1)S(1)} %copy-done, bf16[256,16,128]{2,1,0:T(8,128)(2,1)} %bitcast.300), kind=kOutput, calls=%fused_computation.25 | convolution fusion | flops 270008320 | bytes 6422528 | tf_op jit(solution)/shard_map/ia,sajc->sijc/dot_general | solution.py:51
  101.3 1.7 copy.121
  102.9 12.4 %all-to-all-done.3 = bf16[16,1,2,16,16,128]{5,4,3,2,1,0:T(8,128)(2,1)} async-done(((bf16[16,1,2,16,16,128]{5,4,3,2,1,0:T(8,128)(2,1)}), bf16[16,1,2,16,16,128]{5,4,3,2,1,0:T(8,128)(2,1)}, u32[]{:S(2)}, u32[]{:S(2)}) %all-to-all-start.3) | async-done | bytes 2097184 | tf_op jit(solution)/shard_map/all_to_all | solution.py:103
  115.3 6.3 %all-to-all-start.1 = ((bf16[16,1,2,16,16,128]{5,4,3,2,1,0:T(8,128)(2,1)}), bf16[16,1,2,16,16,128]{5,4,3,2,1,0:T(8,128)(2,1)}, u32[]{:S(2)}, u32[]{:S(2)}) async-start(bf16[16,1,2,16,16,128]{5,4,3,2,1,0:T(8,128)(2,1)} %copy.121), calls=%async_computation.1 | async-start | bytes 4194304 | tf_op jit(solution)/shard_map/all_to_all | solution.py:103
  121.6 2.2 copy.141
  123.9 3.1 %copy.140 = f32[1,256,16,128]{3,2,1,0:T(8,128)} copy(f32[1,256,16,128]{1,3,2,0:T(8,128)} %get-tuple-element.40) | data formatting | bytes 4194304 | tf_op jit(solution)/shard_map/mul | solution.py:61
  127.0 1.9 fusion
  129.8 2.7 %collective-permute-start.2 = (bf16[4,16,16,256]{3,2,1,0:T(8,128)(2,1)}, bf16[4,16,16,256]{3,2,1,0:T(8,128)(2,1)}, u32[]{:S(2)}, u32[]{:S(2)}) collective-permute-start(bf16[4,16,16,256]{3,2,1,0:T(8,128)(2,1)} %get-tuple-element.15), channel_id=1, source_target_pairs={{0,192},{16,208},{32,224},{48,240},{64,0},{80,16},{96,32},{112,48}... | collective-permute-start | bytes 1572872 | tf_op jit(solution)/shard_map/ppermute | solution.py:129
  133.6 21.4 %collective-permute-done.2 = bf16[4,16,16,256]{3,2,1,0:T(8,128)(2,1)} collective-permute-done((bf16[4,16,16,256]{3,2,1,0:T(8,128)(2,1)}, bf16[4,16,16,256]{3,2,1,0:T(8,128)(2,1)}, u32[]{:S(2)}, u32[]{:S(2)}) %collective-permute-start.2) | collective-permute-done | bytes 524320 | tf_op jit(solution)/shard_map/ppermute | solution.py:129
  155.0 4.2 %collective-permute-done = bf16[4,16,16,256]{3,2,1,0:T(8,128)(2,1)} collective-permute-done((bf16[4,16,16,256]{3,2,1,0:T(8,128)(2,1)S(1)}, bf16[4,16,16,256]{3,2,1,0:T(8,128)(2,1)}, u32[]{:S(2)}, u32[]{:S(2)}) %collective-permute-start) | collective-permute-done | bytes 524320 | tf_op jit(solution)/shard_map/ppermute | solution.py:129
  159.2 2.0 fusion.64
  161.9 5.1 %collective-permute-start.5 = (bf16[16,16,256]{2,1,0:T(8,128)(2,1)}, bf16[16,16,256]{2,1,0:T(8,128)(2,1)S(1)}, u32[]{:S(2)}, u32[]{:S(2)}) collective-permute-start(bf16[16,16,256]{2,1,0:T(8,128)(2,1)} %get-tuple-element.34), channel_id=1, source_target_pairs={{0,48},{16,0},{32,16},{48,32},{64,112},{80,64},{96,80},{112,96},{1... | collective-permute-start | bytes 393224 | tf_op jit(solution)/shard_map/ppermute | solution.py:139
  168.2 2.1 collective-permute-start.3
  170.3 1.7 slice_convert_fusion.1
  172.0 3.0 %copy.133 = f32[1,16,256,128]{2,3,1,0:T(8,128)} copy(f32[1,16,256,128]{3,2,1,0:T(8,128)} %bitcast.298) | data formatting | bytes 4194304 | tf_op jit(solution)/shard_map/convert_element_type | solution.py:28
  174.9 2.9 %copy.138 = f32[1,16,256,128]{2,3,1,0:T(8,128)} copy(f32[1,16,256,128]{3,2,1,0:T(8,128)} %bitcast.294) | data formatting | bytes 4194304 | tf_op jit(solution)/shard_map/convert_element_type | solution.py:30
  177.8 3.0 %copy.123 = f32[1,16,256,128]{2,3,1,0:T(8,128)} copy(f32[1,16,256,128]{3,2,1,0:T(8,128)} %bitcast.297) | data formatting | bytes 4194304 | tf_op jit(solution)/shard_map/convert_element_type | solution.py:28
  180.8 1.8 copy.136
  183.3 1.8 fusion.53
  185.0 2.1 fusion.67
  187.9 3.2 %multiply_reduce_fusion = (f32[128]{0:T(128)S(1)}, f32[1,16,256,128]{2,3,1,0:T(8,128)}, bf16[1,16,256,128]{2,3,1,0:T(8,128)(2,1)}) fusion(f32[1,16,256,128]{2,3,1,0:T(8,128)S(1)} %copy-done.14, f32[128]{0:T(128)S(1)} %get-tuple-element.37, f32[1,16,256,128]{2,3,1,0:T(8,128)S(1)} %copy-done.15, bf16[256,16,16,1]{0,2,1,3:T(8,128)(2,1)S(1)} %bitcast.319, ...), kind=kOutput, calls=%fused_computation.40 | convolution fusion | flops 276299648 | bytes 8520704 | tf_op jit(solution)/shard_map/qJj,Jsajc->saqc/dot_general | solution.py:83
  191.1 2.1 fusion.66
  193.9 3.2 %multiply_reduce_fusion.1 = (f32[128]{0:T(128)S(1)}, f32[1,16,256,128]{2,3,1,0:T(8,128)}, bf16[1,16,256,128]{2,3,1,0:T(8,128)(2,1)}) fusion(f32[1,16,256,128]{2,3,1,0:T(8,128)S(1)} %copy-done.12, f32[128]{0:T(128)S(1)} %get-tuple-element.36, f32[1,16,256,128]{2,3,1,0:T(8,128)S(1)} %copy-done.13, bf16[256,16,16,1]{0,2,1,3:T(8,128)(2,1)S(1)} %bitcast.320, ...), kind=kOutput, calls=%fused_computation.41 | convolution fusion | flops 276299648 | bytes 8520704 | tf_op jit(solution)/shard_map/qJj,Jsajc->saqc/dot_general | solution.py:83
  198.0 10.4 %all-to-all-start.4 = ((f32[256,1,256]{2,1,0:T(1,128)}), f32[256,1,256]{2,1,0:T(1,128)}, u32[]{:S(2)}, u32[]{:S(2)}) async-start(f32[256,1,256]{2,1,0:T(1,128)} %broadcast_in_dim.27), calls=%async_computation.4 | async-start | bytes 524288 | tf_op jit(solution)/shard_map/all_to_all | solution.py:142
  208.5 3.3 %fusion.5 = bf16[1,16,256,128]{2,3,1,0:T(8,128)(2,1)} fusion(f32[1,16,256,128]{2,3,1,0:T(8,128)} %get-tuple-element.7, bf16[16,16,256,1]{2,1,0,3:T(8,128)(2,1)S(1)} %bitcast.313, bf16[16,1,1,16,16,128]{5,4,3,2,1,0:T(8,128)(2,1)S(1)} %get-tuple-element.21, f32[128]{0:T(128)S(1)} %get-tuple-element.37), kind=kOutput, calls=%fused_computation.19 | convolution fusion | flops 270008320 | bytes 4325888 | tf_op jit(solution)/shard_map/Jjb,Jsajc->sabc/dot_general | solution.py:89
  211.9 2.4 %copy.134 = bf16[1,16,256,256]{3,2,1,0:T(8,128)(2,1)} copy(bf16[1,16,256,256]{2,3,1,0:T(8,128)(2,1)S(1)} %pad_maximum_fusion.3) | data formatting | bytes 4194304 | tf_op jit(solution)/shard_map/concatenate | solution.py:106
  214.3 2.2 fusion.6
  216.7 2.4 %copy.139 = bf16[1,16,256,256]{3,2,1,0:T(8,128)(2,1)} copy(bf16[1,16,256,256]{2,3,1,0:T(8,128)(2,1)S(1)} %pad_maximum_fusion.4) | data formatting | bytes 4194304 | tf_op jit(solution)/shard_map/concatenate | solution.py:107
  219.1 3.9 %all-to-all-done.4 = f32[256,1,256]{2,1,0:T(1,128)} async-done(((f32[256,1,256]{2,1,0:T(1,128)}), f32[256,1,256]{2,1,0:T(1,128)}, u32[]{:S(2)}, u32[]{:S(2)}) %all-to-all-start.4) | async-done | bytes 262176 | tf_op jit(solution)/shard_map/all_to_all | solution.py:142
  (81 shorter events, 19.7 us)
Async XLA Ops:
  0.6 60.2 %copy-start = (bf16[256,256]{1,0:T(8,128)(2,1)S(1)}, bf16[256,256]{1,0:T(8,128)(2,1)}, u32[]{:S(2)}) copy-start(bf16[256,256]{1,0:T(8,128)(2,1)} %param.13) | copy-start | bytes 393220
  0.6 4.4 %copy-start.22 = (f32[256]{0:T(256)S(1)}, f32[256]{0:T(256)}, u32[]{:S(2)}) copy-start(f32[256]{0:T(256)} %param.10) | copy-start | bytes 3076
  0.7 4.4 %copy-start.21 = (bf16[256,256]{1,0:T(8,128)(2,1)S(1)}, bf16[256,256]{1,0:T(8,128)(2,1)}, u32[]{:S(2)}) copy-start(bf16[256,256]{1,0:T(8,128)(2,1)} %param.15) | copy-start | bytes 393220
  0.7 4.5 %copy-start.2 = (bf16[1,4096,256]{2,1,0:T(8,128)(2,1)S(1)}, bf16[1,4096,256]{2,1,0:T(8,128)(2,1)}, u32[]{:S(2)}) copy-start(bf16[1,4096,256]{2,1,0:T(8,128)(2,1)} %param.9) | copy-start | bytes 6291460
  5.1 14.7 %copy-start.16 = (bf16[256,256]{0,1:T(8,128)(2,1)}, bf16[256,256]{0,1:T(8,128)(2,1)S(1)}, u32[]{:S(2)}) copy-start(bf16[256,256]{0,1:T(8,128)(2,1)S(1)} %copy.113) | copy-start | bytes 393220
  9.1 0.9 copy-start.11
  12.5 7.3 %copy-start.6 = (bf16[1,4096,128]{2,1,0:T(8,128)(2,1)S(1)}, bf16[1,4096,128]{2,1,0:T(8,128)(2,1)}, u32[]{:S(2)}) copy-start(bf16[1,4096,128]{2,1,0:T(8,128)(2,1)} %get-tuple-element.12) | copy-start | bytes 3145732
  12.5 34.9 %all-to-all-start.2 = ((bf16[16,2,1,16,16,128]{5,4,3,2,1,0:T(8,128)(2,1)}), bf16[16,2,1,16,16,128]{5,4,3,2,1,0:T(8,128)(2,1)S(1)}, u32[]{:S(2)}, u32[]{:S(2)}) async-start(bf16[16,2,1,16,16,128]{5,4,3,2,1,0:T(8,128)(2,1)} %copy.124), calls=%async_computation.2 | async-start | bytes 4194304 | tf_op jit(solution)/shard_map/all_to_all | solution.py:99
  19.8 1.2 copy-start.9
  47.4 34.0 %all-to-all-start = ((bf16[16,2,1,16,16,128]{5,4,3,2,1,0:T(8,128)(2,1)}), bf16[16,2,1,16,16,128]{5,4,3,2,1,0:T(8,128)(2,1)}, u32[]{:S(2)}, u32[]{:S(2)}) async-start(bf16[16,2,1,16,16,128]{5,4,3,2,1,0:T(8,128)(2,1)} %copy.114), calls=%async_computation | async-start | bytes 4194304 | tf_op jit(solution)/shard_map/all_to_all | solution.py:99
  59.0 1.4 copy-start.10
  68.1 1.6 copy-start.7
  71.7 16.0 %copy-start.5 = (bf16[256,16,128]{2,1,0:T(8,128)(2,1)S(1)}, bf16[256,16,128]{2,1,0:T(8,128)(2,1)}, u32[]{:S(2)}) copy-start(bf16[256,16,128]{2,1,0:T(8,128)(2,1)} %get-tuple-element.29) | copy-start | bytes 3145732
  81.4 34.0 %all-to-all-start.3 = ((bf16[16,1,2,16,16,128]{5,4,3,2,1,0:T(8,128)(2,1)}), bf16[16,1,2,16,16,128]{5,4,3,2,1,0:T(8,128)(2,1)}, u32[]{:S(2)}, u32[]{:S(2)}) async-start(bf16[16,1,2,16,16,128]{5,4,3,2,1,0:T(8,128)(2,1)} %copy.131), calls=%async_computation.3 | async-start | bytes 4194304 | tf_op jit(solution)/shard_map/all_to_all | solution.py:103
  99.4 1.6 copy-start.8
  115.3 75.7 %all-to-all-start.1 = ((bf16[16,1,2,16,16,128]{5,4,3,2,1,0:T(8,128)(2,1)}), bf16[16,1,2,16,16,128]{5,4,3,2,1,0:T(8,128)(2,1)}, u32[]{:S(2)}, u32[]{:S(2)}) async-start(bf16[16,1,2,16,16,128]{5,4,3,2,1,0:T(8,128)(2,1)} %copy.121), calls=%async_computation.1 | async-start | bytes 4194304 | tf_op jit(solution)/shard_map/all_to_all | solution.py:103
  129.8 25.2 %collective-permute-start.2 = (bf16[4,16,16,256]{3,2,1,0:T(8,128)(2,1)}, bf16[4,16,16,256]{3,2,1,0:T(8,128)(2,1)}, u32[]{:S(2)}, u32[]{:S(2)}) collective-permute-start(bf16[4,16,16,256]{3,2,1,0:T(8,128)(2,1)} %get-tuple-element.15), channel_id=1, source_target_pairs={{0,192},{16,208},{32,224},{48,240},{64,0},{80,16},{96,32},{112,48}... | collective-permute-start | bytes 1572872 | tf_op jit(solution)/shard_map/ppermute | solution.py:129
  132.5 22.5 %collective-permute-start.1 = (bf16[4,16,16,256]{3,2,1,0:T(8,128)(2,1)S(1)}, bf16[4,16,16,256]{3,2,1,0:T(8,128)(2,1)}, u32[]{:S(2)}, u32[]{:S(2)}) collective-permute-start(bf16[4,16,16,256]{3,2,1,0:T(8,128)(2,1)S(1)} %get-tuple-element.16), channel_id=1, source_target_pairs={{0,128},{16,144},{32,160},{48,176},{64,192},{80,208},{96,224},{112... | collective-permute-start | bytes 1572872 | tf_op jit(solution)/shard_map/ppermute | solution.py:129
  132.9 26.3 %collective-permute-start = (bf16[4,16,16,256]{3,2,1,0:T(8,128)(2,1)S(1)}, bf16[4,16,16,256]{3,2,1,0:T(8,128)(2,1)}, u32[]{:S(2)}, u32[]{:S(2)}) collective-permute-start(bf16[4,16,16,256]{3,2,1,0:T(8,128)(2,1)S(1)} %get-tuple-element.14), channel_id=1, source_target_pairs={{0,64},{16,80},{32,96},{48,112},{64,128},{80,144},{96,160},{112,17... | collective-permute-start | bytes 1572872 | tf_op jit(solution)/shard_map/ppermute | solution.py:129
  159.2 11.1 %copy-start.3 = (bf16[1,4096,256]{2,1,0:T(8,128)(2,1)S(1)}, bf16[1,4096,256]{2,1,0:T(8,128)(2,1)}, u32[]{:S(2)}) copy-start(bf16[1,4096,256]{2,1,0:T(8,128)(2,1)} %param.9) | copy-start | bytes 6291460
  161.9 20.7 %collective-permute-start.5 = (bf16[16,16,256]{2,1,0:T(8,128)(2,1)}, bf16[16,16,256]{2,1,0:T(8,128)(2,1)S(1)}, u32[]{:S(2)}, u32[]{:S(2)}) collective-permute-start(bf16[16,16,256]{2,1,0:T(8,128)(2,1)} %get-tuple-element.34), channel_id=1, source_target_pairs={{0,48},{16,0},{32,16},{48,32},{64,112},{80,64},{96,80},{112,96},{1... | collective-permute-start | bytes 393224 | tf_op jit(solution)/shard_map/ppermute | solution.py:139
  167.0 15.5 %collective-permute-start.4 = (bf16[16,16,256]{2,1,0:T(8,128)(2,1)}, bf16[16,16,256]{2,1,0:T(8,128)(2,1)S(1)}, u32[]{:S(2)}, u32[]{:S(2)}) collective-permute-start(bf16[16,16,256]{2,1,0:T(8,128)(2,1)} %get-tuple-element.35), channel_id=1, source_target_pairs={{0,32},{16,48},{32,0},{48,16},{64,96},{80,112},{96,64},{112,80},{1... | collective-permute-start | bytes 393224 | tf_op jit(solution)/shard_map/ppermute | solution.py:139
  168.2 14.4 %collective-permute-start.3 = (bf16[16,16,256]{2,1,0:T(8,128)(2,1)}, bf16[16,16,256]{2,1,0:T(8,128)(2,1)}, u32[]{:S(2)}, u32[]{:S(2)}) collective-permute-start(bf16[16,16,256]{2,1,0:T(8,128)(2,1)} %get-tuple-element.33), channel_id=1, source_target_pairs={{0,16},{16,32},{32,48},{48,0},{64,80},{80,96},{96,112},{112,64},{1... | collective-permute-start | bytes 393224 | tf_op jit(solution)/shard_map/ppermute | solution.py:139
  182.6 0.7 copy-start.20
  183.3 3.8 %copy-start.17 = (bf16[256,256]{0,1:T(8,128)(2,1)S(1)}, bf16[256,256]{0,1:T(8,128)(2,1)}, u32[]{:S(2)}) copy-start(bf16[256,256]{0,1:T(8,128)(2,1)} %copy-done.16) | copy-start | bytes 393220
  185.0 2.2 copy-start.14
  185.0 2.9 %copy-start.15 = (f32[1,16,256,128]{2,3,1,0:T(8,128)S(1)}, f32[1,16,256,128]{2,3,1,0:T(8,128)}, u32[]{:S(2)}) copy-start(f32[1,16,256,128]{2,3,1,0:T(8,128)} %copy.138) | copy-start | bytes 6291460
  191.1 2.2 copy-start.12
  191.1 2.9 %copy-start.13 = (f32[1,16,256,128]{2,3,1,0:T(8,128)S(1)}, f32[1,16,256,128]{2,3,1,0:T(8,128)}, u32[]{:S(2)}) copy-start(f32[1,16,256,128]{2,3,1,0:T(8,128)} %copy.136) | copy-start | bytes 6291460
  198.0 25.0 %all-to-all-start.4 = ((f32[256,1,256]{2,1,0:T(1,128)}), f32[256,1,256]{2,1,0:T(1,128)}, u32[]{:S(2)}, u32[]{:S(2)}) async-start(f32[256,1,256]{2,1,0:T(1,128)} %broadcast_in_dim.27), calls=%async_computation.4 | async-start | bytes 524288 | tf_op jit(solution)/shard_map/all_to_all | solution.py:142
  208.5 3.3 %copy-start.18 = (bf16[1,16,256,128]{2,3,1,0:T(8,128)(2,1)S(1)}, bf16[1,16,256,128]{2,3,1,0:T(8,128)(2,1)}, u32[]{:S(2)}) copy-start(bf16[1,16,256,128]{2,3,1,0:T(8,128)(2,1)} %get-tuple-element.11) | copy-start | bytes 3145732
  208.5 3.3 %copy-start.19 = (bf16[1,16,256,128]{2,3,1,0:T(8,128)(2,1)S(1)}, bf16[1,16,256,128]{2,3,1,0:T(8,128)(2,1)}, u32[]{:S(2)}) copy-start(bf16[1,16,256,128]{2,3,1,0:T(8,128)(2,1)} %get-tuple-element.10) | copy-start | bytes 3145732
  214.3 2.3 %copy-start.4 = (bf16[1,16,256,128]{2,3,1,0:T(8,128)(2,1)S(1)}, bf16[1,16,256,128]{2,3,1,0:T(8,128)(2,1)}, u32[]{:S(2)}) copy-start(bf16[1,16,256,128]{2,3,1,0:T(8,128)(2,1)} %fusion.5) | copy-start | bytes 3145732
  216.6 8.3 %copy-start.1 = (bf16[256,256]{1,0:T(8,128)(2,1)S(1)}, bf16[256,256]{1,0:T(8,128)(2,1)}, u32[]{:S(2)}) copy-start(bf16[256,256]{1,0:T(8,128)(2,1)} %param.13) | copy-start | bytes 393220

commit v7 on v5

--- a/solution.py
+++ b/solution.py
@@ -30,6 +30,14 @@
     grad_unmixed = jnp.einsum(
         "qJj,saqc->Jsajc", unmix_by_dest, grad_values, preferred_element_type=f32
     ).astype(bf16)
+    gate_weight = (
+        inputs.astype(f32) * upstream * gate_sig * (1.0 + gate_pre * (1.0 - gate_sig))
+    )
+    weight_hi = gate_weight.astype(bf16)
+    weight_lo = (gate_weight - weight_hi.astype(f32)).astype(bf16)
+    gain_weight = jnp.einsum(
+        "qJj,saqc->Jsajc", unmix_by_dest, weight_hi, preferred_element_type=f32
+    ) + jnp.einsum("qJj,saqc->Jsajc", unmix_by_dest, weight_lo, preferred_element_type=f32)
     outgoing = jnp.stack([first_mix, grad_unmixed], axis=1)
     incoming = lax.all_to_all(outgoing, "seq", split_axis=0, concat_axis=0, tiled=True)
     incoming = jnp.moveaxis(incoming, 2, 1)
@@ -104,7 +112,7 @@
         + grad_gate * gate_gain
     )
     grad_input = grad_input.astype(bf16).reshape(scenes_here, row_count, channels)
-    gain_term = jnp.sum(inputs.astype(f32) * grad_gate, axis=(0, 1, 2))
+    gain_term = jnp.sum(returned[:, :, 0].astype(f32) * gain_weight, axis=(0, 1, 2, 3))
     devices = lax.axis_size(("scene", "seq"))
     gain_spread = lax.all_to_all(
         jnp.broadcast_to(gain_term, (devices, channels)),

time: 189 us -> 198 us (1.048)
  waiting for transfers between devices: 36.9 us -> 46.5 us
  matrix products: 16.8 us -> 24.4 us
  starting transfers between devices: 42.5 us -> 35.5 us
    ppermute x3, waiting for transfers between devices: 0.01 us -> 21.4 us  [on_device(): kernel_grad = kernel_grad + lax.ppermute(piece, 'scene', pairs).astype(f32)]
    all_to_all x1, waiting for transfers between devices: 11.8 us -> 0.01 us  [on_device(): lax.all_to_all(back, 'seq', split_axis=0, concat_axis=0, tiled=True)]
    all_to_all x1, starting transfers between devices: 22.4 us -> 15.4 us  [on_device(): lax.all_to_all(jnp.broadcast_to(gain_term, (devices, channels)), ('scene'...]
    dot_general x0 -> x2, matrix products: none -> 3.88 us  [the longest x1 2.7 us: on_device(): jnp.einsum('qJj,saqc->Jsajc', unmix_by_dest, weight_hi, preferred_element...]
  transfers between devices with their start and end apart: 8 -> 8, of which waited for: 4 -> 5; matrix products, arithmetic and copies ran while one was open for 16% -> 13% of each run, Pallas kernels for 0% -> 0%
where the time goes in v7:
time: 198 us
  blocking collectives  55.9 us (28%)
  waiting for transfers between devices  46.5 us (23%)
  starting transfers between devices  35.5 us (18%)
  matrix products  24.4 us (12%)
  local copies, waits for them, and re-layouts  22.7 us (11%)
  other arithmetic  12.2 us (6%)
    all_to_all x1, blocking collectives, on_device(): lax.all_to_all(outgoing, 'seq', split_axis=0, concat_axis=0, tiled=True)  55.9 us
    ppermute x3, waiting for transfers between devices, on_device(): kernel_grad = kernel_grad + lax.ppermute(piece, 'scene', pairs).astype(f32)  21.4 us
    ppermute x3, waiting for transfers between devices, on_device(): partial = partial + lax.ppermute(piece, 'scene', pairs).astype(f32)  16.5 us
    all_to_all x1, starting transfers between devices, on_device(): lax.all_to_all(jnp.broadcast_to(gain_term, (devices, channels)), ('scene'...  15.4 us
    reshape x2, local copies, waits for them, and re-layouts, on_device(): kernel_term.reshape(outer, inner, block_len // scene_parts, chunk, channels)  9.87 us
    ppermute x3, starting transfers between devices, on_device(): kernel_grad = kernel_grad + lax.ppermute(piece, 'scene', pairs).astype(f32)  9.59 us
    all_to_all x1, waiting for transfers between devices, on_device(): lax.all_to_all(jnp.broadcast_to(gain_term, (devices, channels)), ('scene'...  8.56 us
    dot_general x1, matrix products, on_device(): jnp.einsum('Jjb,Jsajc->sabc', mix_by_dest, returned[:, :, 1], preferred_e...  6.87 us
  transfers between devices with their start and end apart: 8, of which 5 were waited for; matrix products, arithmetic and copies ran while one was open for 13% of the time, Pallas kernels for 0%

profile of v7, /device:TPU:1, one launch (start us, length us, event | category | flops | bytes accessed | tf_op | source)
XLA Modules:
  0.0 198.0 jit_solution(14037289813333572005)
XLA Ops:
  0.6 0.0 copy-start
  0.6 1.0 copy.61
  1.7 5.1 %subtract_convert_fusion = (bf16[1,4096,256]{2,1,0:T(8,128)(2,1)S(1)}, bf16[1,4096,256]{2,1,0:T(8,128)(2,1)S(1)}, bf16[1,4096,256]{2,1,0:T(8,128)(2,1)}) fusion(f32[256]{0:T(256)} %param.10, bf16[1,4096,256]{2,1,0:T(8,128)(2,1)} %param.9, bf16[1,4096,256]{2,1,0:T(8,128)(2,1)} %param.8), kind=kLoop, calls=%fused_computation.19 | loop fusion | flops 19922944 | bytes 10486784 | tf_op jit(solution)/shard_map/convert_element_type | solution.py:37
  6.8 0.7 convert_bitcast_fusion.1
  7.6 0.9 copy-done.5
  8.4 0.7 convert_bitcast_fusion.2
  9.2 0.4 pad_maximum_fusion
  9.6 0.5 copy.62
  10.1 55.9 %all_to_all.16 = bf16[16,2,1,16,16,256]{5,4,3,2,1,0:T(8,128)(2,1)S(1)} all-to-all(bf16[16,2,1,16,16,256]{5,4,3,2,1,0:T(8,128)(2,1)S(1)} %copy.62), channel_id=1, replica_groups=mesh['scene'=16,'seq'=16] {'seq'}, dimensions={0} | all-to-all | bytes 8388608 | tf_op jit(solution)/shard_map/all_to_all | solution.py:42
  66.1 0.3 copy.117
  66.3 0.0 copy-start.7
  66.3 0.4 fusion.48
  66.8 0.5 copy-done.7
  67.2 1.0 fusion.24
  68.3 3.2 %fusion.4 = (f32[1,256,16,256]{3,1,2,0:T(8,128)}, f32[16,256,256]{1,2,0:T(8,128)S(1)}) fusion(bf16[16,256,256]{1,2,0:T(8,128)(2,1)S(1)} %fusion.24, bf16[256,256]{1,0:T(8,128)(2,1)S(1)} %copy-done, bf16[256,16,256]{2,1,0:T(8,128)(2,1)S(1)} %bitcast.213), kind=kOutput, calls=%fused_computation.11 | convolution fusion | flops 538968064 | bytes 12713984 | tf_op jit(solution)/shard_map/pi,spjc->sijc/dot_general | solution.py:58
  71.5 1.2 fusion.27
  72.7 1.3 fusion.30
  74.0 1.2 copy.70
  75.2 1.2 copy.69
  76.4 2.4 %maximum_bitcast_fusion = bf16[16,1,2,16,16,256]{5,4,3,2,1,0:T(8,128)(2,1)} fusion(bf16[1,16,1,16,16,256]{5,4,3,2,1,0:T(8,128)(2,1)S(1)} %copy.70, bf16[1,16,1,16,16,256]{5,4,3,2,1,0:T(8,128)(2,1)S(1)} %copy.69), kind=kLoop, calls=%fused_computation.5 | loop fusion | flops 2097152 | bytes 8388608 | tf_op jit(solution)/shard_map/transpose | solution.py:100
  78.7 5.5 %all-to-all-start.1 = ((bf16[16,1,2,16,16,256]{5,4,3,2,1,0:T(8,128)(2,1)}), bf16[16,1,2,16,16,256]{5,4,3,2,1,0:T(8,128)(2,1)}, u32[]{:S(2)}, u32[]{:S(2)}) async-start(bf16[16,1,2,16,16,256]{5,4,3,2,1,0:T(8,128)(2,1)} %maximum_bitcast_fusion), calls=%async_computation.1 | async-start | bytes 8388608 | tf_op jit(solution)/shard_map/all_to_all | solution.py:101
  84.3 4.4 %copy.112 = bf16[4,4,16,16,256]{4,3,2,1,0:T(8,128)(2,1)S(1)} copy(f32[4,4,16,16,256]{4,2,1,0,3:T(8,128)} %bitcast.207) | data formatting | bytes 6291456 | tf_op jit(solution)/shard_map/reshape | solution.py:68
  88.7 1.2 dynamic-slice_bitcast_fusion.2
  89.9 1.3 collective-permute-start
  91.2 2.6 %collective-permute-start.1 = (bf16[4,16,16,256]{3,2,1,0:T(8,128)(2,1)}, bf16[4,16,16,256]{3,2,1,0:T(8,128)(2,1)}, u32[]{:S(2)}, u32[]{:S(2)}) collective-permute-start(bf16[4,16,16,256]{3,2,1,0:T(8,128)(2,1)} %get-tuple-element.17), channel_id=1, source_target_pairs={{0,128},{16,144},{32,160},{48,176},{64,192},{80,208},{96,224},{112... | collective-permute-start | bytes 1572872 | tf_op jit(solution)/shard_map/ppermute | solution.py:78
  93.8 1.1 collective-permute-start.2
  94.9 5.4 %copy.73 = f32[4,4,16,16,256]{4,3,2,1,0:T(8,128)S(1)} copy(f32[4,4,16,16,256]{4,2,1,0,3:T(8,128)} %bitcast.208) | data formatting | bytes 8388608 | tf_op jit(solution)/shard_map/reshape | solution.py:68
  100.3 0.0 copy-start.4
  100.3 4.1 %collective-permute-done = bf16[4,16,16,256]{3,2,1,0:T(8,128)(2,1)S(1)} collective-permute-done((bf16[4,16,16,256]{3,2,1,0:T(8,128)(2,1)}, bf16[4,16,16,256]{3,2,1,0:T(8,128)(2,1)S(1)}, u32[]{:S(2)}, u32[]{:S(2)}) %collective-permute-start) | collective-permute-done | bytes 524320 | tf_op jit(solution)/shard_map/ppermute | solution.py:78
  104.4 12.4 %collective-permute-done.1 = bf16[4,16,16,256]{3,2,1,0:T(8,128)(2,1)} collective-permute-done((bf16[4,16,16,256]{3,2,1,0:T(8,128)(2,1)}, bf16[4,16,16,256]{3,2,1,0:T(8,128)(2,1)}, u32[]{:S(2)}, u32[]{:S(2)}) %collective-permute-start.1) | collective-permute-done | bytes 524320 | tf_op jit(solution)/shard_map/ppermute | solution.py:78
  116.8 1.7 fusion.45
  118.5 0.8 dynamic-slice_bitcast_fusion.5
  119.3 3.0 %collective-permute-start.3 = (bf16[16,16,256]{2,1,0:T(8,128)(2,1)}, bf16[16,16,256]{2,1,0:T(8,128)(2,1)S(1)}, u32[]{:S(2)}, u32[]{:S(2)}) collective-permute-start(bf16[16,16,256]{2,1,0:T(8,128)(2,1)} %get-tuple-element.18), channel_id=1, source_target_pairs={{0,16},{16,32},{32,48},{48,0},{64,80},{80,96},{96,112},{112,64},{1... | collective-permute-start | bytes 393224 | tf_op jit(solution)/shard_map/ppermute | solution.py:88
  122.2 4.2 %collective-permute-start.4 = (bf16[16,16,256]{2,1,0:T(8,128)(2,1)}, bf16[16,16,256]{2,1,0:T(8,128)(2,1)}, u32[]{:S(2)}, u32[]{:S(2)}) collective-permute-start(bf16[16,16,256]{2,1,0:T(8,128)(2,1)} %get-tuple-element.20), channel_id=1, source_target_pairs={{0,32},{16,48},{32,0},{48,16},{64,96},{80,112},{96,64},{112,80},{1... | collective-permute-start | bytes 393224 | tf_op jit(solution)/shard_map/ppermute | solution.py:88
  126.4 2.4 %collective-permute-start.5 = (bf16[16,16,256]{2,1,0:T(8,128)(2,1)}, bf16[16,16,256]{2,1,0:T(8,128)(2,1)}, u32[]{:S(2)}, u32[]{:S(2)}) collective-permute-start(bf16[16,16,256]{2,1,0:T(8,128)(2,1)} %get-tuple-element.19), channel_id=1, source_target_pairs={{0,48},{16,0},{32,16},{48,32},{64,112},{80,64},{96,80},{112,96},{1... | collective-permute-start | bytes 393224 | tf_op jit(solution)/shard_map/ppermute | solution.py:88
  128.8 2.7 %fusion.49 = f32[16,256,16,16]{1,3,2,0:T(8,128)} fusion(bf16[16,256,256,1]{2,1,3,0:T(8,128)(2,1)S(1)} %bitcast.212, bf16[256,16,16,1]{0,2,1,3:T(8,128)(2,1)S(1)} %bitcast.220), kind=kOutput, calls=%fused_computation.68 | convolution fusion | flops 536870912 | bytes 6422528 | tf_op jit(solution)/shard_map/qJj,saqc->Jsajc/dot_general | solution.py:38
  131.5 17.7 %collective-permute-done.3 = bf16[16,16,256]{2,1,0:T(8,128)(2,1)S(1)} collective-permute-done((bf16[16,16,256]{2,1,0:T(8,128)(2,1)}, bf16[16,16,256]{2,1,0:T(8,128)(2,1)S(1)}, u32[]{:S(2)}, u32[]{:S(2)}) %collective-permute-start.3) | collective-permute-done | bytes 131104 | tf_op jit(solution)/shard_map/ppermute | solution.py:88
  149.2 3.8 %collective-permute-done.4 = bf16[16,16,256]{2,1,0:T(8,128)(2,1)} collective-permute-done((bf16[16,16,256]{2,1,0:T(8,128)(2,1)}, bf16[16,16,256]{2,1,0:T(8,128)(2,1)}, u32[]{:S(2)}, u32[]{:S(2)}) %collective-permute-start.4) | collective-permute-done | bytes 131104 | tf_op jit(solution)/shard_map/ppermute | solution.py:88
  153.0 1.7 fusion.39
  154.7 4.0 %fusion.47 = (bf16[16,1,1,16,16,256]{5,4,3,2,1,0:T(8,128)(2,1)}, bf16[16,1,1,16,16,256]{5,4,3,2,1,0:T(8,128)(2,1)S(1)}) fusion(bf16[16,1,2,16,16,256]{5,4,3,2,1,0:T(8,128)(2,1)} %all-to-all-done.1), kind=kLoop, calls=%fused_computation.66 | loop fusion | bytes 8388608 | tf_op jit(solution)/shard_map/slice | solution.py:111
  158.8 5.5 %fusion.5 = (bf16[1,16,256,256]{3,2,1,0:T(8,128)(2,1)}, f32[1,16,256,256]{3,2,1,0:T(8,128)}, f32[16,256,256,1]{1,2,3,0:T(8,128)}) fusion(f32[256]{0:T(256)S(1)} %copy-done.10, bf16[1,16,256,256]{3,2,1,0:T(8,128)(2,1)S(1)} %bitcast.215, bf16[256,16,16,1]{0,2,1,3:T(8,128)(2,1)S(1)} %bitcast.221, bf16[16,1,1,16,16,256]{5,4,3,2,1,0:T(8,128)(2,1)S(1)} %get-tuple-element.12), kind=kOutput, calls=%fused_computation.14 | convolution fusion | flops 545259520 | bytes 14812160 | tf_op jit(solution)/shard_map/qJj,Jsajc->saqc/dot_general | solution.py:102
  164.2 1.2 fusion.2
  165.4 0.9 broadcast_in_dim.14
  166.3 15.4 %all-to-all-start.2 = ((f32[256,1,256]{2,1,0:T(1,128)}), f32[256,1,256]{2,1,0:T(1,128)S(1)}, u32[]{:S(2)}, u32[]{:S(2)}) async-start(f32[256,1,256]{2,1,0:T(1,128)} %broadcast_in_dim.14), calls=%async_computation.2 | async-start | bytes 524288 | tf_op jit(solution)/shard_map/all_to_all | solution.py:117
  181.7 6.9 %fusion.3 = bf16[1,16,256,256]{3,2,1,0:T(8,128)(2,1)} fusion(f32[16,256,256,1]{1,2,3,0:T(8,128)} %get-tuple-element.21, f32[1,16,256,256]{3,2,1,0:T(8,128)} %get-tuple-element.7, bf16[16,16,256,1]{2,1,0,3:T(8,128)(2,1)S(1)} %bitcast.225, bf16[16,1,1,16,16,256]{5,4,3,2,1,0:T(8,128)(2,1)} %get-tuple-element.11, f32[256]{0:T(256)S(1)} %copy-done.10, ...), kind=kOutput, calls=%fused_computation.9 | convolution fusion | flops 551550976 | bytes 14812160 | tf_op jit(solution)/shard_map/Jjb,Jsajc->sabc/dot_general | solution.py:111
  188.6 8.6 %all-to-all-done.2 = f32[256,1,256]{2,1,0:T(1,128)S(1)} async-done(((f32[256,1,256]{2,1,0:T(1,128)}), f32[256,1,256]{2,1,0:T(1,128)S(1)}, u32[]{:S(2)}, u32[]{:S(2)}) %all-to-all-start.2) | async-done | bytes 262176 | tf_op jit(solution)/shard_map/all_to_all | solution.py:117
  197.2 0.3 reduce_sum.20
  197.4 0.6 broadcast_multiply_fusion
  (20 shorter events, 0.0 us)
Async XLA Ops:
  0.6 67.6 %copy-start = (bf16[256,256]{1,0:T(8,128)(2,1)S(1)}, bf16[256,256]{1,0:T(8,128)(2,1)}, u32[]{:S(2)}) copy-start(bf16[256,256]{1,0:T(8,128)(2,1)} %param.14) | copy-start | bytes 393220
  6.8 1.6 copy-start.5
  6.8 1.6 copy-start.9
  66.3 0.9 copy-start.7
  68.3 3.2 %copy-start.3 = (bf16[256,16,256]{2,1,0:T(8,128)(2,1)S(1)}, bf16[256,16,256]{2,1,0:T(8,128)(2,1)}, u32[]{:S(2)}) copy-start(bf16[256,16,256]{2,1,0:T(8,128)(2,1)} %param.11) | copy-start | bytes 6291460
  78.7 76.0 %all-to-all-start.1 = ((bf16[16,1,2,16,16,256]{5,4,3,2,1,0:T(8,128)(2,1)}), bf16[16,1,2,16,16,256]{5,4,3,2,1,0:T(8,128)(2,1)}, u32[]{:S(2)}, u32[]{:S(2)}) async-start(bf16[16,1,2,16,16,256]{5,4,3,2,1,0:T(8,128)(2,1)} %maximum_bitcast_fusion), calls=%async_computation.1 | async-start | bytes 8388608 | tf_op jit(solution)/shard_map/all_to_all | solution.py:101
  89.9 14.6 %collective-permute-start = (bf16[4,16,16,256]{3,2,1,0:T(8,128)(2,1)}, bf16[4,16,16,256]{3,2,1,0:T(8,128)(2,1)S(1)}, u32[]{:S(2)}, u32[]{:S(2)}) collective-permute-start(bf16[4,16,16,256]{3,2,1,0:T(8,128)(2,1)} %get-tuple-element.15), channel_id=1, source_target_pairs={{0,64},{16,80},{32,96},{48,112},{64,128},{80,144},{96,160},{112,17... | collective-permute-start | bytes 1572872 | tf_op jit(solution)/shard_map/ppermute | solution.py:78
  91.2 25.6 %collective-permute-start.1 = (bf16[4,16,16,256]{3,2,1,0:T(8,128)(2,1)}, bf16[4,16,16,256]{3,2,1,0:T(8,128)(2,1)}, u32[]{:S(2)}, u32[]{:S(2)}) collective-permute-start(bf16[4,16,16,256]{3,2,1,0:T(8,128)(2,1)} %get-tuple-element.17), channel_id=1, source_target_pairs={{0,128},{16,144},{32,160},{48,176},{64,192},{80,208},{96,224},{112... | collective-permute-start | bytes 1572872 | tf_op jit(solution)/shard_map/ppermute | solution.py:78
  93.8 23.0 %collective-permute-start.2 = (bf16[4,16,16,256]{3,2,1,0:T(8,128)(2,1)S(1)}, bf16[4,16,16,256]{3,2,1,0:T(8,128)(2,1)}, u32[]{:S(2)}, u32[]{:S(2)}) collective-permute-start(bf16[4,16,16,256]{3,2,1,0:T(8,128)(2,1)S(1)} %get-tuple-element.16), channel_id=1, source_target_pairs={{0,192},{16,208},{32,224},{48,240},{64,0},{80,16},{96,32},{112,48}... | collective-permute-start | bytes 1572872 | tf_op jit(solution)/shard_map/ppermute | solution.py:78
  100.3 28.5 %copy-start.4 = (bf16[1,4096,256]{2,1,0:T(8,128)(2,1)S(1)}, bf16[1,4096,256]{2,1,0:T(8,128)(2,1)}, u32[]{:S(2)}) copy-start(bf16[1,4096,256]{2,1,0:T(8,128)(2,1)} %get-tuple-element.10) | copy-start | bytes 6291460
  104.4 12.4 %copy-start.8 = (bf16[4,16,16,256]{3,2,1,0:T(8,128)(2,1)}, bf16[4,16,16,256]{3,2,1,0:T(8,128)(2,1)S(1)}, u32[]{:S(2)}) copy-start(bf16[4,16,16,256]{3,2,1,0:T(8,128)(2,1)S(1)} %collective-permute-done) | copy-start | bytes 1572868
  119.3 30.0 %collective-permute-start.3 = (bf16[16,16,256]{2,1,0:T(8,128)(2,1)}, bf16[16,16,256]{2,1,0:T(8,128)(2,1)S(1)}, u32[]{:S(2)}, u32[]{:S(2)}) collective-permute-start(bf16[16,16,256]{2,1,0:T(8,128)(2,1)} %get-tuple-element.18), channel_id=1, source_target_pairs={{0,16},{16,32},{32,48},{48,0},{64,80},{80,96},{96,112},{112,64},{1... | collective-permute-start | bytes 393224 | tf_op jit(solution)/shard_map/ppermute | solution.py:88
  122.2 30.8 %collective-permute-start.4 = (bf16[16,16,256]{2,1,0:T(8,128)(2,1)}, bf16[16,16,256]{2,1,0:T(8,128)(2,1)}, u32[]{:S(2)}, u32[]{:S(2)}) collective-permute-start(bf16[16,16,256]{2,1,0:T(8,128)(2,1)} %get-tuple-element.20), channel_id=1, source_target_pairs={{0,32},{16,48},{32,0},{48,16},{64,96},{80,112},{96,64},{112,80},{1... | collective-permute-start | bytes 393224 | tf_op jit(solution)/shard_map/ppermute | solution.py:88
  126.4 26.5 %collective-permute-start.5 = (bf16[16,16,256]{2,1,0:T(8,128)(2,1)}, bf16[16,16,256]{2,1,0:T(8,128)(2,1)}, u32[]{:S(2)}, u32[]{:S(2)}) collective-permute-start(bf16[16,16,256]{2,1,0:T(8,128)(2,1)} %get-tuple-element.19), channel_id=1, source_target_pairs={{0,48},{16,0},{32,16},{48,32},{64,112},{80,64},{96,80},{112,96},{1... | collective-permute-start | bytes 393224 | tf_op jit(solution)/shard_map/ppermute | solution.py:88
  154.7 4.0 %copy-start.10 = (f32[256]{0:T(256)S(1)}, f32[256]{0:T(256)}, u32[]{:S(2)}) copy-start(f32[256]{0:T(256)} %param.10) | copy-start | bytes 3076
  154.7 4.0 %copy-start.6 = (bf16[1,4096,256]{2,1,0:T(8,128)(2,1)S(1)}, bf16[1,4096,256]{2,1,0:T(8,128)(2,1)}, u32[]{:S(2)}) copy-start(bf16[1,4096,256]{2,1,0:T(8,128)(2,1)} %param.8) | copy-start | bytes 6291460
  158.8 5.5 %copy-start.2 = (f32[16,256,16,16]{1,3,2,0:T(8,128)S(1)}, f32[16,256,16,16]{1,3,2,0:T(8,128)}, u32[]{:S(2)}) copy-start(f32[16,256,16,16]{1,3,2,0:T(8,128)} %fusion.49) | copy-start | bytes 12582916
  166.3 30.9 %all-to-all-start.2 = ((f32[256,1,256]{2,1,0:T(1,128)}), f32[256,1,256]{2,1,0:T(1,128)S(1)}, u32[]{:S(2)}, u32[]{:S(2)}) async-start(f32[256,1,256]{2,1,0:T(1,128)} %broadcast_in_dim.14), calls=%async_computation.2 | async-start | bytes 524288 | tf_op jit(solution)/shard_map/all_to_all | solution.py:117
  181.7 16.3 %copy-start.1 = (bf16[256,256]{1,0:T(8,128)(2,1)S(1)}, bf16[256,256]{1,0:T(8,128)(2,1)}, u32[]{:S(2)}) copy-start(bf16[256,256]{1,0:T(8,128)(2,1)} %param.14) | copy-start | bytes 393220

commit v8 on v5

--- a/solution.py
+++ b/solution.py
@@ -40,15 +40,19 @@
         scenes_here, parts * local_a, chunk, channels
     )
 
+    flat = chunk * channels
+    spread_mix = spread_mix.reshape(scenes_here, block_len, flat)
+    spread_grad = spread_grad.reshape(scenes_here, block_len, flat)
+    kernel_f = kernel_f.reshape(block_len, flat)
     second_mix = jnp.einsum(
-        "ia,sajc->sijc", across_mix, spread_mix, preferred_element_type=f32
+        "ia,san->sin", across_mix, spread_mix, preferred_element_type=f32
     ).astype(bf16)
     weighted = (second_mix.astype(f32) * kernel_f).astype(bf16)
     unmixed = jnp.einsum(
-        "pi,sijc->spjc", across_unmix, weighted, preferred_element_type=f32
+        "pi,sin->spn", across_unmix, weighted, preferred_element_type=f32
     ).astype(bf16)
     grad_weighted = jnp.einsum(
-        "pi,spjc->sijc", across_unmix, spread_grad, preferred_element_type=f32
+        "pi,spn->sin", across_unmix, spread_grad, preferred_element_type=f32
     )
     kernel_term = jnp.sum(grad_weighted * second_mix.astype(f32), axis=0)
     scene_parts = lax.axis_size("scene")
@@ -80,7 +84,7 @@
         kernel_grad = kernel_grad + lax.ppermute(piece, "scene", pairs).astype(f32)
     grad_second = (grad_weighted * kernel_f).astype(bf16)
     grad_first = jnp.einsum(
-        "ia,sijc->sajc", across_mix, grad_second, preferred_element_type=f32
+        "ia,sin->san", across_mix, grad_second, preferred_element_type=f32
     ).astype(bf16)
     back = jnp.stack(
         [

time: 189 us -> 223 us (1.18)
  blocking collectives: 55.9 us -> 0 us
  waiting for transfers between devices: 36.9 us -> 86.5 us
  local copies, waits for them, and re-layouts: 24.1 us -> 51.3 us
  starting transfers between devices: 42.5 us -> 54.1 us
  matrix products: 16.8 us -> 19.4 us
    all_to_all x1 -> x0, blocking collectives: 55.9 us -> none  [on_device(): lax.all_to_all(outgoing, 'seq', split_axis=0, concat_axis=0, tiled=True)]
    all_to_all x0 -> x1, waiting for transfers between devices: none -> 48.7 us  [on_device(): lax.all_to_all(outgoing, 'seq', split_axis=0, concat_axis=0, tiled=True)]
    unnamed x21 -> x32, local copies, waits for them, and re-layouts: 3.74 us -> 18.2 us
    reshape x2 -> x0, local copies, waits for them, and re-layouts: 9.86 us -> none  [on_device(): kernel_term.reshape(outer, inner, block_len // scene_parts, chunk, channels)]
    convert_element_type x0 -> x2, local copies, waits for them, and re-layouts: none -> 8.16 us  [the longest x1 4.09 us: on_device(): unmixed = jnp.einsum('pi,sin->spn', across_unmix, weighted, preferred_ele...]
    all_to_all x0 -> x1, starting transfers between devices: none -> 7.47 us  [on_device(): lax.all_to_all(outgoing, 'seq', split_axis=0, concat_axis=0, tiled=True)]
    all_to_all x1, starting transfers between devices: 5.52 us -> 12 us  [on_device(): lax.all_to_all(back, 'seq', split_axis=0, concat_axis=0, tiled=True)]
    ppermute x3, waiting for transfers between devices: 16.5 us -> 22.3 us  [on_device(): partial = partial + lax.ppermute(piece, 'scene', pairs).astype(f32)]
  transfers between devices with their start and end apart: 8 -> 9, of which waited for: 4 -> 5; matrix products, arithmetic and copies ran while one was open for 16% -> 16% of each run, Pallas kernels for 0% -> 0%
where the time goes in v8:
time: 223 us; the launch traced here: 222 us
  waiting for transfers between devices  86.5 us (39%)
  starting transfers between devices  54.1 us (24%)
  local copies, waits for them, and re-layouts  51.3 us (23%)
  matrix products  19.4 us (9%)
  other arithmetic  9.9 us (4%)
    all_to_all x1, waiting for transfers between devices, on_device(): lax.all_to_all(outgoing, 'seq', split_axis=0, concat_axis=0, tiled=True)  48.7 us
    ppermute x3, waiting for transfers between devices, on_device(): partial = partial + lax.ppermute(piece, 'scene', pairs).astype(f32)  22.3 us
    all_to_all x1, starting transfers between devices, on_device(): lax.all_to_all(jnp.broadcast_to(gain_term, (devices, channels)), ('scene'...  18.7 us
    unnamed x32, local copies, waits for them, and re-layouts  18.2 us
    all_to_all x1, starting transfers between devices, on_device(): lax.all_to_all(back, 'seq', split_axis=0, concat_axis=0, tiled=True)  12 us
    ppermute x3, starting transfers between devices, on_device(): kernel_grad = kernel_grad + lax.ppermute(piece, 'scene', pairs).astype(f32)  9.59 us
    all_to_all x1, waiting for transfers between devices, on_device(): lax.all_to_all(jnp.broadcast_to(gain_term, (devices, channels)), ('scene'...  8.53 us
    all_to_all x1, starting transfers between devices, on_device(): lax.all_to_all(outgoing, 'seq', split_axis=0, concat_axis=0, tiled=True)  7.47 us
  transfers between devices with their start and end apart: 9, of which 5 were waited for; matrix products, arithmetic and copies ran while one was open for 16% of the time, Pallas kernels for 0%

profile of v8, /device:TPU:1, one launch (start us, length us, event | category | flops | bytes accessed | tf_op | source)
XLA Modules:
  0.0 222.0 jit_solution(4129847883463848720)
XLA Ops:
  0.6 1.0 copy.44
  1.7 3.5 %multiply_convert_fusion = bf16[1,4096,256]{2,1,0:T(8,128)(2,1)S(1)} fusion(f32[256]{0:T(256)} %param.10, bf16[1,4096,256]{2,1,0:T(8,128)(2,1)} %param.8, bf16[1,4096,256]{2,1,0:T(8,128)(2,1)} %param.9), kind=kLoop, calls=%fused_computation.24 | loop fusion | flops 9437184 | bytes 6292480 | tf_op jit(solution)/shard_map/convert_element_type | solution.py:24
  5.3 0.7 convert_bitcast_fusion
  6.0 0.8 copy-done.3
  6.8 0.7 convert_bitcast_fusion.1
  7.9 2.6 %copy.45 = bf16[16,2,1,16,16,256]{5,4,3,2,1,0:T(8,128)(2,1)} copy(bf16[16,2,1,16,16,256]{5,4,0,3,2,1:T(8,128)(2,1)S(1)} %pad_maximum_fusion) | data formatting | bytes 8388608 | tf_op jit(solution)/shard_map/stack | solution.py:33
  10.5 7.5 %all-to-all-start = ((bf16[16,2,1,16,16,256]{5,4,3,2,1,0:T(8,128)(2,1)}), bf16[16,2,1,16,16,256]{5,4,3,2,1,0:T(8,128)(2,1)}, u32[]{:S(2)}, u32[]{:S(2)}) async-start(bf16[16,2,1,16,16,256]{5,4,3,2,1,0:T(8,128)(2,1)} %copy.45), calls=%async_computation | async-start | bytes 8388608 | tf_op jit(solution)/shard_map/all_to_all | solution.py:34
  18.0 5.0 %copy.46 = f32[256,16,256]{0,2,1:T(8,128)} copy(bf16[256,16,256]{2,1,0:T(8,128)(2,1)} %param.11) | data formatting | bytes 6291456 | tf_op jit(solution)/shard_map/broadcast_in_dim;reshape | solution.py:50
  23.0 48.7 %all-to-all-done = bf16[16,2,1,16,16,256]{5,4,3,2,1,0:T(8,128)(2,1)} async-done(((bf16[16,2,1,16,16,256]{5,4,3,2,1,0:T(8,128)(2,1)}), bf16[16,2,1,16,16,256]{5,4,3,2,1,0:T(8,128)(2,1)}, u32[]{:S(2)}, u32[]{:S(2)}) %all-to-all-start) | async-done | bytes 4194336 | tf_op jit(solution)/shard_map/all_to_all | solution.py:34
  71.7 2.5 %fusion.22 = (bf16[16,1,1,16,16,256]{5,4,3,2,0,1:T(8,128)(2,1)S(1)}, bf16[16,1,1,16,16,256]{5,4,3,2,0,1:T(8,128)(2,1)S(1)}) fusion(bf16[16,1,2,16,16,256]{5,4,3,2,0,1:T(8,128)(2,1)} %bitcast.16), kind=kLoop, calls=%fused_computation.48 | loop fusion | bytes 8388608 | tf_op jit(solution)/shard_map/slice | solution.py:36
  74.1 1.0 copy.61
  75.1 1.0 copy.63
  76.1 0.8 fusion.2
  76.9 1.4 copy-done.5
  78.3 4.3 %fusion.20 = (f32[1,256,4096]{1,2,0:T(8,128)}, bf16[1,256,4096]{1,2,0:T(8,128)(2,1)S(1)}, bf16[1,256,4096]{1,2,0:T(8,128)(2,1)}) fusion(f32[1,256,4096]{1,2,0:T(8,128)S(1)} %fusion.2, f32[256,16,256]{0,2,1:T(8,128)S(1)} %copy-done.5, bf16[256,4096]{1,0:T(8,128)(2,1)S(1)} %bitcast.167, bf16[256,256]{1,0:T(8,128)(2,1)S(1)} %copy-done), kind=kOutput, calls=%fused_computation.46 | convolution fusion | flops 542113792 | bytes 19005440 | tf_op jit(solution)/shard_map/pi,spn->sin/dot_general | solution.py:54
  82.7 2.1 fusion.3
  84.7 4.1 %copy.47 = bf16[1,256,4096]{2,1,0:T(8,128)(2,1)} copy(bf16[1,256,4096]{1,2,0:T(8,128)(2,1)} %fusion.3) | data formatting | bytes 4194304 | tf_op jit(solution)/shard_map/convert_element_type | solution.py:53
  88.8 3.7 %copy.62 = bf16[32,8,16,256]{3,2,1,0:T(8,128)(2,1)} copy(bf16[32,8,16,256]{3,1,2,0:T(8,128)(2,1)} %bitcast.168) | data formatting | bytes 4194304
  92.5 2.0 fusion.4
  94.5 4.1 %copy.48 = bf16[1,256,4096]{2,1,0:T(8,128)(2,1)} copy(bf16[1,256,4096]{1,2,0:T(8,128)(2,1)} %fusion.4) | data formatting | bytes 4194304 | tf_op jit(solution)/shard_map/convert_element_type | solution.py:88
  98.6 2.4 %copy.64 = bf16[32,8,16,256]{3,2,1,0:T(8,128)(2,1)S(1)} copy(bf16[32,8,16,256]{3,1,2,0:T(8,128)(2,1)} %bitcast.169) | data formatting | bytes 4194304
  101.4 2.5 %copy.49 = bf16[16,1,2,16,16,256]{5,4,3,2,1,0:T(8,128)(2,1)} copy(bf16[16,1,2,16,16,256]{5,4,3,0,2,1:T(8,128)(2,1)S(1)} %maximum_bitcast_fusion) | data formatting | bytes 8388608 | tf_op jit(solution)/shard_map/transpose | solution.py:96
  103.9 12.0 %all-to-all-start.1 = ((bf16[16,1,2,16,16,256]{5,4,3,2,1,0:T(8,128)(2,1)}), bf16[16,1,2,16,16,256]{5,4,3,2,1,0:T(8,128)(2,1)}, u32[]{:S(2)}, u32[]{:S(2)}) async-start(bf16[16,1,2,16,16,256]{5,4,3,2,1,0:T(8,128)(2,1)} %copy.49), calls=%async_computation.1 | async-start | bytes 8388608 | tf_op jit(solution)/shard_map/all_to_all | solution.py:97
  115.9 5.7 %copy.52 = f32[1,256,4096]{2,1,0:T(8,128)} copy(f32[1,256,4096]{1,2,0:T(8,128)} %get-tuple-element.8) | data formatting | bytes 8388608 | tf_op jit(solution)/shard_map/mul | solution.py:57
  121.5 3.9 %copy.65 = f32[32,8,16,256]{3,2,1,0:T(8,128)S(1)} copy(f32[32,8,16,256]{3,1,2,0:T(8,128)} %bitcast.165) | data formatting | bytes 8388608
  125.8 1.7 copy-done.2
  127.4 1.1 dynamic-slice_bitcast_fusion.2
  128.6 2.6 %collective-permute-start = (bf16[4,16,16,256]{3,2,1,0:T(8,128)(2,1)}, bf16[4,16,16,256]{3,2,1,0:T(8,128)(2,1)S(1)}, u32[]{:S(2)}, u32[]{:S(2)}) collective-permute-start(bf16[4,16,16,256]{3,2,1,0:T(8,128)(2,1)} %get-tuple-element.15), channel_id=1, source_target_pairs={{0,64},{16,80},{32,96},{48,112},{64,128},{80,144},{96,160},{112,17... | collective-permute-start | bytes 1572872 | tf_op jit(solution)/shard_map/ppermute | solution.py:74
  131.2 2.6 %collective-permute-start.1 = (bf16[4,16,16,256]{3,2,1,0:T(8,128)(2,1)}, bf16[4,16,16,256]{3,2,1,0:T(8,128)(2,1)}, u32[]{:S(2)}, u32[]{:S(2)}) collective-permute-start(bf16[4,16,16,256]{3,2,1,0:T(8,128)(2,1)} %get-tuple-element.17), channel_id=1, source_target_pairs={{0,128},{16,144},{32,160},{48,176},{64,192},{80,208},{96,224},{112... | collective-permute-start | bytes 1572872 | tf_op jit(solution)/shard_map/ppermute | solution.py:74
  133.8 1.1 collective-permute-start.2
  134.9 10.1 %collective-permute-done = bf16[4,16,16,256]{3,2,1,0:T(8,128)(2,1)S(1)} collective-permute-done((bf16[4,16,16,256]{3,2,1,0:T(8,128)(2,1)}, bf16[4,16,16,256]{3,2,1,0:T(8,128)(2,1)S(1)}, u32[]{:S(2)}, u32[]{:S(2)}) %collective-permute-start) | collective-permute-done | bytes 524320 | tf_op jit(solution)/shard_map/ppermute | solution.py:74
  145.0 12.1 %collective-permute-done.1 = bf16[4,16,16,256]{3,2,1,0:T(8,128)(2,1)} collective-permute-done((bf16[4,16,16,256]{3,2,1,0:T(8,128)(2,1)}, bf16[4,16,16,256]{3,2,1,0:T(8,128)(2,1)}, u32[]{:S(2)}, u32[]{:S(2)}) %collective-permute-start.1) | collective-permute-done | bytes 524320 | tf_op jit(solution)/shard_map/ppermute | solution.py:74
  157.1 2.0 fusion.18
  159.2 0.8 dynamic-slice_bitcast_fusion.5
  159.9 3.0 %collective-permute-start.3 = (bf16[16,16,256]{2,1,0:T(8,128)(2,1)}, bf16[16,16,256]{2,1,0:T(8,128)(2,1)S(1)}, u32[]{:S(2)}, u32[]{:S(2)}) collective-permute-start(bf16[16,16,256]{2,1,0:T(8,128)(2,1)} %get-tuple-element.18), channel_id=1, source_target_pairs={{0,16},{16,32},{32,48},{48,0},{64,80},{80,96},{96,112},{112,64},{1... | collective-permute-start | bytes 393224 | tf_op jit(solution)/shard_map/ppermute | solution.py:84
  162.9 4.2 %collective-permute-start.4 = (bf16[16,16,256]{2,1,0:T(8,128)(2,1)}, bf16[16,16,256]{2,1,0:T(8,128)(2,1)}, u32[]{:S(2)}, u32[]{:S(2)}) collective-permute-start(bf16[16,16,256]{2,1,0:T(8,128)(2,1)} %get-tuple-element.20), channel_id=1, source_target_pairs={{0,32},{16,48},{32,0},{48,16},{64,96},{80,112},{96,64},{112,80},{1... | collective-permute-start | bytes 393224 | tf_op jit(solution)/shard_map/ppermute | solution.py:84
  167.1 2.4 %collective-permute-start.5 = (bf16[16,16,256]{2,1,0:T(8,128)(2,1)}, bf16[16,16,256]{2,1,0:T(8,128)(2,1)}, u32[]{:S(2)}, u32[]{:S(2)}) collective-permute-start(bf16[16,16,256]{2,1,0:T(8,128)(2,1)} %get-tuple-element.19), channel_id=1, source_target_pairs={{0,48},{16,0},{32,16},{48,32},{64,112},{80,64},{96,80},{112,96},{1... | collective-permute-start | bytes 393224 | tf_op jit(solution)/shard_map/ppermute | solution.py:84
  169.5 7.0 %all-to-all-done.1 = bf16[16,1,2,16,16,256]{5,4,3,2,1,0:T(8,128)(2,1)} async-done(((bf16[16,1,2,16,16,256]{5,4,3,2,1,0:T(8,128)(2,1)}), bf16[16,1,2,16,16,256]{5,4,3,2,1,0:T(8,128)(2,1)}, u32[]{:S(2)}, u32[]{:S(2)}) %all-to-all-start.1) | async-done | bytes 4194336 | tf_op jit(solution)/shard_map/all_to_all | solution.py:97
  176.5 4.1 %fusion.21 = (bf16[16,1,1,16,16,256]{5,4,3,2,1,0:T(8,128)(2,1)}, bf16[16,1,1,16,16,256]{5,4,3,2,1,0:T(8,128)(2,1)S(1)}) fusion(bf16[16,1,2,16,16,256]{5,4,3,2,1,0:T(8,128)(2,1)} %all-to-all-done.1), kind=kLoop, calls=%fused_computation.47 | loop fusion | bytes 8388608 | tf_op jit(solution)/shard_map/slice | solution.py:107
  180.6 3.6 %fusion.8 = (f32[1,16,256,256]{3,2,1,0:T(8,128)S(1)}, bf16[1,16,256,256]{3,2,1,0:T(8,128)(2,1)}) fusion(f32[256]{0:T(256)S(1)} %copy-done.12, bf16[1,4096,256]{2,1,0:T(8,128)(2,1)S(1)} %copy-done.3, bf16[256,16,16,1]{0,2,1,3:T(8,128)(2,1)S(1)} %bitcast.180, bf16[16,1,1,16,16,256]{5,4,3,2,1,0:T(8,128)(2,1)S(1)} %get-tuple-element.12, ...), kind=kOutput, calls=%fused_computation.17 | convolution fusion | flops 552599552 | bytes 12715008 | tf_op jit(solution)/shard_map/qJj,Jsajc->saqc/dot_general | solution.py:98
  184.2 0.7 multiply_reduce_fusion
  184.9 1.2 copy-done.4
  186.2 0.8 broadcast_in_dim.2
  187.0 18.7 %all-to-all-start.2 = ((f32[256,1,256]{2,1,0:T(1,128)}), f32[256,1,256]{2,1,0:T(1,128)S(1)}, u32[]{:S(2)}, u32[]{:S(2)}) async-start(f32[256,1,256]{2,1,0:T(1,128)} %broadcast_in_dim.2), calls=%async_computation.2 | async-start | bytes 524288 | tf_op jit(solution)/shard_map/all_to_all | solution.py:113
  205.8 1.7 fusion.17
  207.5 5.1 %fusion.5 = bf16[1,16,256,256]{3,2,1,0:T(8,128)(2,1)} fusion(f32[1,16,256,256]{3,2,1,0:T(8,128)} %copy-done.4, bf16[16,16,256,1]{2,1,0,3:T(8,128)(2,1)S(1)} %bitcast.178, bf16[16,1,1,16,16,256]{5,4,3,2,1,0:T(8,128)(2,1)} %get-tuple-element.11, f32[256]{0:T(256)S(1)} %copy-done.12), kind=kOutput, calls=%fused_computation.12 | convolution fusion | flops 540016640 | bytes 8520704 | tf_op jit(solution)/shard_map/Jjb,Jsajc->sabc/dot_general | solution.py:107
  212.6 8.5 %all-to-all-done.2 = f32[256,1,256]{2,1,0:T(1,128)S(1)} async-done(((f32[256,1,256]{2,1,0:T(1,128)}), f32[256,1,256]{2,1,0:T(1,128)S(1)}, u32[]{:S(2)}, u32[]{:S(2)}) %all-to-all-start.2) | async-done | bytes 262176 | tf_op jit(solution)/shard_map/all_to_all | solution.py:113
  221.4 0.6 broadcast_multiply_fusion
  (30 shorter events, 1.4 us)
Async XLA Ops:
  0.6 76.3 %copy-start = (bf16[256,256]{1,0:T(8,128)(2,1)S(1)}, bf16[256,256]{1,0:T(8,128)(2,1)}, u32[]{:S(2)}) copy-start(bf16[256,256]{1,0:T(8,128)(2,1)} %param.14) | copy-start | bytes 393220
  5.2 1.6 copy-start.3
  5.2 1.6 copy-start.10
  10.5 61.1 %all-to-all-start = ((bf16[16,2,1,16,16,256]{5,4,3,2,1,0:T(8,128)(2,1)}), bf16[16,2,1,16,16,256]{5,4,3,2,1,0:T(8,128)(2,1)}, u32[]{:S(2)}, u32[]{:S(2)}) async-start(bf16[16,2,1,16,16,256]{5,4,3,2,1,0:T(8,128)(2,1)} %copy.45), calls=%async_computation | async-start | bytes 8388608 | tf_op jit(solution)/shard_map/all_to_all | solution.py:34
  75.1 1.0 copy-start.9
  76.1 2.2 copy-start.5
  88.8 3.7 %copy-start.6 = (bf16[1,256,4096]{1,2,0:T(8,128)(2,1)S(1)}, bf16[1,256,4096]{1,2,0:T(8,128)(2,1)}, u32[]{:S(2)}) copy-start(bf16[1,256,4096]{1,2,0:T(8,128)(2,1)} %get-tuple-element.10) | copy-start | bytes 6291460
  98.6 2.4 %copy-start.7 = (bf16[32,8,16,256]{3,2,1,0:T(8,128)(2,1)S(1)}, bf16[32,8,16,256]{3,2,1,0:T(8,128)(2,1)}, u32[]{:S(2)}) copy-start(bf16[32,8,16,256]{3,2,1,0:T(8,128)(2,1)} %copy.62) | copy-start | bytes 6291460
  103.9 72.6 %all-to-all-start.1 = ((bf16[16,1,2,16,16,256]{5,4,3,2,1,0:T(8,128)(2,1)}), bf16[16,1,2,16,16,256]{5,4,3,2,1,0:T(8,128)(2,1)}, u32[]{:S(2)}, u32[]{:S(2)}) async-start(bf16[16,1,2,16,16,256]{5,4,3,2,1,0:T(8,128)(2,1)} %copy.49), calls=%async_computation.1 | async-start | bytes 8388608 | tf_op jit(solution)/shard_map/all_to_all | solution.py:97
  125.5 2.0 copy-start.2
  128.6 16.4 %collective-permute-start = (bf16[4,16,16,256]{3,2,1,0:T(8,128)(2,1)}, bf16[4,16,16,256]{3,2,1,0:T(8,128)(2,1)S(1)}, u32[]{:S(2)}, u32[]{:S(2)}) collective-permute-start(bf16[4,16,16,256]{3,2,1,0:T(8,128)(2,1)} %get-tuple-element.15), channel_id=1, source_target_pairs={{0,64},{16,80},{32,96},{48,112},{64,128},{80,144},{96,160},{112,17... | collective-permute-start | bytes 1572872 | tf_op jit(solution)/shard_map/ppermute | solution.py:74
  131.2 26.0 %collective-permute-start.1 = (bf16[4,16,16,256]{3,2,1,0:T(8,128)(2,1)}, bf16[4,16,16,256]{3,2,1,0:T(8,128)(2,1)}, u32[]{:S(2)}, u32[]{:S(2)}) collective-permute-start(bf16[4,16,16,256]{3,2,1,0:T(8,128)(2,1)} %get-tuple-element.17), channel_id=1, source_target_pairs={{0,128},{16,144},{32,160},{48,176},{64,192},{80,208},{96,224},{112... | collective-permute-start | bytes 1572872 | tf_op jit(solution)/shard_map/ppermute | solution.py:74
  133.8 23.3 %collective-permute-start.2 = (bf16[4,16,16,256]{3,2,1,0:T(8,128)(2,1)S(1)}, bf16[4,16,16,256]{3,2,1,0:T(8,128)(2,1)}, u32[]{:S(2)}, u32[]{:S(2)}) collective-permute-start(bf16[4,16,16,256]{3,2,1,0:T(8,128)(2,1)S(1)} %get-tuple-element.16), channel_id=1, source_target_pairs={{0,192},{16,208},{32,224},{48,240},{64,0},{80,16},{96,32},{112,48}... | collective-permute-start | bytes 1572872 | tf_op jit(solution)/shard_map/ppermute | solution.py:74
  145.0 12.1 %copy-start.11 = (bf16[4,16,16,256]{3,2,1,0:T(8,128)(2,1)}, bf16[4,16,16,256]{3,2,1,0:T(8,128)(2,1)S(1)}, u32[]{:S(2)}) copy-start(bf16[4,16,16,256]{3,2,1,0:T(8,128)(2,1)S(1)} %collective-permute-done) | copy-start | bytes 1572868
  159.9 45.8 %collective-permute-start.3 = (bf16[16,16,256]{2,1,0:T(8,128)(2,1)}, bf16[16,16,256]{2,1,0:T(8,128)(2,1)S(1)}, u32[]{:S(2)}, u32[]{:S(2)}) collective-permute-start(bf16[16,16,256]{2,1,0:T(8,128)(2,1)} %get-tuple-element.18), channel_id=1, source_target_pairs={{0,16},{16,32},{32,48},{48,0},{64,80},{80,96},{96,112},{112,64},{1... | collective-permute-start | bytes 393224 | tf_op jit(solution)/shard_map/ppermute | solution.py:84
  162.9 42.8 %collective-permute-start.4 = (bf16[16,16,256]{2,1,0:T(8,128)(2,1)}, bf16[16,16,256]{2,1,0:T(8,128)(2,1)}, u32[]{:S(2)}, u32[]{:S(2)}) collective-permute-start(bf16[16,16,256]{2,1,0:T(8,128)(2,1)} %get-tuple-element.20), channel_id=1, source_target_pairs={{0,32},{16,48},{32,0},{48,16},{64,96},{80,112},{96,64},{112,80},{1... | collective-permute-start | bytes 393224 | tf_op jit(solution)/shard_map/ppermute | solution.py:84
  167.1 13.5 %copy-start.12 = (f32[256]{0:T(256)S(1)}, f32[256]{0:T(256)}, u32[]{:S(2)}) copy-start(f32[256]{0:T(256)} %param.10) | copy-start | bytes 3076
  167.1 38.6 %collective-permute-start.5 = (bf16[16,16,256]{2,1,0:T(8,128)(2,1)}, bf16[16,16,256]{2,1,0:T(8,128)(2,1)}, u32[]{:S(2)}, u32[]{:S(2)}) collective-permute-start(bf16[16,16,256]{2,1,0:T(8,128)(2,1)} %get-tuple-element.19), channel_id=1, source_target_pairs={{0,48},{16,0},{32,16},{48,32},{64,112},{80,64},{96,80},{112,96},{1... | collective-permute-start | bytes 393224 | tf_op jit(solution)/shard_map/ppermute | solution.py:84
  176.5 4.1 %copy-start.8 = (bf16[1,4096,256]{2,1,0:T(8,128)(2,1)S(1)}, bf16[1,4096,256]{2,1,0:T(8,128)(2,1)}, u32[]{:S(2)}) copy-start(bf16[1,4096,256]{2,1,0:T(8,128)(2,1)} %param.9) | copy-start | bytes 6291460
  184.2 1.9 copy-start.4
  187.0 34.2 %all-to-all-start.2 = ((f32[256,1,256]{2,1,0:T(1,128)}), f32[256,1,256]{2,1,0:T(1,128)S(1)}, u32[]{:S(2)}, u32[]{:S(2)}) async-start(f32[256,1,256]{2,1,0:T(1,128)} %broadcast_in_dim.2), calls=%async_computation.2 | async-start | bytes 524288 | tf_op jit(solution)/shard_map/all_to_all | solution.py:113
  207.5 14.5 %copy-start.1 = (bf16[256,256]{1,0:T(8,128)(2,1)S(1)}, bf16[256,256]{1,0:T(8,128)(2,1)}, u32[]{:S(2)}) copy-start(bf16[256,256]{1,0:T(8,128)(2,1)} %param.14) | copy-start | bytes 393220

commit v9 on v7

--- a/solution.py
+++ b/solution.py
@@ -99,6 +99,7 @@
     )
     back = jnp.moveaxis(back, 1, 0)
     returned = lax.all_to_all(back, "seq", split_axis=0, concat_axis=0, tiled=True)
+    returned, kernel_grad = lax.optimization_barrier((returned, kernel_grad))
     values = jnp.einsum(
         "qJj,Jsajc->saqc",
         unmix_by_dest,

time: 198 us -> 192 us (0.970)
  local copies, waits for them, and re-layouts: 22.7 us -> 18.9 us
  waiting for transfers between devices: 46.5 us -> 42.8 us
    slice x1 -> x0, local copies, waits for them, and re-layouts: 4.03 us -> none  [on_device(): returned[:, :, 1]]
    all_to_all x1, waiting for transfers between devices: 8.56 us -> 4.85 us  [on_device(): lax.all_to_all(jnp.broadcast_to(gain_term, (devices, channels)), ('scene'...]
    dot_general x1, matrix products: 1.18 us -> 3.88 us  [on_device(): jnp.einsum('qJj,saqc->Jsajc', unmix_by_dest, weight_lo, preferred_element...]
  transfers between devices with their start and end apart: 8 -> 8, of which waited for: 5 -> 5; matrix products, arithmetic and copies ran while one was open for 13% -> 15% of each run, Pallas kernels for 0% -> 0%
where the time goes in v9:
time: 192 us; the launch traced here: 191 us
  blocking collectives  55.9 us (29%)
  waiting for transfers between devices  42.8 us (22%)
  starting transfers between devices  35.5 us (18%)
  matrix products  25.3 us (13%)
  local copies, waits for them, and re-layouts  18.9 us (10%)
  other arithmetic  12.1 us (6%)
    all_to_all x1, blocking collectives, on_device(): lax.all_to_all(outgoing, 'seq', split_axis=0, concat_axis=0, tiled=True)  55.9 us
    ppermute x3, waiting for transfers between devices, on_device(): kernel_grad = kernel_grad + lax.ppermute(piece, 'scene', pairs).astype(f32)  21.5 us
    ppermute x3, waiting for transfers between devices, on_device(): partial = partial + lax.ppermute(piece, 'scene', pairs).astype(f32)  16.5 us
    all_to_all x1, starting transfers between devices, on_device(): lax.all_to_all(jnp.broadcast_to(gain_term, (devices, channels)), ('scene'...  15.4 us
    reshape x2, local copies, waits for them, and re-layouts, on_device(): kernel_term.reshape(outer, inner, block_len // scene_parts, chunk, channels)  9.86 us
    ppermute x3, starting transfers between devices, on_device(): kernel_grad = kernel_grad + lax.ppermute(piece, 'scene', pairs).astype(f32)  9.55 us
    all_to_all x1, starting transfers between devices, on_device(): lax.all_to_all(back, 'seq', split_axis=0, concat_axis=0, tiled=True)  5.52 us
    dot_general x1, matrix products, on_device(): jnp.einsum('Jjb,Jsajc->sabc', mix_by_dest, returned[:, :, 1], preferred_e...  5.29 us
  transfers between devices with their start and end apart: 8, of which 5 were waited for; matrix products, arithmetic and copies ran while one was open for 15% of the time, Pallas kernels for 0%

profile of v9, /device:TPU:1, one launch (start us, length us, event | category | flops | bytes accessed | tf_op | source)
XLA Modules:
  0.0 191.3 jit_solution(16061623677585677335)
XLA Ops:
  0.6 0.0 copy-start
  0.6 1.0 copy.61
  1.7 5.1 %subtract_convert_fusion = (bf16[1,4096,256]{2,1,0:T(8,128)(2,1)S(1)}, bf16[1,4096,256]{2,1,0:T(8,128)(2,1)S(1)}, bf16[1,4096,256]{2,1,0:T(8,128)(2,1)}) fusion(f32[256]{0:T(256)} %param.10, bf16[1,4096,256]{2,1,0:T(8,128)(2,1)} %param.9, bf16[1,4096,256]{2,1,0:T(8,128)(2,1)} %param.8), kind=kLoop, calls=%fused_computation.19 | loop fusion | flops 19922944 | bytes 10486784 | tf_op jit(solution)/shard_map/convert_element_type | solution.py:37
  6.8 0.7 convert_bitcast_fusion.1
  7.6 0.9 copy-done.4
  8.4 0.7 convert_bitcast_fusion.2
  9.2 0.4 pad_maximum_fusion
  9.6 0.5 copy.62
  10.1 55.9 %all_to_all.16 = bf16[16,2,1,16,16,256]{5,4,3,2,1,0:T(8,128)(2,1)S(1)} all-to-all(bf16[16,2,1,16,16,256]{5,4,3,2,1,0:T(8,128)(2,1)S(1)} %copy.62), channel_id=1, replica_groups=mesh['scene'=16,'seq'=16] {'seq'}, dimensions={0} | all-to-all | bytes 8388608 | tf_op jit(solution)/shard_map/all_to_all | solution.py:42
  66.1 0.4 copy.114
  66.5 0.0 copy-start.6
  66.5 0.3 fusion.47
  66.8 0.6 copy-done.6
  67.4 1.0 fusion.24
  68.4 0.0 copy-start.2
  68.5 3.2 %fusion.8 = (f32[1,256,16,256]{3,1,2,0:T(8,128)}, f32[16,256,256]{1,2,0:T(8,128)S(1)}) fusion(bf16[16,256,256]{1,2,0:T(8,128)(2,1)S(1)} %fusion.24, bf16[256,256]{1,0:T(8,128)(2,1)S(1)} %copy-done, bf16[256,16,256]{2,1,0:T(8,128)(2,1)S(1)} %bitcast.213), kind=kOutput, calls=%fused_computation.17 | convolution fusion | flops 538968064 | bytes 12713984 | tf_op jit(solution)/shard_map/pi,spjc->sijc/dot_general | solution.py:58
  71.6 1.2 fusion.27
  72.9 1.3 fusion.30
  74.2 1.2 copy.70
  75.3 1.2 copy.69
  76.5 2.4 %maximum_bitcast_fusion = bf16[16,1,2,16,16,256]{5,4,3,2,1,0:T(8,128)(2,1)} fusion(bf16[1,16,1,16,16,256]{5,4,3,2,1,0:T(8,128)(2,1)S(1)} %copy.70, bf16[1,16,1,16,16,256]{5,4,3,2,1,0:T(8,128)(2,1)S(1)} %copy.69), kind=kLoop, calls=%fused_computation.5 | loop fusion | flops 2097152 | bytes 8388608 | tf_op jit(solution)/shard_map/transpose | solution.py:100
  78.9 5.5 %all-to-all-start.1 = ((bf16[16,1,2,16,16,256]{5,4,3,2,1,0:T(8,128)(2,1)}), bf16[16,1,2,16,16,256]{5,4,3,2,1,0:T(8,128)(2,1)}, u32[]{:S(2)}, u32[]{:S(2)}) async-start(bf16[16,1,2,16,16,256]{5,4,3,2,1,0:T(8,128)(2,1)} %maximum_bitcast_fusion), calls=%async_computation.1 | async-start | bytes 8388608 | tf_op jit(solution)/shard_map/all_to_all | solution.py:101
  84.4 4.4 %copy.103 = bf16[4,4,16,16,256]{4,3,2,1,0:T(8,128)(2,1)S(1)} copy(f32[4,4,16,16,256]{4,2,1,0,3:T(8,128)} %bitcast.207) | data formatting | bytes 6291456 | tf_op jit(solution)/shard_map/reshape | solution.py:68
  88.8 1.2 dynamic-slice_bitcast_fusion.2
  90.0 1.3 collective-permute-start
  91.3 2.6 %collective-permute-start.1 = (bf16[4,16,16,256]{3,2,1,0:T(8,128)(2,1)}, bf16[4,16,16,256]{3,2,1,0:T(8,128)(2,1)}, u32[]{:S(2)}, u32[]{:S(2)}) collective-permute-start(bf16[4,16,16,256]{3,2,1,0:T(8,128)(2,1)} %get-tuple-element.19), channel_id=1, source_target_pairs={{0,128},{16,144},{32,160},{48,176},{64,192},{80,208},{96,224},{112... | collective-permute-start | bytes 1572872 | tf_op jit(solution)/shard_map/ppermute | solution.py:78
  94.0 1.1 collective-permute-start.2
  95.0 5.4 %copy.71 = f32[4,4,16,16,256]{4,3,2,1,0:T(8,128)S(1)} copy(f32[4,4,16,16,256]{4,2,1,0,3:T(8,128)} %bitcast.208) | data formatting | bytes 8388608 | tf_op jit(solution)/shard_map/reshape | solution.py:68
  100.5 0.0 copy-start.3
  100.5 4.2 %collective-permute-done = bf16[4,16,16,256]{3,2,1,0:T(8,128)(2,1)S(1)} collective-permute-done((bf16[4,16,16,256]{3,2,1,0:T(8,128)(2,1)}, bf16[4,16,16,256]{3,2,1,0:T(8,128)(2,1)S(1)}, u32[]{:S(2)}, u32[]{:S(2)}) %collective-permute-start) | collective-permute-done | bytes 524320 | tf_op jit(solution)/shard_map/ppermute | solution.py:78
  104.6 12.3 %collective-permute-done.1 = bf16[4,16,16,256]{3,2,1,0:T(8,128)(2,1)} collective-permute-done((bf16[4,16,16,256]{3,2,1,0:T(8,128)(2,1)}, bf16[4,16,16,256]{3,2,1,0:T(8,128)(2,1)}, u32[]{:S(2)}, u32[]{:S(2)}) %collective-permute-start.1) | collective-permute-done | bytes 524320 | tf_op jit(solution)/shard_map/ppermute | solution.py:78
  117.0 1.7 fusion.45
  118.7 0.8 dynamic-slice_bitcast_fusion.5
  119.4 3.0 %collective-permute-start.3 = (bf16[16,16,256]{2,1,0:T(8,128)(2,1)}, bf16[16,16,256]{2,1,0:T(8,128)(2,1)S(1)}, u32[]{:S(2)}, u32[]{:S(2)}) collective-permute-start(bf16[16,16,256]{2,1,0:T(8,128)(2,1)} %get-tuple-element.20), channel_id=1, source_target_pairs={{0,16},{16,32},{32,48},{48,0},{64,80},{80,96},{96,112},{112,64},{1... | collective-permute-start | bytes 393224 | tf_op jit(solution)/shard_map/ppermute | solution.py:88
  122.4 4.2 %collective-permute-start.4 = (bf16[16,16,256]{2,1,0:T(8,128)(2,1)}, bf16[16,16,256]{2,1,0:T(8,128)(2,1)}, u32[]{:S(2)}, u32[]{:S(2)}) collective-permute-start(bf16[16,16,256]{2,1,0:T(8,128)(2,1)} %get-tuple-element.22), channel_id=1, source_target_pairs={{0,32},{16,48},{32,0},{48,16},{64,96},{80,112},{96,64},{112,80},{1... | collective-permute-start | bytes 393224 | tf_op jit(solution)/shard_map/ppermute | solution.py:88
  126.6 2.4 %collective-permute-start.5 = (bf16[16,16,256]{2,1,0:T(8,128)(2,1)}, bf16[16,16,256]{2,1,0:T(8,128)(2,1)}, u32[]{:S(2)}, u32[]{:S(2)}) collective-permute-start(bf16[16,16,256]{2,1,0:T(8,128)(2,1)} %get-tuple-element.21), channel_id=1, source_target_pairs={{0,48},{16,0},{32,16},{48,32},{64,112},{80,64},{96,80},{112,96},{1... | collective-permute-start | bytes 393224 | tf_op jit(solution)/shard_map/ppermute | solution.py:88
  129.0 2.7 %fusion.48 = f32[16,256,16,16]{1,3,2,0:T(8,128)} fusion(bf16[16,256,256,1]{2,1,3,0:T(8,128)(2,1)S(1)} %bitcast.212, bf16[256,16,16,1]{0,2,1,3:T(8,128)(2,1)S(1)} %bitcast.220), kind=kOutput, calls=%fused_computation.67 | convolution fusion | flops 536870912 | bytes 6422528 | tf_op jit(solution)/shard_map/qJj,saqc->Jsajc/dot_general | solution.py:38
  131.7 17.7 %collective-permute-done.3 = bf16[16,16,256]{2,1,0:T(8,128)(2,1)S(1)} collective-permute-done((bf16[16,16,256]{2,1,0:T(8,128)(2,1)}, bf16[16,16,256]{2,1,0:T(8,128)(2,1)S(1)}, u32[]{:S(2)}, u32[]{:S(2)}) %collective-permute-start.3) | collective-permute-done | bytes 131104 | tf_op jit(solution)/shard_map/ppermute | solution.py:88
  149.4 3.8 %collective-permute-done.4 = bf16[16,16,256]{2,1,0:T(8,128)(2,1)} collective-permute-done((bf16[16,16,256]{2,1,0:T(8,128)(2,1)}, bf16[16,16,256]{2,1,0:T(8,128)(2,1)}, u32[]{:S(2)}, u32[]{:S(2)}) %collective-permute-start.4) | collective-permute-done | bytes 131104 | tf_op jit(solution)/shard_map/ppermute | solution.py:88
  153.1 1.7 fusion.39
  154.9 3.9 %fusion.2 = f32[256]{0:T(256)S(1)} fusion(f32[16,256,16,16]{1,3,2,0:T(8,128)} %fusion.48, bf16[16,256,256,1]{2,1,3,0:T(8,128)(2,1)S(1)} %bitcast.211, bf16[256,16,16,1]{0,2,1,3:T(8,128)(2,1)S(1)} %bitcast.221, bf16[16,1,2,16,16,256]{5,4,3,2,1,0:T(8,128)(2,1)} %all-to-all-done.1), kind=kOutput, calls=%fused_computation.7 | convolution fusion | flops 541064960 | bytes 8520704 | tf_op jit(solution)/shard_map/qJj,saqc->Jsajc/dot_general | solution.py:40
  158.8 0.9 broadcast_in_dim.14
  159.6 15.4 %all-to-all-start.2 = ((f32[256,1,256]{2,1,0:T(1,128)}), f32[256,1,256]{2,1,0:T(1,128)S(1)}, u32[]{:S(2)}, u32[]{:S(2)}) async-start(f32[256,1,256]{2,1,0:T(1,128)} %broadcast_in_dim.14), calls=%async_computation.2 | async-start | bytes 524288 | tf_op jit(solution)/shard_map/all_to_all | solution.py:118
  175.1 5.3 %fusion.4 = (bf16[1,16,256,256]{3,2,1,0:T(8,128)(2,1)}, f32[1,16,256,256]{3,2,1,0:T(8,128)S(1)}, f32[16,256,256,1]{1,2,3,0:T(8,128)S(1)}) fusion(f32[256]{0:T(256)S(1)} %copy-done.9, bf16[1,16,256,256]{3,2,1,0:T(8,128)(2,1)} %bitcast.214, bf16[256,16,16,1]{0,2,1,3:T(8,128)(2,1)S(1)} %bitcast.222, bf16[16,1,2,16,16,256]{5,4,3,2,1,0:T(8,128)(2,1)} %all-to-all-done.1), kind=kOutput, calls=%fused_computation.12 | convolution fusion | flops 545259520 | bytes 14812160 | tf_op jit(solution)/shard_map/qJj,Jsajc->saqc/dot_general | solution.py:103
  180.3 5.3 %fusion.3 = bf16[1,16,256,256]{3,2,1,0:T(8,128)(2,1)} fusion(f32[16,256,256,1]{1,2,3,0:T(8,128)S(1)} %get-tuple-element.25, f32[1,16,256,256]{3,2,1,0:T(8,128)S(1)} %get-tuple-element.9, bf16[16,16,256,1]{2,1,0,3:T(8,128)(2,1)S(1)} %bitcast.225, f32[256]{0:T(256)S(1)} %copy-done.9, bf16[1,16,256,256]{3,2,1,0:T(8,128)(2,1)S(1)} %bitcast.223, ...), kind=kOutput, calls=%fused_computation.9 | convolution fusion | flops 551550976 | bytes 14812160 | tf_op jit(solution)/shard_map/Jjb,Jsajc->sabc/dot_general | solution.py:112
  185.6 4.8 %all-to-all-done.2 = f32[256,1,256]{2,1,0:T(1,128)S(1)} async-done(((f32[256,1,256]{2,1,0:T(1,128)}), f32[256,1,256]{2,1,0:T(1,128)S(1)}, u32[]{:S(2)}, u32[]{:S(2)}) %all-to-all-start.2) | async-done | bytes 262176 | tf_op jit(solution)/shard_map/all_to_all | solution.py:118
  190.5 0.3 reduce_sum.20
  190.8 0.6 broadcast_multiply_fusion
  (17 shorter events, 0.0 us)
Async XLA Ops:
  0.6 67.8 %copy-start = (bf16[256,256]{1,0:T(8,128)(2,1)S(1)}, bf16[256,256]{1,0:T(8,128)(2,1)}, u32[]{:S(2)}) copy-start(bf16[256,256]{1,0:T(8,128)(2,1)} %param.14) | copy-start | bytes 393220
  6.8 1.6 copy-start.4
  6.8 1.6 copy-start.8
  66.5 0.9 copy-start.6
  68.4 3.2 %copy-start.2 = (bf16[256,16,256]{2,1,0:T(8,128)(2,1)S(1)}, bf16[256,16,256]{2,1,0:T(8,128)(2,1)}, u32[]{:S(2)}) copy-start(bf16[256,16,256]{2,1,0:T(8,128)(2,1)} %param.11) | copy-start | bytes 6291460
  78.9 76.0 %all-to-all-start.1 = ((bf16[16,1,2,16,16,256]{5,4,3,2,1,0:T(8,128)(2,1)}), bf16[16,1,2,16,16,256]{5,4,3,2,1,0:T(8,128)(2,1)}, u32[]{:S(2)}, u32[]{:S(2)}) async-start(bf16[16,1,2,16,16,256]{5,4,3,2,1,0:T(8,128)(2,1)} %maximum_bitcast_fusion), calls=%async_computation.1 | async-start | bytes 8388608 | tf_op jit(solution)/shard_map/all_to_all | solution.py:101
  90.0 14.6 %collective-permute-start = (bf16[4,16,16,256]{3,2,1,0:T(8,128)(2,1)}, bf16[4,16,16,256]{3,2,1,0:T(8,128)(2,1)S(1)}, u32[]{:S(2)}, u32[]{:S(2)}) collective-permute-start(bf16[4,16,16,256]{3,2,1,0:T(8,128)(2,1)} %get-tuple-element.17), channel_id=1, source_target_pairs={{0,64},{16,80},{32,96},{48,112},{64,128},{80,144},{96,160},{112,17... | collective-permute-start | bytes 1572872 | tf_op jit(solution)/shard_map/ppermute | solution.py:78
  91.3 25.6 %collective-permute-start.1 = (bf16[4,16,16,256]{3,2,1,0:T(8,128)(2,1)}, bf16[4,16,16,256]{3,2,1,0:T(8,128)(2,1)}, u32[]{:S(2)}, u32[]{:S(2)}) collective-permute-start(bf16[4,16,16,256]{3,2,1,0:T(8,128)(2,1)} %get-tuple-element.19), channel_id=1, source_target_pairs={{0,128},{16,144},{32,160},{48,176},{64,192},{80,208},{96,224},{112... | collective-permute-start | bytes 1572872 | tf_op jit(solution)/shard_map/ppermute | solution.py:78
  94.0 23.0 %collective-permute-start.2 = (bf16[4,16,16,256]{3,2,1,0:T(8,128)(2,1)S(1)}, bf16[4,16,16,256]{3,2,1,0:T(8,128)(2,1)}, u32[]{:S(2)}, u32[]{:S(2)}) collective-permute-start(bf16[4,16,16,256]{3,2,1,0:T(8,128)(2,1)S(1)} %get-tuple-element.18), channel_id=1, source_target_pairs={{0,192},{16,208},{32,224},{48,240},{64,0},{80,16},{96,32},{112,48}... | collective-permute-start | bytes 1572872 | tf_op jit(solution)/shard_map/ppermute | solution.py:78
  100.5 28.5 %copy-start.3 = (bf16[1,4096,256]{2,1,0:T(8,128)(2,1)S(1)}, bf16[1,4096,256]{2,1,0:T(8,128)(2,1)}, u32[]{:S(2)}) copy-start(bf16[1,4096,256]{2,1,0:T(8,128)(2,1)} %get-tuple-element.14) | copy-start | bytes 6291460
  104.6 12.3 %copy-start.7 = (bf16[4,16,16,256]{3,2,1,0:T(8,128)(2,1)}, bf16[4,16,16,256]{3,2,1,0:T(8,128)(2,1)S(1)}, u32[]{:S(2)}) copy-start(bf16[4,16,16,256]{3,2,1,0:T(8,128)(2,1)S(1)} %collective-permute-done) | copy-start | bytes 1572868
  119.4 29.9 %collective-permute-start.3 = (bf16[16,16,256]{2,1,0:T(8,128)(2,1)}, bf16[16,16,256]{2,1,0:T(8,128)(2,1)S(1)}, u32[]{:S(2)}, u32[]{:S(2)}) collective-permute-start(bf16[16,16,256]{2,1,0:T(8,128)(2,1)} %get-tuple-element.20), channel_id=1, source_target_pairs={{0,16},{16,32},{32,48},{48,0},{64,80},{80,96},{96,112},{112,64},{1... | collective-permute-start | bytes 393224 | tf_op jit(solution)/shard_map/ppermute | solution.py:88
  122.4 30.7 %collective-permute-start.4 = (bf16[16,16,256]{2,1,0:T(8,128)(2,1)}, bf16[16,16,256]{2,1,0:T(8,128)(2,1)}, u32[]{:S(2)}, u32[]{:S(2)}) collective-permute-start(bf16[16,16,256]{2,1,0:T(8,128)(2,1)} %get-tuple-element.22), channel_id=1, source_target_pairs={{0,32},{16,48},{32,0},{48,16},{64,96},{80,112},{96,64},{112,80},{1... | collective-permute-start | bytes 393224 | tf_op jit(solution)/shard_map/ppermute | solution.py:88
  126.6 26.5 %collective-permute-start.5 = (bf16[16,16,256]{2,1,0:T(8,128)(2,1)}, bf16[16,16,256]{2,1,0:T(8,128)(2,1)}, u32[]{:S(2)}, u32[]{:S(2)}) collective-permute-start(bf16[16,16,256]{2,1,0:T(8,128)(2,1)} %get-tuple-element.21), channel_id=1, source_target_pairs={{0,48},{16,0},{32,16},{48,32},{64,112},{80,64},{96,80},{112,96},{1... | collective-permute-start | bytes 393224 | tf_op jit(solution)/shard_map/ppermute | solution.py:88
  154.9 20.2 %copy-start.9 = (f32[256]{0:T(256)S(1)}, f32[256]{0:T(256)}, u32[]{:S(2)}) copy-start(f32[256]{0:T(256)} %param.10) | copy-start | bytes 3076
  159.6 30.8 %all-to-all-start.2 = ((f32[256,1,256]{2,1,0:T(1,128)}), f32[256,1,256]{2,1,0:T(1,128)S(1)}, u32[]{:S(2)}, u32[]{:S(2)}) async-start(f32[256,1,256]{2,1,0:T(1,128)} %broadcast_in_dim.14), calls=%async_computation.2 | async-start | bytes 524288 | tf_op jit(solution)/shard_map/all_to_all | solution.py:118
  175.0 5.3 %copy-start.5 = (bf16[1,4096,256]{2,1,0:T(8,128)(2,1)S(1)}, bf16[1,4096,256]{2,1,0:T(8,128)(2,1)}, u32[]{:S(2)}) copy-start(bf16[1,4096,256]{2,1,0:T(8,128)(2,1)} %param.9) | copy-start | bytes 6291460
  180.3 11.0 %copy-start.1 = (bf16[256,256]{1,0:T(8,128)(2,1)S(1)}, bf16[256,256]{1,0:T(8,128)(2,1)}, u32[]{:S(2)}) copy-start(bf16[256,256]{1,0:T(8,128)(2,1)} %param.14) | copy-start | bytes 393220

commit v10 on v5

--- a/solution.py
+++ b/solution.py
@@ -59,6 +59,19 @@
     inner_index = scene_index % inner
     term_by_dest = kernel_term.reshape(outer, inner, block_len // scene_parts, chunk, channels)
     term_sent = term_by_dest.astype(bf16)
+    grad_second = (grad_weighted * kernel_f).astype(bf16)
+    grad_first = jnp.einsum(
+        "ia,sijc->sajc", across_mix, grad_second, preferred_element_type=f32
+    ).astype(bf16)
+    back = jnp.stack(
+        [
+            unmixed.reshape(scenes_here, parts, local_a, chunk, channels),
+            grad_first.reshape(scenes_here, parts, local_a, chunk, channels),
+        ],
+        axis=2,
+    )
+    back = jnp.moveaxis(back, 1, 0)
+    back, term_sent = lax.optimization_barrier((back, term_sent))
     partial = lax.dynamic_index_in_dim(term_by_dest, outer_index, 0, False)
     for shift in range(1, outer):
         piece = lax.dynamic_index_in_dim(term_sent, (outer_index + shift) % outer, 0, False)
@@ -78,18 +91,6 @@
             for k in range(inner)
         ]
         kernel_grad = kernel_grad + lax.ppermute(piece, "scene", pairs).astype(f32)
-    grad_second = (grad_weighted * kernel_f).astype(bf16)
-    grad_first = jnp.einsum(
-        "ia,sijc->sajc", across_mix, grad_second, preferred_element_type=f32
-    ).astype(bf16)
-    back = jnp.stack(
-        [
-            unmixed.reshape(scenes_here, parts, local_a, chunk, channels),
-            grad_first.reshape(scenes_here, parts, local_a, chunk, channels),
-        ],
-        axis=2,
-    )
-    back = jnp.moveaxis(back, 1, 0)
     returned = lax.all_to_all(back, "seq", split_axis=0, concat_axis=0, tiled=True)
     values = jnp.einsum(
         "qJj,Jsajc->saqc",

time: 189 us -> 191 us (1.011)
  waiting for transfers between devices: 36.9 us -> 41.5 us
  matrix products: 16.8 us -> 14.7 us
    all_to_all x1, waiting for transfers between devices: 11.8 us -> 16.2 us  [on_device(): lax.all_to_all(back, 'seq', split_axis=0, concat_axis=0, tiled=True)]
    dot_general x1, matrix products: 3.15 us -> 1.18 us  [on_device(): jnp.einsum('pi,spjc->sijc', across_unmix, spread_grad, preferred_element_...]
    unnamed x21 -> x23, local copies, waits for them, and re-layouts: 3.74 us -> 3.99 us
  transfers between devices with their start and end apart: 8 -> 8, of which waited for: 4 -> 4; matrix products, arithmetic and copies ran while one was open for 16% -> 14% of each run, Pallas kernels for 0% -> 0%
where the time goes in v10:
time: 191 us
  blocking collectives  55.9 us (29%)
  waiting for transfers between devices  41.5 us (22%)
  starting transfers between devices  41.4 us (22%)
  local copies, waits for them, and re-layouts  24.9 us (13%)
  matrix products  14.7 us (8%)
  other arithmetic  11.3 us (6%)
    all_to_all x1, blocking collectives, on_device(): lax.all_to_all(outgoing, 'seq', split_axis=0, concat_axis=0, tiled=True)  55.9 us
    all_to_all x1, starting transfers between devices, on_device(): lax.all_to_all(jnp.broadcast_to(gain_term, (devices, channels)), ('scene'...  21.2 us
    ppermute x3, waiting for transfers between devices, on_device(): partial = partial + lax.ppermute(piece, 'scene', pairs).astype(f32)  16.7 us
    all_to_all x1, waiting for transfers between devices, on_device(): lax.all_to_all(back, 'seq', split_axis=0, concat_axis=0, tiled=True)  16.2 us
    ppermute x3, starting transfers between devices, on_device(): kernel_grad = kernel_grad + lax.ppermute(piece, 'scene', pairs).astype(f32)  9.6 us
    reshape x2, local copies, waits for them, and re-layouts, on_device(): kernel_term.reshape(outer, inner, block_len // scene_parts, chunk, channels)  9 us
    all_to_all x1, waiting for transfers between devices, on_device(): lax.all_to_all(jnp.broadcast_to(gain_term, (devices, channels)), ('scene'...  8.52 us
    all_to_all x1, starting transfers between devices, on_device(): lax.all_to_all(back, 'seq', split_axis=0, concat_axis=0, tiled=True)  5.52 us
  transfers between devices with their start and end apart: 8, of which 4 were waited for; matrix products, arithmetic and copies ran while one was open for 14% of the time, Pallas kernels for 0%

profile of v10, /device:TPU:1, one launch (start us, length us, event | category | flops | bytes accessed | tf_op | source)
XLA Modules:
  0.0 190.5 jit_solution(5534642040370078263)
XLA Ops:
  0.6 0.0 copy-start
  0.6 1.0 copy.59
  1.7 3.5 %multiply_convert_fusion = bf16[1,4096,256]{2,1,0:T(8,128)(2,1)S(1)} fusion(f32[256]{0:T(256)} %param.10, bf16[1,4096,256]{2,1,0:T(8,128)(2,1)} %param.8, bf16[1,4096,256]{2,1,0:T(8,128)(2,1)} %param.9), kind=kLoop, calls=%fused_computation.18 | loop fusion | flops 9437184 | bytes 6292480 | tf_op jit(solution)/shard_map/convert_element_type | solution.py:24
  5.2 0.0 copy-start.3
  5.3 0.7 convert_bitcast_fusion.1
  6.0 0.8 copy-done.3
  6.8 0.7 convert_bitcast_fusion.2
  7.6 0.4 pad_maximum_fusion
  7.9 0.5 copy.60
  8.5 55.9 %all_to_all.16 = bf16[16,2,1,16,16,256]{5,4,3,2,1,0:T(8,128)(2,1)S(1)} all-to-all(bf16[16,2,1,16,16,256]{5,4,3,2,1,0:T(8,128)(2,1)S(1)} %copy.60), channel_id=1, replica_groups=mesh['scene'=16,'seq'=16] {'seq'}, dimensions={0} | all-to-all | bytes 8388608 | tf_op jit(solution)/shard_map/all_to_all | solution.py:34
  64.4 0.4 copy.110
  64.9 0.0 copy-start.7
  64.9 0.5 fusion.43
  65.3 0.4 copy-done.7
  65.8 1.0 fusion.21
  66.8 1.2 fusion.6
  68.0 0.4 copy-done.5
  68.4 1.1 fusion.24
  69.6 1.2 fusion.27
  70.8 1.2 copy.68
  71.9 1.2 copy.67
  73.1 3.6 %copy.105 = bf16[4,4,16,16,256]{4,3,2,1,0:T(8,128)(2,1)} copy(f32[4,4,16,16,256]{4,2,1,0,3:T(8,128)S(1)} %bitcast.182) | data formatting | bytes 6291456 | tf_op jit(solution)/shard_map/reshape | solution.py:60
  76.7 2.4 %maximum_bitcast_fusion = bf16[16,1,2,16,16,256]{5,4,3,2,1,0:T(8,128)(2,1)} fusion(bf16[1,16,1,16,16,256]{5,4,3,2,1,0:T(8,128)(2,1)S(1)} %copy.68, bf16[1,16,1,16,16,256]{5,4,3,2,1,0:T(8,128)(2,1)S(1)} %copy.67), kind=kLoop, calls=%fused_computation.5 | loop fusion | flops 2097152 | bytes 8388608 | tf_op jit(solution)/shard_map/transpose | solution.py:73
  79.1 5.5 %all-to-all-start.1 = ((bf16[16,1,2,16,16,256]{5,4,3,2,1,0:T(8,128)(2,1)}), bf16[16,1,2,16,16,256]{5,4,3,2,1,0:T(8,128)(2,1)}, u32[]{:S(2)}, u32[]{:S(2)}) async-start(bf16[16,1,2,16,16,256]{5,4,3,2,1,0:T(8,128)(2,1)} %maximum_bitcast_fusion), calls=%async_computation.1 | async-start | bytes 8388608 | tf_op jit(solution)/shard_map/all_to_all | solution.py:94
  84.6 2.5 %dynamic-slice_bitcast_fusion.2 = (bf16[4,16,16,256]{3,2,1,0:T(8,128)(2,1)}, bf16[4,16,16,256]{3,2,1,0:T(8,128)(2,1)S(1)}, bf16[4,16,16,256]{3,2,1,0:T(8,128)(2,1)}) fusion(bf16[4,4,16,16,256]{4,3,2,1,0:T(8,128)(2,1)} %copy.105, s32[]{:T(128)S(6)} %select_n.66, s32[]{:T(128)S(6)} %select_n.70, s32[]{:T(128)S(6)} %select_n.68), kind=kLoop, calls=%fused_computation.45 | loop fusion | bytes 3145740 | tf_op jit(solution)/shard_map/jit(dynamic_index_in_dim)/squeeze | solution.py:77
  87.1 1.3 collective-permute-start
  88.4 2.6 %collective-permute-start.1 = (bf16[4,16,16,256]{3,2,1,0:T(8,128)(2,1)}, bf16[4,16,16,256]{3,2,1,0:T(8,128)(2,1)}, u32[]{:S(2)}, u32[]{:S(2)}) collective-permute-start(bf16[4,16,16,256]{3,2,1,0:T(8,128)(2,1)} %get-tuple-element.18), channel_id=1, source_target_pairs={{0,128},{16,144},{32,160},{48,176},{64,192},{80,208},{96,224},{112... | collective-permute-start | bytes 1572872 | tf_op jit(solution)/shard_map/ppermute | solution.py:83
  91.0 1.1 collective-permute-start.2
  92.1 5.4 %copy.69 = f32[4,4,16,16,256]{4,3,2,1,0:T(8,128)S(1)} copy(f32[4,4,16,16,256]{4,2,1,0,3:T(8,128)} %bitcast.183) | data formatting | bytes 8388608 | tf_op jit(solution)/shard_map/reshape | solution.py:60
  97.5 4.3 %collective-permute-done = bf16[4,16,16,256]{3,2,1,0:T(8,128)(2,1)S(1)} collective-permute-done((bf16[4,16,16,256]{3,2,1,0:T(8,128)(2,1)}, bf16[4,16,16,256]{3,2,1,0:T(8,128)(2,1)S(1)}, u32[]{:S(2)}, u32[]{:S(2)}) %collective-permute-start) | collective-permute-done | bytes 524320 | tf_op jit(solution)/shard_map/ppermute | solution.py:83
  101.9 12.3 %collective-permute-done.1 = bf16[4,16,16,256]{3,2,1,0:T(8,128)(2,1)} collective-permute-done((bf16[4,16,16,256]{3,2,1,0:T(8,128)(2,1)}, bf16[4,16,16,256]{3,2,1,0:T(8,128)(2,1)}, u32[]{:S(2)}, u32[]{:S(2)}) %collective-permute-start.1) | collective-permute-done | bytes 524320 | tf_op jit(solution)/shard_map/ppermute | solution.py:83
  114.2 1.7 fusion.40
  115.9 0.8 dynamic-slice_bitcast_fusion.5
  116.7 3.0 %collective-permute-start.3 = (bf16[16,16,256]{2,1,0:T(8,128)(2,1)}, bf16[16,16,256]{2,1,0:T(8,128)(2,1)S(1)}, u32[]{:S(2)}, u32[]{:S(2)}) collective-permute-start(bf16[16,16,256]{2,1,0:T(8,128)(2,1)} %get-tuple-element.19), channel_id=1, source_target_pairs={{0,16},{16,32},{32,48},{48,0},{64,80},{80,96},{96,112},{112,64},{1... | collective-permute-start | bytes 393224 | tf_op jit(solution)/shard_map/ppermute | solution.py:93
  119.7 4.2 %collective-permute-start.4 = (bf16[16,16,256]{2,1,0:T(8,128)(2,1)}, bf16[16,16,256]{2,1,0:T(8,128)(2,1)}, u32[]{:S(2)}, u32[]{:S(2)}) collective-permute-start(bf16[16,16,256]{2,1,0:T(8,128)(2,1)} %get-tuple-element.21), channel_id=1, source_target_pairs={{0,32},{16,48},{32,0},{48,16},{64,96},{80,112},{96,64},{112,80},{1... | collective-permute-start | bytes 393224 | tf_op jit(solution)/shard_map/ppermute | solution.py:93
  123.9 2.4 %collective-permute-start.5 = (bf16[16,16,256]{2,1,0:T(8,128)(2,1)}, bf16[16,16,256]{2,1,0:T(8,128)(2,1)}, u32[]{:S(2)}, u32[]{:S(2)}) collective-permute-start(bf16[16,16,256]{2,1,0:T(8,128)(2,1)} %get-tuple-element.20), channel_id=1, source_target_pairs={{0,48},{16,0},{32,16},{48,32},{64,112},{80,64},{96,80},{112,96},{1... | collective-permute-start | bytes 393224 | tf_op jit(solution)/shard_map/ppermute | solution.py:93
  126.3 16.2 %all-to-all-done.1 = bf16[16,1,2,16,16,256]{5,4,3,2,1,0:T(8,128)(2,1)} async-done(((bf16[16,1,2,16,16,256]{5,4,3,2,1,0:T(8,128)(2,1)}), bf16[16,1,2,16,16,256]{5,4,3,2,1,0:T(8,128)(2,1)}, u32[]{:S(2)}, u32[]{:S(2)}) %all-to-all-start.1) | async-done | bytes 4194336 | tf_op jit(solution)/shard_map/all_to_all | solution.py:94
  142.5 4.0 %fusion.42 = (bf16[16,1,1,16,16,256]{5,4,3,2,1,0:T(8,128)(2,1)}, bf16[16,1,1,16,16,256]{5,4,3,2,1,0:T(8,128)(2,1)S(1)}) fusion(bf16[16,1,2,16,16,256]{5,4,3,2,1,0:T(8,128)(2,1)} %all-to-all-done.1), kind=kLoop, calls=%fused_computation.59 | loop fusion | bytes 8388608 | tf_op jit(solution)/shard_map/slice | solution.py:104
  146.6 3.6 %fusion.5 = (f32[1,16,256,256]{3,2,1,0:T(8,128)S(1)}, bf16[1,16,256,256]{3,2,1,0:T(8,128)(2,1)}) fusion(f32[256]{0:T(256)S(1)} %copy-done.10, bf16[1,4096,256]{2,1,0:T(8,128)(2,1)S(1)} %copy-done.3, bf16[256,16,16,1]{0,2,1,3:T(8,128)(2,1)S(1)} %bitcast.197, bf16[16,1,1,16,16,256]{5,4,3,2,1,0:T(8,128)(2,1)S(1)} %get-tuple-element.13, ...), kind=kOutput, calls=%fused_computation.12 | convolution fusion | flops 552599552 | bytes 12715008 | tf_op jit(solution)/shard_map/qJj,Jsajc->saqc/dot_general | solution.py:95
  150.2 0.7 multiply_reduce_fusion
  150.9 1.2 copy-done.4
  152.1 0.9 broadcast_in_dim.14
  153.0 21.2 %all-to-all-start.2 = ((f32[256,1,256]{2,1,0:T(1,128)}), f32[256,1,256]{2,1,0:T(1,128)S(1)}, u32[]{:S(2)}, u32[]{:S(2)}) async-start(f32[256,1,256]{2,1,0:T(1,128)} %broadcast_in_dim.14), calls=%async_computation.2 | async-start | bytes 524288 | tf_op jit(solution)/shard_map/all_to_all | solution.py:110
  174.3 1.7 fusion.35
  176.0 5.1 %fusion.2 = bf16[1,16,256,256]{3,2,1,0:T(8,128)(2,1)} fusion(f32[1,16,256,256]{3,2,1,0:T(8,128)} %copy-done.4, bf16[16,16,256,1]{2,1,0,3:T(8,128)(2,1)S(1)} %bitcast.195, bf16[16,1,1,16,16,256]{5,4,3,2,1,0:T(8,128)(2,1)} %get-tuple-element.12, f32[256]{0:T(256)S(1)} %copy-done.10), kind=kOutput, calls=%fused_computation.7 | convolution fusion | flops 540016640 | bytes 8520704 | tf_op jit(solution)/shard_map/Jjb,Jsajc->sabc/dot_general | solution.py:104
  181.1 8.5 %all-to-all-done.2 = f32[256,1,256]{2,1,0:T(1,128)S(1)} async-done(((f32[256,1,256]{2,1,0:T(1,128)}), f32[256,1,256]{2,1,0:T(1,128)S(1)}, u32[]{:S(2)}, u32[]{:S(2)}) %all-to-all-start.2) | async-done | bytes 262176 | tf_op jit(solution)/shard_map/all_to_all | solution.py:110
  189.7 0.3 reduce_sum.20
  189.9 0.6 broadcast_multiply_fusion
  (19 shorter events, 0.0 us)
Async XLA Ops:
  0.6 66.2 %copy-start = (bf16[256,256]{1,0:T(8,128)(2,1)S(1)}, bf16[256,256]{1,0:T(8,128)(2,1)}, u32[]{:S(2)}) copy-start(bf16[256,256]{1,0:T(8,128)(2,1)} %param.14) | copy-start | bytes 393220
  5.2 1.6 copy-start.3
  5.2 1.6 copy-start.8
  64.9 0.9 copy-start.7
  66.8 1.6 copy-start.5
  68.4 4.7 %copy-start.2 = (f32[1,256,16,256]{3,1,2,0:T(8,128)}, f32[1,256,16,256]{3,1,2,0:T(8,128)S(1)}, u32[]{:S(2)}) copy-start(f32[1,256,16,256]{3,1,2,0:T(8,128)S(1)} %get-tuple-element.22) | copy-start | bytes 12582916
  79.1 63.4 %all-to-all-start.1 = ((bf16[16,1,2,16,16,256]{5,4,3,2,1,0:T(8,128)(2,1)}), bf16[16,1,2,16,16,256]{5,4,3,2,1,0:T(8,128)(2,1)}, u32[]{:S(2)}, u32[]{:S(2)}) async-start(bf16[16,1,2,16,16,256]{5,4,3,2,1,0:T(8,128)(2,1)} %maximum_bitcast_fusion), calls=%async_computation.1 | async-start | bytes 8388608 | tf_op jit(solution)/shard_map/all_to_all | solution.py:94
  87.1 14.8 %collective-permute-start = (bf16[4,16,16,256]{3,2,1,0:T(8,128)(2,1)}, bf16[4,16,16,256]{3,2,1,0:T(8,128)(2,1)S(1)}, u32[]{:S(2)}, u32[]{:S(2)}) collective-permute-start(bf16[4,16,16,256]{3,2,1,0:T(8,128)(2,1)} %get-tuple-element.16), channel_id=1, source_target_pairs={{0,64},{16,80},{32,96},{48,112},{64,128},{80,144},{96,160},{112,17... | collective-permute-start | bytes 1572872 | tf_op jit(solution)/shard_map/ppermute | solution.py:83
  88.4 25.8 %collective-permute-start.1 = (bf16[4,16,16,256]{3,2,1,0:T(8,128)(2,1)}, bf16[4,16,16,256]{3,2,1,0:T(8,128)(2,1)}, u32[]{:S(2)}, u32[]{:S(2)}) collective-permute-start(bf16[4,16,16,256]{3,2,1,0:T(8,128)(2,1)} %get-tuple-element.18), channel_id=1, source_target_pairs={{0,128},{16,144},{32,160},{48,176},{64,192},{80,208},{96,224},{112... | collective-permute-start | bytes 1572872 | tf_op jit(solution)/shard_map/ppermute | solution.py:83
  91.0 23.2 %collective-permute-start.2 = (bf16[4,16,16,256]{3,2,1,0:T(8,128)(2,1)S(1)}, bf16[4,16,16,256]{3,2,1,0:T(8,128)(2,1)}, u32[]{:S(2)}, u32[]{:S(2)}) collective-permute-start(bf16[4,16,16,256]{3,2,1,0:T(8,128)(2,1)S(1)} %get-tuple-element.17), channel_id=1, source_target_pairs={{0,192},{16,208},{32,224},{48,240},{64,0},{80,16},{96,32},{112,48}... | collective-permute-start | bytes 1572872 | tf_op jit(solution)/shard_map/ppermute | solution.py:83
  101.9 12.3 %copy-start.9 = (bf16[4,16,16,256]{3,2,1,0:T(8,128)(2,1)}, bf16[4,16,16,256]{3,2,1,0:T(8,128)(2,1)S(1)}, u32[]{:S(2)}) copy-start(bf16[4,16,16,256]{3,2,1,0:T(8,128)(2,1)S(1)} %collective-permute-done) | copy-start | bytes 1572868
  116.7 57.6 %collective-permute-start.3 = (bf16[16,16,256]{2,1,0:T(8,128)(2,1)}, bf16[16,16,256]{2,1,0:T(8,128)(2,1)S(1)}, u32[]{:S(2)}, u32[]{:S(2)}) collective-permute-start(bf16[16,16,256]{2,1,0:T(8,128)(2,1)} %get-tuple-element.19), channel_id=1, source_target_pairs={{0,16},{16,32},{32,48},{48,0},{64,80},{80,96},{96,112},{112,64},{1... | collective-permute-start | bytes 393224 | tf_op jit(solution)/shard_map/ppermute | solution.py:93
  119.7 54.6 %collective-permute-start.4 = (bf16[16,16,256]{2,1,0:T(8,128)(2,1)}, bf16[16,16,256]{2,1,0:T(8,128)(2,1)}, u32[]{:S(2)}, u32[]{:S(2)}) collective-permute-start(bf16[16,16,256]{2,1,0:T(8,128)(2,1)} %get-tuple-element.21), channel_id=1, source_target_pairs={{0,32},{16,48},{32,0},{48,16},{64,96},{80,112},{96,64},{112,80},{1... | collective-permute-start | bytes 393224 | tf_op jit(solution)/shard_map/ppermute | solution.py:93
  123.9 22.7 %copy-start.10 = (f32[256]{0:T(256)S(1)}, f32[256]{0:T(256)}, u32[]{:S(2)}) copy-start(f32[256]{0:T(256)} %param.10) | copy-start | bytes 3076
  123.9 50.4 %collective-permute-start.5 = (bf16[16,16,256]{2,1,0:T(8,128)(2,1)}, bf16[16,16,256]{2,1,0:T(8,128)(2,1)}, u32[]{:S(2)}, u32[]{:S(2)}) collective-permute-start(bf16[16,16,256]{2,1,0:T(8,128)(2,1)} %get-tuple-element.20), channel_id=1, source_target_pairs={{0,48},{16,0},{32,16},{48,32},{64,112},{80,64},{96,80},{112,96},{1... | collective-permute-start | bytes 393224 | tf_op jit(solution)/shard_map/ppermute | solution.py:93
  142.5 4.1 %copy-start.6 = (bf16[1,4096,256]{2,1,0:T(8,128)(2,1)S(1)}, bf16[1,4096,256]{2,1,0:T(8,128)(2,1)}, u32[]{:S(2)}) copy-start(bf16[1,4096,256]{2,1,0:T(8,128)(2,1)} %param.9) | copy-start | bytes 6291460
  150.2 1.9 %copy-start.4 = (f32[1,16,256,256]{3,2,1,0:T(8,128)}, f32[1,16,256,256]{3,2,1,0:T(8,128)S(1)}, u32[]{:S(2)}) copy-start(f32[1,16,256,256]{3,2,1,0:T(8,128)S(1)} %get-tuple-element.10) | copy-start | bytes 12582916
  153.0 36.7 %all-to-all-start.2 = ((f32[256,1,256]{2,1,0:T(1,128)}), f32[256,1,256]{2,1,0:T(1,128)S(1)}, u32[]{:S(2)}, u32[]{:S(2)}) async-start(f32[256,1,256]{2,1,0:T(1,128)} %broadcast_in_dim.14), calls=%async_computation.2 | async-start | bytes 524288 | tf_op jit(solution)/shard_map/all_to_all | solution.py:110
  176.0 14.5 %copy-start.1 = (bf16[256,256]{1,0:T(8,128)(2,1)S(1)}, bf16[256,256]{1,0:T(8,128)(2,1)}, u32[]{:S(2)}) copy-start(bf16[256,256]{1,0:T(8,128)(2,1)} %param.14) | copy-start | bytes 393220

commit v11 on v5

--- a/solution.py
+++ b/solution.py
@@ -105,10 +105,10 @@
     )
     grad_input = grad_input.astype(bf16).reshape(scenes_here, row_count, channels)
     gain_term = jnp.sum(inputs.astype(f32) * grad_gate, axis=(0, 1, 2))
-    devices = lax.axis_size(("scene", "seq"))
+    devices = lax.axis_size(("seq", "scene"))
     gain_spread = lax.all_to_all(
         jnp.broadcast_to(gain_term, (devices, channels)),
-        ("scene", "seq"),
+        ("seq", "scene"),
         split_axis=0,
         concat_axis=0,
         tiled=True,

time: 189 us -> 189 us (level)
  no operation moved by 1% of the time
where the time goes in v11:
time: 189 us; the launch traced here: 188 us
  blocking collectives  55.9 us (30%)
  starting transfers between devices  42.5 us (22%)
  waiting for transfers between devices  36.8 us (19%)
  local copies, waits for them, and re-layouts  24.1 us (13%)
  matrix products  16.8 us (9%)
  other arithmetic  11.2 us (6%)
    all_to_all x1, blocking collectives, on_device(): lax.all_to_all(outgoing, 'seq', split_axis=0, concat_axis=0, tiled=True)  55.9 us
    all_to_all x1, starting transfers between devices, on_device(): lax.all_to_all(jnp.broadcast_to(gain_term, (devices, channels)), ('seq',...  22.4 us
    ppermute x3, waiting for transfers between devices, on_device(): partial = partial + lax.ppermute(piece, 'scene', pairs).astype(f32)  16.5 us
    all_to_all x1, waiting for transfers between devices, on_device(): lax.all_to_all(back, 'seq', split_axis=0, concat_axis=0, tiled=True)  11.8 us
    reshape x2, local copies, waits for them, and re-layouts, on_device(): kernel_term.reshape(outer, inner, block_len // scene_parts, chunk, channels)  9.86 us
    ppermute x3, starting transfers between devices, on_device(): kernel_grad = kernel_grad + lax.ppermute(piece, 'scene', pairs).astype(f32)  9.58 us
    all_to_all x1, waiting for transfers between devices, on_device(): lax.all_to_all(jnp.broadcast_to(gain_term, (devices, channels)), ('seq',...  8.41 us
    all_to_all x1, starting transfers between devices, on_device(): lax.all_to_all(back, 'seq', split_axis=0, concat_axis=0, tiled=True)  5.52 us
  transfers between devices with their start and end apart: 8, of which 4 were waited for; matrix products, arithmetic and copies ran while one was open for 16% of the time, Pallas kernels for 0%

profile of v11, /device:TPU:1, one launch (start us, length us, event | category | flops | bytes accessed | tf_op | source)
XLA Modules:
  0.0 188.2 jit_solution(2364500195781720568)
XLA Ops:
  0.6 0.0 copy-start
  0.6 1.0 copy.59
  1.7 3.5 %multiply_convert_fusion = bf16[1,4096,256]{2,1,0:T(8,128)(2,1)S(1)} fusion(f32[256]{0:T(256)} %param.10, bf16[1,4096,256]{2,1,0:T(8,128)(2,1)} %param.8, bf16[1,4096,256]{2,1,0:T(8,128)(2,1)} %param.9), kind=kLoop, calls=%fused_computation.18 | loop fusion | flops 9437184 | bytes 6292480 | tf_op jit(solution)/shard_map/convert_element_type | solution.py:24
  5.2 0.0 copy-start.2
  5.2 0.0 copy-start.7
  5.3 0.7 convert_bitcast_fusion.1
  6.0 0.8 copy-done.2
  6.8 0.7 convert_bitcast_fusion.2
  7.6 0.4 pad_maximum_fusion
  7.9 0.5 copy.60
  8.5 55.9 %all_to_all.16 = bf16[16,2,1,16,16,256]{5,4,3,2,1,0:T(8,128)(2,1)S(1)} all-to-all(bf16[16,2,1,16,16,256]{5,4,3,2,1,0:T(8,128)(2,1)S(1)} %copy.60), channel_id=1, replica_groups=mesh['scene'=16,'seq'=16] {'seq'}, dimensions={0} | all-to-all | bytes 8388608 | tf_op jit(solution)/shard_map/all_to_all | solution.py:34
  64.4 0.4 copy.110
  64.9 0.3 fusion.43
  65.2 0.6 copy-done.6
  65.8 1.0 fusion.21
  66.8 0.0 copy-start.4
  66.8 3.2 %fusion.3 = (f32[1,256,16,256]{3,1,2,0:T(8,128)}, f32[16,256,256]{1,2,0:T(8,128)S(1)}) fusion(bf16[16,256,256]{1,2,0:T(8,128)(2,1)S(1)} %fusion.21, bf16[256,256]{1,0:T(8,128)(2,1)S(1)} %copy-done, bf16[256,16,256]{2,1,0:T(8,128)(2,1)S(1)} %bitcast.188), kind=kOutput, calls=%fused_computation.9 | convolution fusion | flops 538968064 | bytes 12713984 | tf_op jit(solution)/shard_map/pi,spjc->sijc/dot_general | solution.py:50
  70.0 1.2 fusion.24
  71.2 1.3 fusion.27
  72.5 1.2 copy.68
  73.7 1.2 copy.67
  74.9 2.4 %maximum_bitcast_fusion = bf16[16,1,2,16,16,256]{5,4,3,2,1,0:T(8,128)(2,1)} fusion(bf16[1,16,1,16,16,256]{5,4,3,2,1,0:T(8,128)(2,1)S(1)} %copy.68, bf16[1,16,1,16,16,256]{5,4,3,2,1,0:T(8,128)(2,1)S(1)} %copy.67), kind=kLoop, calls=%fused_computation.5 | loop fusion | flops 2097152 | bytes 8388608 | tf_op jit(solution)/shard_map/transpose | solution.py:92
  77.2 5.5 %all-to-all-start.1 = ((bf16[16,1,2,16,16,256]{5,4,3,2,1,0:T(8,128)(2,1)}), bf16[16,1,2,16,16,256]{5,4,3,2,1,0:T(8,128)(2,1)}, u32[]{:S(2)}, u32[]{:S(2)}) async-start(bf16[16,1,2,16,16,256]{5,4,3,2,1,0:T(8,128)(2,1)} %maximum_bitcast_fusion), calls=%async_computation.1 | async-start | bytes 8388608 | tf_op jit(solution)/shard_map/all_to_all | solution.py:93
  82.8 4.4 %copy.105 = bf16[4,4,16,16,256]{4,3,2,1,0:T(8,128)(2,1)S(1)} copy(f32[4,4,16,16,256]{4,2,1,0,3:T(8,128)} %bitcast.182) | data formatting | bytes 6291456 | tf_op jit(solution)/shard_map/reshape | solution.py:60
  87.2 1.1 dynamic-slice_bitcast_fusion.2
  88.3 1.3 collective-permute-start
  89.6 2.6 %collective-permute-start.1 = (bf16[4,16,16,256]{3,2,1,0:T(8,128)(2,1)}, bf16[4,16,16,256]{3,2,1,0:T(8,128)(2,1)}, u32[]{:S(2)}, u32[]{:S(2)}) collective-permute-start(bf16[4,16,16,256]{3,2,1,0:T(8,128)(2,1)} %get-tuple-element.14), channel_id=1, source_target_pairs={{0,128},{16,144},{32,160},{48,176},{64,192},{80,208},{96,224},{112... | collective-permute-start | bytes 1572872 | tf_op jit(solution)/shard_map/ppermute | solution.py:70
  92.2 1.1 collective-permute-start.2
  93.3 5.4 %copy.71 = f32[4,4,16,16,256]{4,3,2,1,0:T(8,128)S(1)} copy(f32[4,4,16,16,256]{4,2,1,0,3:T(8,128)} %bitcast.183) | data formatting | bytes 8388608 | tf_op jit(solution)/shard_map/reshape | solution.py:60
  98.8 4.2 %collective-permute-done = bf16[4,16,16,256]{3,2,1,0:T(8,128)(2,1)S(1)} collective-permute-done((bf16[4,16,16,256]{3,2,1,0:T(8,128)(2,1)}, bf16[4,16,16,256]{3,2,1,0:T(8,128)(2,1)S(1)}, u32[]{:S(2)}, u32[]{:S(2)}) %collective-permute-start) | collective-permute-done | bytes 524320 | tf_op jit(solution)/shard_map/ppermute | solution.py:70
  102.9 12.3 %collective-permute-done.1 = bf16[4,16,16,256]{3,2,1,0:T(8,128)(2,1)} collective-permute-done((bf16[4,16,16,256]{3,2,1,0:T(8,128)(2,1)}, bf16[4,16,16,256]{3,2,1,0:T(8,128)(2,1)}, u32[]{:S(2)}, u32[]{:S(2)}) %collective-permute-start.1) | collective-permute-done | bytes 524320 | tf_op jit(solution)/shard_map/ppermute | solution.py:70
  115.3 1.7 fusion.40
  116.9 0.8 dynamic-slice_bitcast_fusion.5
  117.7 3.0 %collective-permute-start.3 = (bf16[16,16,256]{2,1,0:T(8,128)(2,1)}, bf16[16,16,256]{2,1,0:T(8,128)(2,1)S(1)}, u32[]{:S(2)}, u32[]{:S(2)}) collective-permute-start(bf16[16,16,256]{2,1,0:T(8,128)(2,1)} %get-tuple-element.15), channel_id=1, source_target_pairs={{0,16},{16,32},{32,48},{48,0},{64,80},{80,96},{96,112},{112,64},{1... | collective-permute-start | bytes 393224 | tf_op jit(solution)/shard_map/ppermute | solution.py:80
  120.7 4.2 %collective-permute-start.4 = (bf16[16,16,256]{2,1,0:T(8,128)(2,1)}, bf16[16,16,256]{2,1,0:T(8,128)(2,1)}, u32[]{:S(2)}, u32[]{:S(2)}) collective-permute-start(bf16[16,16,256]{2,1,0:T(8,128)(2,1)} %get-tuple-element.17), channel_id=1, source_target_pairs={{0,32},{16,48},{32,0},{48,16},{64,96},{80,112},{96,64},{112,80},{1... | collective-permute-start | bytes 393224 | tf_op jit(solution)/shard_map/ppermute | solution.py:80
  124.9 2.4 %collective-permute-start.5 = (bf16[16,16,256]{2,1,0:T(8,128)(2,1)}, bf16[16,16,256]{2,1,0:T(8,128)(2,1)}, u32[]{:S(2)}, u32[]{:S(2)}) collective-permute-start(bf16[16,16,256]{2,1,0:T(8,128)(2,1)} %get-tuple-element.16), channel_id=1, source_target_pairs={{0,48},{16,0},{32,16},{48,32},{64,112},{80,64},{96,80},{112,96},{1... | collective-permute-start | bytes 393224 | tf_op jit(solution)/shard_map/ppermute | solution.py:80
  127.3 11.8 %all-to-all-done.1 = bf16[16,1,2,16,16,256]{5,4,3,2,1,0:T(8,128)(2,1)} async-done(((bf16[16,1,2,16,16,256]{5,4,3,2,1,0:T(8,128)(2,1)}), bf16[16,1,2,16,16,256]{5,4,3,2,1,0:T(8,128)(2,1)}, u32[]{:S(2)}, u32[]{:S(2)}) %all-to-all-start.1) | async-done | bytes 4194336 | tf_op jit(solution)/shard_map/all_to_all | solution.py:93
  139.1 4.1 %fusion.42 = (bf16[16,1,1,16,16,256]{5,4,3,2,1,0:T(8,128)(2,1)}, bf16[16,1,1,16,16,256]{5,4,3,2,1,0:T(8,128)(2,1)S(1)}) fusion(bf16[16,1,2,16,16,256]{5,4,3,2,1,0:T(8,128)(2,1)} %all-to-all-done.1), kind=kLoop, calls=%fused_computation.59 | loop fusion | bytes 8388608 | tf_op jit(solution)/shard_map/slice | solution.py:103
  143.2 3.6 %fusion.6 = (f32[1,16,256,256]{3,2,1,0:T(8,128)S(1)}, bf16[1,16,256,256]{3,2,1,0:T(8,128)(2,1)}) fusion(f32[256]{0:T(256)S(1)} %copy-done.9, bf16[1,4096,256]{2,1,0:T(8,128)(2,1)S(1)} %copy-done.2, bf16[256,16,16,1]{0,2,1,3:T(8,128)(2,1)S(1)} %bitcast.197, bf16[16,1,1,16,16,256]{5,4,3,2,1,0:T(8,128)(2,1)S(1)} %get-tuple-element.9, ...), kind=kOutput, calls=%fused_computation.14 | convolution fusion | flops 552599552 | bytes 12715008 | tf_op jit(solution)/shard_map/qJj,Jsajc->saqc/dot_general | solution.py:94
  146.8 0.7 multiply_reduce_fusion
  147.5 1.2 copy-done.3
  148.8 0.8 broadcast_in_dim.14
  149.6 22.4 %all-to-all-start.2 = ((f32[256,1,256]{2,1,0:T(1,128)}), f32[256,1,256]{2,1,0:T(1,128)S(1)}, u32[]{:S(2)}, u32[]{:S(2)}) async-start(f32[256,1,256]{2,1,0:T(1,128)} %broadcast_in_dim.14), calls=%async_computation.2 | async-start | bytes 524288 | tf_op jit(solution)/shard_map/all_to_all | solution.py:109
  172.1 1.7 fusion.35
  173.8 5.1 %fusion.2 = bf16[1,16,256,256]{3,2,1,0:T(8,128)(2,1)} fusion(f32[1,16,256,256]{3,2,1,0:T(8,128)} %copy-done.3, bf16[16,16,256,1]{2,1,0,3:T(8,128)(2,1)S(1)} %bitcast.195, bf16[16,1,1,16,16,256]{5,4,3,2,1,0:T(8,128)(2,1)} %get-tuple-element.8, f32[256]{0:T(256)S(1)} %copy-done.9), kind=kOutput, calls=%fused_computation.7 | convolution fusion | flops 540016640 | bytes 8520704 | tf_op jit(solution)/shard_map/Jjb,Jsajc->sabc/dot_general | solution.py:103
  178.9 8.4 %all-to-all-done.2 = f32[256,1,256]{2,1,0:T(1,128)S(1)} async-done(((f32[256,1,256]{2,1,0:T(1,128)}), f32[256,1,256]{2,1,0:T(1,128)S(1)}, u32[]{:S(2)}, u32[]{:S(2)}) %all-to-all-start.2) | async-done | bytes 262176 | tf_op jit(solution)/shard_map/all_to_all | solution.py:109
  187.3 0.3 reduce_sum.20
  187.6 0.6 broadcast_multiply_fusion
  (17 shorter events, 0.0 us)
Async XLA Ops:
  0.6 66.2 %copy-start = (bf16[256,256]{1,0:T(8,128)(2,1)S(1)}, bf16[256,256]{1,0:T(8,128)(2,1)}, u32[]{:S(2)}) copy-start(bf16[256,256]{1,0:T(8,128)(2,1)} %param.14) | copy-start | bytes 393220
  5.2 1.6 copy-start.2
  5.2 1.6 copy-start.7
  64.9 0.9 copy-start.6
  66.8 3.2 %copy-start.4 = (bf16[256,16,256]{2,1,0:T(8,128)(2,1)S(1)}, bf16[256,16,256]{2,1,0:T(8,128)(2,1)}, u32[]{:S(2)}) copy-start(bf16[256,16,256]{2,1,0:T(8,128)(2,1)} %param.11) | copy-start | bytes 6291460
  77.2 61.9 %all-to-all-start.1 = ((bf16[16,1,2,16,16,256]{5,4,3,2,1,0:T(8,128)(2,1)}), bf16[16,1,2,16,16,256]{5,4,3,2,1,0:T(8,128)(2,1)}, u32[]{:S(2)}, u32[]{:S(2)}) async-start(bf16[16,1,2,16,16,256]{5,4,3,2,1,0:T(8,128)(2,1)} %maximum_bitcast_fusion), calls=%async_computation.1 | async-start | bytes 8388608 | tf_op jit(solution)/shard_map/all_to_all | solution.py:93
  88.3 14.6 %collective-permute-start = (bf16[4,16,16,256]{3,2,1,0:T(8,128)(2,1)}, bf16[4,16,16,256]{3,2,1,0:T(8,128)(2,1)S(1)}, u32[]{:S(2)}, u32[]{:S(2)}) collective-permute-start(bf16[4,16,16,256]{3,2,1,0:T(8,128)(2,1)} %get-tuple-element.12), channel_id=1, source_target_pairs={{0,64},{16,80},{32,96},{48,112},{64,128},{80,144},{96,160},{112,17... | collective-permute-start | bytes 1572872 | tf_op jit(solution)/shard_map/ppermute | solution.py:70
  89.6 25.7 %collective-permute-start.1 = (bf16[4,16,16,256]{3,2,1,0:T(8,128)(2,1)}, bf16[4,16,16,256]{3,2,1,0:T(8,128)(2,1)}, u32[]{:S(2)}, u32[]{:S(2)}) collective-permute-start(bf16[4,16,16,256]{3,2,1,0:T(8,128)(2,1)} %get-tuple-element.14), channel_id=1, source_target_pairs={{0,128},{16,144},{32,160},{48,176},{64,192},{80,208},{96,224},{112... | collective-permute-start | bytes 1572872 | tf_op jit(solution)/shard_map/ppermute | solution.py:70
  92.2 23.0 %collective-permute-start.2 = (bf16[4,16,16,256]{3,2,1,0:T(8,128)(2,1)S(1)}, bf16[4,16,16,256]{3,2,1,0:T(8,128)(2,1)}, u32[]{:S(2)}, u32[]{:S(2)}) collective-permute-start(bf16[4,16,16,256]{3,2,1,0:T(8,128)(2,1)S(1)} %get-tuple-element.13), channel_id=1, source_target_pairs={{0,192},{16,208},{32,224},{48,240},{64,0},{80,16},{96,32},{112,48}... | collective-permute-start | bytes 1572872 | tf_op jit(solution)/shard_map/ppermute | solution.py:70
  102.9 12.3 %copy-start.8 = (bf16[4,16,16,256]{3,2,1,0:T(8,128)(2,1)}, bf16[4,16,16,256]{3,2,1,0:T(8,128)(2,1)S(1)}, u32[]{:S(2)}) copy-start(bf16[4,16,16,256]{3,2,1,0:T(8,128)(2,1)S(1)} %collective-permute-done) | copy-start | bytes 1572868
  117.7 54.3 %collective-permute-start.3 = (bf16[16,16,256]{2,1,0:T(8,128)(2,1)}, bf16[16,16,256]{2,1,0:T(8,128)(2,1)S(1)}, u32[]{:S(2)}, u32[]{:S(2)}) collective-permute-start(bf16[16,16,256]{2,1,0:T(8,128)(2,1)} %get-tuple-element.15), channel_id=1, source_target_pairs={{0,16},{16,32},{32,48},{48,0},{64,80},{80,96},{96,112},{112,64},{1... | collective-permute-start | bytes 393224 | tf_op jit(solution)/shard_map/ppermute | solution.py:80
  120.7 51.4 %collective-permute-start.4 = (bf16[16,16,256]{2,1,0:T(8,128)(2,1)}, bf16[16,16,256]{2,1,0:T(8,128)(2,1)}, u32[]{:S(2)}, u32[]{:S(2)}) collective-permute-start(bf16[16,16,256]{2,1,0:T(8,128)(2,1)} %get-tuple-element.17), channel_id=1, source_target_pairs={{0,32},{16,48},{32,0},{48,16},{64,96},{80,112},{96,64},{112,80},{1... | collective-permute-start | bytes 393224 | tf_op jit(solution)/shard_map/ppermute | solution.py:80
  124.9 18.3 %copy-start.9 = (f32[256]{0:T(256)S(1)}, f32[256]{0:T(256)}, u32[]{:S(2)}) copy-start(f32[256]{0:T(256)} %param.10) | copy-start | bytes 3076
  124.9 47.1 %collective-permute-start.5 = (bf16[16,16,256]{2,1,0:T(8,128)(2,1)}, bf16[16,16,256]{2,1,0:T(8,128)(2,1)}, u32[]{:S(2)}, u32[]{:S(2)}) collective-permute-start(bf16[16,16,256]{2,1,0:T(8,128)(2,1)} %get-tuple-element.16), channel_id=1, source_target_pairs={{0,48},{16,0},{32,16},{48,32},{64,112},{80,64},{96,80},{112,96},{1... | collective-permute-start | bytes 393224 | tf_op jit(solution)/shard_map/ppermute | solution.py:80
  139.1 4.1 %copy-start.5 = (bf16[1,4096,256]{2,1,0:T(8,128)(2,1)S(1)}, bf16[1,4096,256]{2,1,0:T(8,128)(2,1)}, u32[]{:S(2)}) copy-start(bf16[1,4096,256]{2,1,0:T(8,128)(2,1)} %param.9) | copy-start | bytes 6291460
  146.8 1.9 %copy-start.3 = (f32[1,16,256,256]{3,2,1,0:T(8,128)}, f32[1,16,256,256]{3,2,1,0:T(8,128)S(1)}, u32[]{:S(2)}) copy-start(f32[1,16,256,256]{3,2,1,0:T(8,128)S(1)} %get-tuple-element.6) | copy-start | bytes 12582916
  149.6 37.7 %all-to-all-start.2 = ((f32[256,1,256]{2,1,0:T(1,128)}), f32[256,1,256]{2,1,0:T(1,128)S(1)}, u32[]{:S(2)}, u32[]{:S(2)}) async-start(f32[256,1,256]{2,1,0:T(1,128)} %broadcast_in_dim.14), calls=%async_computation.2 | async-start | bytes 524288 | tf_op jit(solution)/shard_map/all_to_all | solution.py:109
  173.8 14.4 %copy-start.1 = (bf16[256,256]{1,0:T(8,128)(2,1)S(1)}, bf16[256,256]{1,0:T(8,128)(2,1)}, u32[]{:S(2)}) copy-start(bf16[256,256]{1,0:T(8,128)(2,1)} %param.14) | copy-start | bytes 393220

commit v12 on v7

--- a/solution.py
+++ b/solution.py
@@ -78,6 +78,7 @@
         partial = partial + lax.ppermute(piece, "scene", pairs).astype(f32)
     kernel_grad = lax.dynamic_index_in_dim(partial, inner_index, 0, False)
     partial_sent = partial.astype(bf16)
+    stage_two = []
     for shift in range(1, inner):
         piece = lax.dynamic_index_in_dim(partial_sent, (inner_index + shift) % inner, 0, False)
         pairs = [
@@ -85,7 +86,7 @@
             for o in range(outer)
             for k in range(inner)
         ]
-        kernel_grad = kernel_grad + lax.ppermute(piece, "scene", pairs).astype(f32)
+        stage_two.append(lax.ppermute(piece, "scene", pairs))
     grad_second = (grad_weighted * kernel_f).astype(bf16)
     grad_first = jnp.einsum(
         "ia,sijc->sajc", across_mix, grad_second, preferred_element_type=f32
@@ -113,6 +114,10 @@
     )
     grad_input = grad_input.astype(bf16).reshape(scenes_here, row_count, channels)
     gain_term = jnp.sum(returned[:, :, 0].astype(f32) * gain_weight, axis=(0, 1, 2, 3))
+    mixed_out, grad_input, stage_two = lax.optimization_barrier((mixed_out, grad_input, stage_two))
+    for moved in stage_two:
+        kernel_grad = kernel_grad + moved.astype(f32)
+    gain_term, kernel_grad = lax.optimization_barrier((gain_term, kernel_grad))
     devices = lax.axis_size(("scene", "seq"))
     gain_spread = lax.all_to_all(
         jnp.broadcast_to(gain_term, (devices, channels)),

time: 198 us -> 192 us (0.970)
  blocking collectives: 55.9 us -> 90.6 us
  waiting for transfers between devices: 46.5 us -> 29.3 us
  starting transfers between devices: 35.5 us -> 20.1 us
  matrix products: 24.4 us -> 20.1 us
  local copies, waits for them, and re-layouts: 22.7 us -> 18.7 us
    all_to_all x0 -> x1, blocking collectives: none -> 34.6 us  [on_device(): lax.all_to_all(jnp.broadcast_to(gain_term, (devices, channels)), ('scene'...]
    ppermute x3, waiting for transfers between devices: 21.4 us -> 3.17 us  [on_device(): stage_two.append(lax.ppermute(piece, 'scene', pairs))]
    all_to_all x1 -> x0, starting transfers between devices: 15.4 us -> none  [on_device(): lax.all_to_all(jnp.broadcast_to(gain_term, (devices, channels)), ('scene'...]
    all_to_all x1, waiting for transfers between devices: 0.01 us -> 11.9 us  [on_device(): lax.all_to_all(back, 'seq', split_axis=0, concat_axis=0, tiled=True)]
    all_to_all x1 -> x0, waiting for transfers between devices: 8.56 us -> none  [on_device(): lax.all_to_all(jnp.broadcast_to(gain_term, (devices, channels)), ('scene'...]
    dot_general x1, matrix products: 6.87 us -> 3.43 us  [on_device(): jnp.einsum('Jjb,Jsajc->sabc', mix_by_dest, returned[:, :, 1], preferred_e...]
    dot_general x1, matrix products: 5.47 us -> 2.89 us  [on_device(): jnp.einsum('qJj,Jsajc->saqc', unmix_by_dest, returned[:, :, 0], preferred...]
    ppermute x3, waiting for transfers between devices: 16.5 us -> 14.3 us  [on_device(): partial = partial + lax.ppermute(piece, 'scene', pairs).astype(f32)]
  transfers between devices with their start and end apart: 8 -> 7, of which waited for: 5 -> 4; matrix products, arithmetic and copies ran while one was open for 13% -> 13% of each run, Pallas kernels for 0% -> 0%
where the time goes in v12:
time: 192 us
  blocking collectives  90.6 us (47%)
  waiting for transfers between devices  29.3 us (15%)
  matrix products  20.1 us (10%)
  starting transfers between devices  20.1 us (10%)
  local copies, waits for them, and re-layouts  18.7 us (10%)
  other arithmetic  12.2 us (6%)
    all_to_all x1, blocking collectives, on_device(): lax.all_to_all(outgoing, 'seq', split_axis=0, concat_axis=0, tiled=True)  55.9 us
    all_to_all x1, blocking collectives, on_device(): lax.all_to_all(jnp.broadcast_to(gain_term, (devices, channels)), ('scene'...  34.6 us
    ppermute x3, waiting for transfers between devices, on_device(): partial = partial + lax.ppermute(piece, 'scene', pairs).astype(f32)  14.3 us
    all_to_all x1, waiting for transfers between devices, on_device(): lax.all_to_all(back, 'seq', split_axis=0, concat_axis=0, tiled=True)  11.9 us
    ppermute x3, starting transfers between devices, on_device(): stage_two.append(lax.ppermute(piece, 'scene', pairs))  9.56 us
    reshape x2, local copies, waits for them, and re-layouts, on_device(): kernel_term.reshape(outer, inner, block_len // scene_parts, chunk, channels)  7.68 us
    all_to_all x1, starting transfers between devices, on_device(): lax.all_to_all(back, 'seq', split_axis=0, concat_axis=0, tiled=True)  5.52 us
    convert_element_type x1, other arithmetic, on_device(): weight_lo = (gate_weight - weight_hi.astype(f32)).astype(bf16)  5.15 us
  transfers between devices with their start and end apart: 7, of which 4 were waited for; matrix products, arithmetic and copies ran while one was open for 13% of the time, Pallas kernels for 0%

profile of v12, /device:TPU:1, one launch (start us, length us, event | category | flops | bytes accessed | tf_op | source)
XLA Modules:
  0.0 191.8 jit_solution(16795155182492463985)
XLA Ops:
  0.6 0.0 copy-start
  0.6 1.0 copy.61
  1.7 5.1 %subtract_convert_fusion = (bf16[1,4096,256]{2,1,0:T(8,128)(2,1)S(1)}, bf16[1,4096,256]{2,1,0:T(8,128)(2,1)S(1)}, bf16[1,4096,256]{2,1,0:T(8,128)(2,1)}) fusion(f32[256]{0:T(256)} %param.10, bf16[1,4096,256]{2,1,0:T(8,128)(2,1)} %param.9, bf16[1,4096,256]{2,1,0:T(8,128)(2,1)} %param.8), kind=kLoop, calls=%fused_computation.19 | loop fusion | flops 19922944 | bytes 10486784 | tf_op jit(solution)/shard_map/convert_element_type | solution.py:37
  6.8 0.7 convert_bitcast_fusion.1
  7.6 0.9 copy-done.5
  8.4 0.7 convert_bitcast_fusion.2
  9.2 0.4 pad_maximum_fusion
  9.6 0.5 copy.62
  10.1 55.9 %all_to_all.16 = bf16[16,2,1,16,16,256]{5,4,3,2,1,0:T(8,128)(2,1)S(1)} all-to-all(bf16[16,2,1,16,16,256]{5,4,3,2,1,0:T(8,128)(2,1)S(1)} %copy.62), channel_id=1, replica_groups=mesh['scene'=16,'seq'=16] {'seq'}, dimensions={0} | all-to-all | bytes 8388608 | tf_op jit(solution)/shard_map/all_to_all | solution.py:42
  66.1 0.4 copy.117
  66.5 0.0 copy-start.8
  66.5 0.3 fusion.48
  66.8 0.6 copy-done.8
  67.4 1.0 fusion.24
  68.4 0.0 copy-start.4
  68.5 3.2 %fusion.4 = (f32[1,256,16,256]{3,1,2,0:T(8,128)}, f32[16,256,256]{1,2,0:T(8,128)S(1)}) fusion(bf16[16,256,256]{1,2,0:T(8,128)(2,1)S(1)} %fusion.24, bf16[256,256]{1,0:T(8,128)(2,1)S(1)} %copy-done, bf16[256,16,256]{2,1,0:T(8,128)(2,1)S(1)} %bitcast.213), kind=kOutput, calls=%fused_computation.11 | convolution fusion | flops 538968064 | bytes 12713984 | tf_op jit(solution)/shard_map/pi,spjc->sijc/dot_general | solution.py:58
  71.6 1.2 fusion.27
  72.8 1.3 fusion.30
  74.1 1.2 copy.70
  75.3 1.2 copy.69
  76.5 2.4 %maximum_bitcast_fusion = bf16[16,1,2,16,16,256]{5,4,3,2,1,0:T(8,128)(2,1)} fusion(bf16[1,16,1,16,16,256]{5,4,3,2,1,0:T(8,128)(2,1)S(1)} %copy.70, bf16[1,16,1,16,16,256]{5,4,3,2,1,0:T(8,128)(2,1)S(1)} %copy.69), kind=kLoop, calls=%fused_computation.5 | loop fusion | flops 2097152 | bytes 8388608 | tf_op jit(solution)/shard_map/transpose | solution.py:101
  78.9 5.5 %all-to-all-start.1 = ((bf16[16,1,2,16,16,256]{5,4,3,2,1,0:T(8,128)(2,1)}), bf16[16,1,2,16,16,256]{5,4,3,2,1,0:T(8,128)(2,1)}, u32[]{:S(2)}, u32[]{:S(2)}) async-start(bf16[16,1,2,16,16,256]{5,4,3,2,1,0:T(8,128)(2,1)} %maximum_bitcast_fusion), calls=%async_computation.1 | async-start | bytes 8388608 | tf_op jit(solution)/shard_map/all_to_all | solution.py:102
  84.4 4.4 %copy.112 = bf16[4,4,16,16,256]{4,3,2,1,0:T(8,128)(2,1)S(1)} copy(f32[4,4,16,16,256]{4,2,1,0,3:T(8,128)} %bitcast.207) | data formatting | bytes 6291456 | tf_op jit(solution)/shard_map/reshape | solution.py:68
  88.8 1.1 dynamic-slice_bitcast_fusion.2
  90.0 1.3 collective-permute-start
  91.3 2.6 %collective-permute-start.1 = (bf16[4,16,16,256]{3,2,1,0:T(8,128)(2,1)}, bf16[4,16,16,256]{3,2,1,0:T(8,128)(2,1)}, u32[]{:S(2)}, u32[]{:S(2)}) collective-permute-start(bf16[4,16,16,256]{3,2,1,0:T(8,128)(2,1)} %get-tuple-element.31), channel_id=1, source_target_pairs={{0,128},{16,144},{32,160},{48,176},{64,192},{80,208},{96,224},{112... | collective-permute-start | bytes 1572872 | tf_op jit(solution)/shard_map/ppermute | solution.py:78
  93.9 1.1 collective-permute-start.2
  95.0 4.4 %fusion.49 = f32[16,256,16,16]{1,3,2,0:T(8,128)} fusion(bf16[16,256,256,1]{2,1,3,0:T(8,128)(2,1)} %bitcast.212, bf16[256,16,16,1]{0,2,1,3:T(8,128)(2,1)S(1)} %bitcast.220), kind=kOutput, calls=%fused_computation.68 | convolution fusion | flops 536870912 | bytes 6422528 | tf_op jit(solution)/shard_map/qJj,saqc->Jsajc/dot_general | solution.py:38
  99.4 3.3 %copy.73 = f32[4,4,16,16,256]{4,3,2,1,0:T(8,128)S(1)} copy(f32[4,4,16,16,256]{4,2,1,0,3:T(8,128)S(1)} %bitcast.208) | data formatting | bytes 8388608 | tf_op jit(solution)/shard_map/reshape | solution.py:68
  102.7 1.9 collective-permute-done
  104.6 12.3 %collective-permute-done.1 = bf16[4,16,16,256]{3,2,1,0:T(8,128)(2,1)} collective-permute-done((bf16[4,16,16,256]{3,2,1,0:T(8,128)(2,1)}, bf16[4,16,16,256]{3,2,1,0:T(8,128)(2,1)}, u32[]{:S(2)}, u32[]{:S(2)}) %collective-permute-start.1) | collective-permute-done | bytes 524320 | tf_op jit(solution)/shard_map/ppermute | solution.py:78
  116.9 1.7 fusion.45
  118.6 0.7 dynamic-slice_bitcast_fusion.3
  119.3 3.0 %collective-permute-start.3 = (bf16[16,16,256]{2,1,0:T(8,128)(2,1)}, bf16[16,16,256]{2,1,0:T(8,128)(2,1)}, u32[]{:S(2)}, u32[]{:S(2)}) collective-permute-start(bf16[16,16,256]{2,1,0:T(8,128)(2,1)} %get-tuple-element.34), channel_id=1, source_target_pairs={{0,16},{16,32},{32,48},{48,0},{64,80},{80,96},{96,112},{112,64},{1... | collective-permute-start | bytes 393224 | tf_op jit(solution)/shard_map/ppermute | solution.py:89
  122.3 4.2 %collective-permute-start.4 = (bf16[16,16,256]{2,1,0:T(8,128)(2,1)}, bf16[16,16,256]{2,1,0:T(8,128)(2,1)}, u32[]{:S(2)}, u32[]{:S(2)}) collective-permute-start(bf16[16,16,256]{2,1,0:T(8,128)(2,1)} %get-tuple-element.33), channel_id=1, source_target_pairs={{0,32},{16,48},{32,0},{48,16},{64,96},{80,112},{96,64},{112,80},{1... | collective-permute-start | bytes 393224 | tf_op jit(solution)/shard_map/ppermute | solution.py:89
  126.5 2.4 %collective-permute-start.5 = (bf16[16,16,256]{2,1,0:T(8,128)(2,1)S(1)}, bf16[16,16,256]{2,1,0:T(8,128)(2,1)}, u32[]{:S(2)}, u32[]{:S(2)}) collective-permute-start(bf16[16,16,256]{2,1,0:T(8,128)(2,1)S(1)} %get-tuple-element.32), channel_id=1, source_target_pairs={{0,48},{16,0},{32,16},{48,32},{64,112},{80,64},{96,80},{112,96},{1... | collective-permute-start | bytes 393224 | tf_op jit(solution)/shard_map/ppermute | solution.py:89
  128.9 11.9 %all-to-all-done.1 = bf16[16,1,2,16,16,256]{5,4,3,2,1,0:T(8,128)(2,1)} async-done(((bf16[16,1,2,16,16,256]{5,4,3,2,1,0:T(8,128)(2,1)}), bf16[16,1,2,16,16,256]{5,4,3,2,1,0:T(8,128)(2,1)}, u32[]{:S(2)}, u32[]{:S(2)}) %all-to-all-start.1) | async-done | bytes 4194336 | tf_op jit(solution)/shard_map/all_to_all | solution.py:102
  140.8 2.6 %fusion.47 = (bf16[16,1,1,16,16,256]{5,4,3,2,1,0:T(8,128)(2,1)S(1)}, bf16[16,1,1,16,16,256]{5,4,3,2,1,0:T(8,128)(2,1)S(1)}) fusion(bf16[16,1,2,16,16,256]{5,4,3,2,1,0:T(8,128)(2,1)} %all-to-all-done.1), kind=kLoop, calls=%fused_computation.66 | loop fusion | bytes 8388608 | tf_op jit(solution)/shard_map/slice | solution.py:112
  143.4 0.2 copy-done.6
  143.6 2.9 %fusion.5 = (bf16[1,16,256,256]{3,2,1,0:T(8,128)(2,1)}, f32[1,16,256,256]{3,2,1,0:T(8,128)S(1)}, f32[16,256,256,1]{1,2,3,0:T(8,128)S(1)}) fusion(f32[256]{0:T(256)S(1)} %copy-done.11, bf16[1,16,256,256]{3,2,1,0:T(8,128)(2,1)S(1)} %bitcast.215, bf16[256,16,16,1]{0,2,1,3:T(8,128)(2,1)S(1)} %bitcast.221, ...), kind=kOutput, calls=%fused_computation.14 | convolution fusion | flops 545259520 | bytes 14812160 | tf_op jit(solution)/shard_map/qJj,Jsajc->saqc/dot_general | solution.py:103
  146.5 3.4 %fusion.3 = bf16[1,16,256,256]{3,2,1,0:T(8,128)(2,1)} fusion(f32[16,256,256,1]{1,2,3,0:T(8,128)S(1)} %get-tuple-element.35, f32[1,16,256,256]{3,2,1,0:T(8,128)S(1)} %get-tuple-element.21, bf16[16,16,256,1]{2,1,0,3:T(8,128)(2,1)S(1)} %bitcast.225, bf16[16,1,1,16,16,256]{5,4,3,2,1,0:T(8,128)(2,1)S(1)} %get-tuple-element.25, f32[256]{0:T(256)S(1)} %copy-done.11, ...), kind=kOutput, calls=%fused_computation.9 | convolution fusion | flops 551550976 | bytes 14812160 | tf_op jit(solution)/shard_map/Jjb,Jsajc->sabc/dot_general | solution.py:112
  150.0 3.2 %collective-permute-done.4 = bf16[16,16,256]{2,1,0:T(8,128)(2,1)} collective-permute-done((bf16[16,16,256]{2,1,0:T(8,128)(2,1)}, bf16[16,16,256]{2,1,0:T(8,128)(2,1)}, u32[]{:S(2)}, u32[]{:S(2)}) %collective-permute-start.4) | collective-permute-done | bytes 131104 | tf_op jit(solution)/shard_map/ppermute | solution.py:89
  153.1 1.3 fusion.2
  154.4 1.8 fusion.39
  156.2 0.1 broadcast_in_dim.14
  156.3 34.6 %all_to_all.17 = f32[256,1,256]{2,1,0:T(1,128)S(1)} all-to-all(f32[256,1,256]{2,1,0:T(1,128)S(1)} %broadcast_in_dim.14), channel_id=1, replica_groups=mesh['scene'=16,'seq'=16] {'scene','seq'}, dimensions={0} | all-to-all | bytes 524288 | tf_op jit(solution)/shard_map/all_to_all | solution.py:122
  191.0 0.3 reduce_sum.20
  191.2 0.6 broadcast_multiply_fusion
  (21 shorter events, 0.0 us)
Async XLA Ops:
  0.6 67.8 %copy-start = (bf16[256,256]{1,0:T(8,128)(2,1)S(1)}, bf16[256,256]{1,0:T(8,128)(2,1)}, u32[]{:S(2)}) copy-start(bf16[256,256]{1,0:T(8,128)(2,1)} %param.14) | copy-start | bytes 393220
  6.8 1.6 copy-start.5
  6.8 1.6 copy-start.10
  66.5 0.9 copy-start.8
  68.4 3.2 %copy-start.4 = (bf16[256,16,256]{2,1,0:T(8,128)(2,1)S(1)}, bf16[256,16,256]{2,1,0:T(8,128)(2,1)}, u32[]{:S(2)}) copy-start(bf16[256,16,256]{2,1,0:T(8,128)(2,1)} %param.11) | copy-start | bytes 6291460
  78.9 61.9 %all-to-all-start.1 = ((bf16[16,1,2,16,16,256]{5,4,3,2,1,0:T(8,128)(2,1)}), bf16[16,1,2,16,16,256]{5,4,3,2,1,0:T(8,128)(2,1)}, u32[]{:S(2)}, u32[]{:S(2)}) async-start(bf16[16,1,2,16,16,256]{5,4,3,2,1,0:T(8,128)(2,1)} %maximum_bitcast_fusion), calls=%async_computation.1 | async-start | bytes 8388608 | tf_op jit(solution)/shard_map/all_to_all | solution.py:102
  90.0 14.6 %collective-permute-start = (bf16[4,16,16,256]{3,2,1,0:T(8,128)(2,1)}, bf16[4,16,16,256]{3,2,1,0:T(8,128)(2,1)S(1)}, u32[]{:S(2)}, u32[]{:S(2)}) collective-permute-start(bf16[4,16,16,256]{3,2,1,0:T(8,128)(2,1)} %get-tuple-element.29), channel_id=1, source_target_pairs={{0,64},{16,80},{32,96},{48,112},{64,128},{80,144},{96,160},{112,17... | collective-permute-start | bytes 1572872 | tf_op jit(solution)/shard_map/ppermute | solution.py:78
  91.3 25.6 %collective-permute-start.1 = (bf16[4,16,16,256]{3,2,1,0:T(8,128)(2,1)}, bf16[4,16,16,256]{3,2,1,0:T(8,128)(2,1)}, u32[]{:S(2)}, u32[]{:S(2)}) collective-permute-start(bf16[4,16,16,256]{3,2,1,0:T(8,128)(2,1)} %get-tuple-element.31), channel_id=1, source_target_pairs={{0,128},{16,144},{32,160},{48,176},{64,192},{80,208},{96,224},{112... | collective-permute-start | bytes 1572872 | tf_op jit(solution)/shard_map/ppermute | solution.py:78
  93.9 23.0 %collective-permute-start.2 = (bf16[4,16,16,256]{3,2,1,0:T(8,128)(2,1)S(1)}, bf16[4,16,16,256]{3,2,1,0:T(8,128)(2,1)}, u32[]{:S(2)}, u32[]{:S(2)}) collective-permute-start(bf16[4,16,16,256]{3,2,1,0:T(8,128)(2,1)S(1)} %get-tuple-element.30), channel_id=1, source_target_pairs={{0,192},{16,208},{32,224},{48,240},{64,0},{80,16},{96,32},{112,48}... | collective-permute-start | bytes 1572872 | tf_op jit(solution)/shard_map/ppermute | solution.py:78
  95.0 4.4 %copy-start.2 = (f32[1,256,16,256]{3,1,2,0:T(8,128)S(1)}, f32[1,256,16,256]{3,1,2,0:T(8,128)}, u32[]{:S(2)}) copy-start(f32[1,256,16,256]{3,1,2,0:T(8,128)} %get-tuple-element.36) | copy-start | bytes 12582916
  104.6 12.3 %copy-start.9 = (bf16[4,16,16,256]{3,2,1,0:T(8,128)(2,1)}, bf16[4,16,16,256]{3,2,1,0:T(8,128)(2,1)S(1)}, u32[]{:S(2)}) copy-start(bf16[4,16,16,256]{3,2,1,0:T(8,128)(2,1)S(1)} %collective-permute-done) | copy-start | bytes 1572868
  119.3 30.6 %collective-permute-start.3 = (bf16[16,16,256]{2,1,0:T(8,128)(2,1)}, bf16[16,16,256]{2,1,0:T(8,128)(2,1)}, u32[]{:S(2)}, u32[]{:S(2)}) collective-permute-start(bf16[16,16,256]{2,1,0:T(8,128)(2,1)} %get-tuple-element.34), channel_id=1, source_target_pairs={{0,16},{16,32},{32,48},{48,0},{64,80},{80,96},{96,112},{112,64},{1... | collective-permute-start | bytes 393224 | tf_op jit(solution)/shard_map/ppermute | solution.py:89
  122.3 30.8 %collective-permute-start.4 = (bf16[16,16,256]{2,1,0:T(8,128)(2,1)}, bf16[16,16,256]{2,1,0:T(8,128)(2,1)}, u32[]{:S(2)}, u32[]{:S(2)}) collective-permute-start(bf16[16,16,256]{2,1,0:T(8,128)(2,1)} %get-tuple-element.33), channel_id=1, source_target_pairs={{0,32},{16,48},{32,0},{48,16},{64,96},{80,112},{96,64},{112,80},{1... | collective-permute-start | bytes 393224 | tf_op jit(solution)/shard_map/ppermute | solution.py:89
  126.5 16.9 %copy-start.11 = (f32[256]{0:T(256)S(1)}, f32[256]{0:T(256)}, u32[]{:S(2)}) copy-start(f32[256]{0:T(256)} %param.10) | copy-start | bytes 3076
  126.5 26.6 %collective-permute-start.5 = (bf16[16,16,256]{2,1,0:T(8,128)(2,1)S(1)}, bf16[16,16,256]{2,1,0:T(8,128)(2,1)}, u32[]{:S(2)}, u32[]{:S(2)}) collective-permute-start(bf16[16,16,256]{2,1,0:T(8,128)(2,1)S(1)} %get-tuple-element.32), channel_id=1, source_target_pairs={{0,48},{16,0},{32,16},{48,32},{64,112},{80,64},{96,80},{112,96},{1... | collective-permute-start | bytes 393224 | tf_op jit(solution)/shard_map/ppermute | solution.py:89
  140.8 2.9 %copy-start.6 = (bf16[1,4096,256]{2,1,0:T(8,128)(2,1)S(1)}, bf16[1,4096,256]{2,1,0:T(8,128)(2,1)}, u32[]{:S(2)}) copy-start(bf16[1,4096,256]{2,1,0:T(8,128)(2,1)} %param.8) | copy-start | bytes 6291460
  143.6 2.9 %copy-start.7 = (bf16[1,4096,256]{2,1,0:T(8,128)(2,1)S(1)}, bf16[1,4096,256]{2,1,0:T(8,128)(2,1)}, u32[]{:S(2)}) copy-start(bf16[1,4096,256]{2,1,0:T(8,128)(2,1)} %param.9) | copy-start | bytes 6291460
  146.5 6.6 %copy-start.3 = (f32[16,256,16,16]{1,3,2,0:T(8,128)S(1)}, f32[16,256,16,16]{1,3,2,0:T(8,128)}, u32[]{:S(2)}) copy-start(f32[16,256,16,16]{1,3,2,0:T(8,128)} %fusion.49) | copy-start | bytes 12582916
  153.1 38.7 %copy-start.1 = (bf16[256,256]{1,0:T(8,128)(2,1)S(1)}, bf16[256,256]{1,0:T(8,128)(2,1)}, u32[]{:S(2)}) copy-start(bf16[256,256]{1,0:T(8,128)(2,1)} %param.14) | copy-start | bytes 393220

commit v13 on v5

--- a/solution.py
+++ b/solution.py
@@ -55,15 +55,16 @@
     inner = 4 if scene_parts % 4 == 0 else 1
     outer = scene_parts // inner
     scene_index = lax.axis_index("scene")
-    outer_index = scene_index // inner
-    inner_index = scene_index % inner
-    term_by_dest = kernel_term.reshape(outer, inner, block_len // scene_parts, chunk, channels)
+    outer_index = scene_index % outer
+    inner_index = scene_index // outer
+    term_by_dest = kernel_term.reshape(inner, outer, block_len // scene_parts, chunk, channels)
+    term_by_dest = jnp.swapaxes(term_by_dest, 0, 1)
     term_sent = term_by_dest.astype(bf16)
     partial = lax.dynamic_index_in_dim(term_by_dest, outer_index, 0, False)
     for shift in range(1, outer):
         piece = lax.dynamic_index_in_dim(term_sent, (outer_index + shift) % outer, 0, False)
         pairs = [
-            (o * inner + k, ((o + shift) % outer) * inner + k)
+            (k * outer + o, k * outer + (o + shift) % outer)
             for o in range(outer)
             for k in range(inner)
         ]
@@ -73,7 +74,7 @@
     for shift in range(1, inner):
         piece = lax.dynamic_index_in_dim(partial_sent, (inner_index + shift) % inner, 0, False)
         pairs = [
-            (o * inner + k, o * inner + (k + shift) % inner)
+            (k * outer + o, ((k + shift) % inner) * outer + o)
             for o in range(outer)
             for k in range(inner)
         ]

time: 189 us -> 231 us (1.22)
  waiting for transfers between devices: 36.9 us -> 76.9 us
    ppermute x3, waiting for transfers between devices: 16.5 us -> 68.3 us  [on_device(): partial = partial + lax.ppermute(piece, 'scene', pairs).astype(f32)]
    all_to_all x1, waiting for transfers between devices: 11.8 us -> 0.01 us  [on_device(): lax.all_to_all(back, 'seq', split_axis=0, concat_axis=0, tiled=True)]
    ppermute x3, starting transfers between devices: 9.58 us -> 4.43 us  [on_device(): kernel_grad = kernel_grad + lax.ppermute(piece, 'scene', pairs).astype(f32)]
    ppermute x3, starting transfers between devices: 5 us -> 9.56 us  [on_device(): partial = partial + lax.ppermute(piece, 'scene', pairs).astype(f32)]
    all_to_all x1, starting transfers between devices: 22.4 us -> 24.7 us  [on_device(): lax.all_to_all(jnp.broadcast_to(gain_term, (devices, channels)), ('scene'...]
    unnamed x21 -> x23, local copies, waits for them, and re-layouts: 3.74 us -> 4.62 us
  transfers between devices with their start and end apart: 8 -> 8, of which waited for: 4 -> 3; matrix products, arithmetic and copies ran while one was open for 16% -> 13% of each run, Pallas kernels for 0% -> 0%
where the time goes in v13:
time: 231 us; the launch traced here: 230 us
  waiting for transfers between devices  76.9 us (33%)
  blocking collectives  55.9 us (24%)
  starting transfers between devices  44.3 us (19%)
  local copies, waits for them, and re-layouts  25 us (11%)
  matrix products  18.6 us (8%)
  other arithmetic  9.01 us (4%)
    ppermute x3, waiting for transfers between devices, on_device(): partial = partial + lax.ppermute(piece, 'scene', pairs).astype(f32)  68.3 us
    all_to_all x1, blocking collectives, on_device(): lax.all_to_all(outgoing, 'seq', split_axis=0, concat_axis=0, tiled=True)  55.9 us
    all_to_all x1, starting transfers between devices, on_device(): lax.all_to_all(jnp.broadcast_to(gain_term, (devices, channels)), ('scene'...  24.7 us
    reshape x2, local copies, waits for them, and re-layouts, on_device(): kernel_term.reshape(inner, outer, block_len // scene_parts, chunk, channels)  9.86 us
    ppermute x3, starting transfers between devices, on_device(): partial = partial + lax.ppermute(piece, 'scene', pairs).astype(f32)  9.56 us
    all_to_all x1, waiting for transfers between devices, on_device(): lax.all_to_all(jnp.broadcast_to(gain_term, (devices, channels)), ('scene'...  8.58 us
    all_to_all x1, starting transfers between devices, on_device(): lax.all_to_all(back, 'seq', split_axis=0, concat_axis=0, tiled=True)  5.53 us
    dot_general x1, matrix products, on_device(): jnp.einsum('Jjb,Jsajc->sabc', mix_by_dest, returned[:, :, 1], preferred_e...  5.12 us
  transfers between devices with their start and end apart: 8, of which 3 were waited for; matrix products, arithmetic and copies ran while one was open for 13% of the time, Pallas kernels for 0%

profile of v13, /device:TPU:1, one launch (start us, length us, event | category | flops | bytes accessed | tf_op | source)
XLA Modules:
  0.0 230.5 jit_solution(4108395747728792040)
XLA Ops:
  0.6 0.0 copy-start
  0.6 1.0 copy.59
  1.7 0.0 copy-start.10
  1.7 2.5 %convert_bitcast_fusion.2 = bf16[16,1,1,16,16,256]{5,4,0,3,2,1:T(8,128)(2,1)S(1)} fusion(bf16[16,256,256,1]{2,1,3,0:T(8,128)(2,1)} %bitcast.184, bf16[16,16,256,1]{2,1,0,3:T(8,128)(2,1)} %bitcast.194), kind=kOutput, calls=%fused_computation.34 | convolution fusion | flops 537919488 | bytes 4325376 | tf_op jit(solution)/shard_map/Jjb,sabc->Jsajc/dot_general | solution.py:27
  4.2 0.4 copy-done.5
  4.6 1.4 multiply_convert_fusion
  6.0 0.7 convert_bitcast_fusion.1
  6.7 0.4 pad_maximum_fusion
  7.1 0.5 copy.60
  7.6 55.9 %all_to_all.16 = bf16[16,2,1,16,16,256]{5,4,3,2,1,0:T(8,128)(2,1)S(1)} all-to-all(bf16[16,2,1,16,16,256]{5,4,3,2,1,0:T(8,128)(2,1)S(1)} %copy.60), channel_id=1, replica_groups=mesh['scene'=16,'seq'=16] {'seq'}, dimensions={0} | all-to-all | bytes 8388608 | tf_op jit(solution)/shard_map/all_to_all | solution.py:34
  63.6 0.4 copy.110
  64.0 0.0 copy-start.7
  64.0 0.3 fusion.43
  64.3 0.6 copy-done.7
  64.9 1.0 fusion.21
  65.9 0.6 copy-done.4
  66.5 1.2 fusion.24
  67.7 1.2 copy.67
  68.9 3.2 %fusion.3 = (f32[1,256,16,256]{3,1,2,0:T(8,128)}, f32[16,256,256]{1,2,0:T(8,128)S(1)}) fusion(bf16[16,256,256]{1,2,0:T(8,128)(2,1)S(1)} %fusion.21, bf16[256,256]{1,0:T(8,128)(2,1)S(1)} %copy-done, bf16[256,16,256]{2,1,0:T(8,128)(2,1)S(1)} %bitcast.188), kind=kOutput, calls=%fused_computation.9 | convolution fusion | flops 538968064 | bytes 12713984 | tf_op jit(solution)/shard_map/pi,spjc->sijc/dot_general | solution.py:50
  72.1 1.3 fusion.27
  73.4 1.2 copy.68
  74.5 2.4 %maximum_bitcast_fusion = bf16[16,1,2,16,16,256]{5,4,3,2,1,0:T(8,128)(2,1)} fusion(bf16[1,16,1,16,16,256]{5,4,3,2,1,0:T(8,128)(2,1)S(1)} %copy.68, bf16[1,16,1,16,16,256]{5,4,3,2,1,0:T(8,128)(2,1)S(1)} %copy.67), kind=kLoop, calls=%fused_computation.5 | loop fusion | flops 2097152 | bytes 8388608 | tf_op jit(solution)/shard_map/transpose | solution.py:93
  76.9 5.5 %all-to-all-start.1 = ((bf16[16,1,2,16,16,256]{5,4,3,2,1,0:T(8,128)(2,1)}), bf16[16,1,2,16,16,256]{5,4,3,2,1,0:T(8,128)(2,1)}, u32[]{:S(2)}, u32[]{:S(2)}) async-start(bf16[16,1,2,16,16,256]{5,4,3,2,1,0:T(8,128)(2,1)} %maximum_bitcast_fusion), calls=%async_computation.1 | async-start | bytes 8388608 | tf_op jit(solution)/shard_map/all_to_all | solution.py:94
  82.4 4.4 %copy.105 = bf16[4,4,16,16,256]{4,3,2,0,1:T(8,128)(2,1)S(1)} copy(f32[4,4,16,16,256]{4,2,1,0,3:T(8,128)} %bitcast.182) | data formatting | bytes 6291456 | tf_op jit(solution)/shard_map/reshape | solution.py:60
  86.9 1.1 dynamic-slice_bitcast_fusion.2
  88.0 3.0 %collective-permute-start = (bf16[4,16,16,256]{3,2,1,0:T(8,128)(2,1)}, bf16[4,16,16,256]{3,2,1,0:T(8,128)(2,1)S(1)}, u32[]{:S(2)}, u32[]{:S(2)}) collective-permute-start(bf16[4,16,16,256]{3,2,1,0:T(8,128)(2,1)} %get-tuple-element.12), channel_id=1, source_target_pairs={{0,16},{64,80},{128,144},{192,208},{16,32},{80,96},{144,160},{208,... | collective-permute-start | bytes 1572872 | tf_op jit(solution)/shard_map/ppermute | solution.py:71
  91.0 2.1 collective-permute-start.2
  93.1 4.4 %collective-permute-start.1 = (bf16[4,16,16,256]{3,2,1,0:T(8,128)(2,1)S(1)}, bf16[4,16,16,256]{3,2,1,0:T(8,128)(2,1)}, u32[]{:S(2)}, u32[]{:S(2)}) collective-permute-start(bf16[4,16,16,256]{3,2,1,0:T(8,128)(2,1)S(1)} %get-tuple-element.14), channel_id=1, source_target_pairs={{0,32},{64,96},{128,160},{192,224},{16,48},{80,112},{144,176},{208... | collective-permute-start | bytes 1572872 | tf_op jit(solution)/shard_map/ppermute | solution.py:71
  97.6 5.4 %copy.71 = f32[4,4,16,16,256]{4,3,2,0,1:T(8,128)S(1)} copy(f32[4,4,16,16,256]{4,2,1,0,3:T(8,128)} %bitcast.183) | data formatting | bytes 8388608 | tf_op jit(solution)/shard_map/reshape | solution.py:60
  103.0 56.5 %collective-permute-done = bf16[4,16,16,256]{3,2,1,0:T(8,128)(2,1)S(1)} collective-permute-done((bf16[4,16,16,256]{3,2,1,0:T(8,128)(2,1)}, bf16[4,16,16,256]{3,2,1,0:T(8,128)(2,1)S(1)}, u32[]{:S(2)}, u32[]{:S(2)}) %collective-permute-start) | collective-permute-done | bytes 524320 | tf_op jit(solution)/shard_map/ppermute | solution.py:71
  159.5 0.8 copy-done.9
  160.3 11.8 %collective-permute-done.1 = bf16[4,16,16,256]{3,2,1,0:T(8,128)(2,1)} collective-permute-done((bf16[4,16,16,256]{3,2,1,0:T(8,128)(2,1)S(1)}, bf16[4,16,16,256]{3,2,1,0:T(8,128)(2,1)}, u32[]{:S(2)}, u32[]{:S(2)}) %collective-permute-start.1) | collective-permute-done | bytes 524320 | tf_op jit(solution)/shard_map/ppermute | solution.py:71
  172.1 1.7 fusion.40
  173.8 0.8 dynamic-slice_bitcast_fusion.5
  174.5 1.3 collective-permute-start.3
  175.9 1.5 collective-permute-start.5
  177.3 1.6 collective-permute-start.4
  179.0 4.0 %fusion.42 = (bf16[16,1,1,16,16,256]{5,4,3,2,1,0:T(8,128)(2,1)}, bf16[16,1,1,16,16,256]{5,4,3,2,1,0:T(8,128)(2,1)S(1)}) fusion(bf16[16,1,2,16,16,256]{5,4,3,2,1,0:T(8,128)(2,1)} %all-to-all-done.1), kind=kLoop, calls=%fused_computation.59 | loop fusion | bytes 8388608 | tf_op jit(solution)/shard_map/slice | solution.py:104
  183.0 3.6 %fusion.6 = (f32[1,16,256,256]{3,2,1,0:T(8,128)S(1)}, bf16[1,16,256,256]{3,2,1,0:T(8,128)(2,1)}) fusion(f32[256]{0:T(256)S(1)} %copy-done.10, bf16[1,4096,256]{2,1,0:T(8,128)(2,1)S(1)} %copy-done.2, bf16[256,16,16,1]{0,2,1,3:T(8,128)(2,1)S(1)} %bitcast.197, bf16[16,1,1,16,16,256]{5,4,3,2,1,0:T(8,128)(2,1)S(1)} %get-tuple-element.9, ...), kind=kOutput, calls=%fused_computation.14 | convolution fusion | flops 552599552 | bytes 12715008 | tf_op jit(solution)/shard_map/qJj,Jsajc->saqc/dot_general | solution.py:95
  186.7 0.7 multiply_reduce_fusion
  187.4 1.2 copy-done.3
  188.6 0.9 broadcast_in_dim.14
  189.4 24.7 %all-to-all-start.2 = ((f32[256,1,256]{2,1,0:T(1,128)}), f32[256,1,256]{2,1,0:T(1,128)S(1)}, u32[]{:S(2)}, u32[]{:S(2)}) async-start(f32[256,1,256]{2,1,0:T(1,128)} %broadcast_in_dim.14), calls=%async_computation.2 | async-start | bytes 524288 | tf_op jit(solution)/shard_map/all_to_all | solution.py:110
  214.2 1.7 fusion.35
  215.9 5.1 %fusion.2 = bf16[1,16,256,256]{3,2,1,0:T(8,128)(2,1)} fusion(f32[1,16,256,256]{3,2,1,0:T(8,128)} %copy-done.3, bf16[16,16,256,1]{2,1,0,3:T(8,128)(2,1)S(1)} %bitcast.195, bf16[16,1,1,16,16,256]{5,4,3,2,1,0:T(8,128)(2,1)} %get-tuple-element.8, f32[256]{0:T(256)S(1)} %copy-done.10), kind=kOutput, calls=%fused_computation.7 | convolution fusion | flops 540016640 | bytes 8520704 | tf_op jit(solution)/shard_map/Jjb,Jsajc->sabc/dot_general | solution.py:104
  221.0 8.6 %all-to-all-done.2 = f32[256,1,256]{2,1,0:T(1,128)S(1)} async-done(((f32[256,1,256]{2,1,0:T(1,128)}), f32[256,1,256]{2,1,0:T(1,128)S(1)}, u32[]{:S(2)}, u32[]{:S(2)}) %all-to-all-start.2) | async-done | bytes 262176 | tf_op jit(solution)/shard_map/all_to_all | solution.py:110
  229.6 0.3 reduce_sum.20
  229.9 0.6 broadcast_multiply_fusion
  (19 shorter events, 0.0 us)
Async XLA Ops:
  0.6 65.3 %copy-start = (bf16[256,256]{1,0:T(8,128)(2,1)S(1)}, bf16[256,256]{1,0:T(8,128)(2,1)}, u32[]{:S(2)}) copy-start(bf16[256,256]{1,0:T(8,128)(2,1)} %param.14) | copy-start | bytes 393220
  1.7 2.5 %copy-start.2 = (bf16[1,4096,256]{2,1,0:T(8,128)(2,1)S(1)}, bf16[1,4096,256]{2,1,0:T(8,128)(2,1)}, u32[]{:S(2)}) copy-start(bf16[1,4096,256]{2,1,0:T(8,128)(2,1)} %param.8) | copy-start | bytes 6291460
  1.7 2.9 %copy-start.5 = (bf16[1,4096,256]{2,1,0:T(8,128)(2,1)S(1)}, bf16[1,4096,256]{2,1,0:T(8,128)(2,1)}, u32[]{:S(2)}) copy-start(bf16[1,4096,256]{2,1,0:T(8,128)(2,1)} %param.9) | copy-start | bytes 6291460
  1.7 2.9 %copy-start.10 = (f32[256]{0:T(256)S(1)}, f32[256]{0:T(256)}, u32[]{:S(2)}) copy-start(f32[256]{0:T(256)} %param.10) | copy-start | bytes 3076
  64.0 0.9 copy-start.7
  64.9 1.6 copy-start.4
  76.9 102.0 %all-to-all-start.1 = ((bf16[16,1,2,16,16,256]{5,4,3,2,1,0:T(8,128)(2,1)}), bf16[16,1,2,16,16,256]{5,4,3,2,1,0:T(8,128)(2,1)}, u32[]{:S(2)}, u32[]{:S(2)}) async-start(bf16[16,1,2,16,16,256]{5,4,3,2,1,0:T(8,128)(2,1)} %maximum_bitcast_fusion), calls=%async_computation.1 | async-start | bytes 8388608 | tf_op jit(solution)/shard_map/all_to_all | solution.py:94
  88.0 71.5 %collective-permute-start = (bf16[4,16,16,256]{3,2,1,0:T(8,128)(2,1)}, bf16[4,16,16,256]{3,2,1,0:T(8,128)(2,1)S(1)}, u32[]{:S(2)}, u32[]{:S(2)}) collective-permute-start(bf16[4,16,16,256]{3,2,1,0:T(8,128)(2,1)} %get-tuple-element.12), channel_id=1, source_target_pairs={{0,16},{64,80},{128,144},{192,208},{16,32},{80,96},{144,160},{208,... | collective-permute-start | bytes 1572872 | tf_op jit(solution)/shard_map/ppermute | solution.py:71
  91.0 68.5 %collective-permute-start.2 = (bf16[4,16,16,256]{3,2,1,0:T(8,128)(2,1)}, bf16[4,16,16,256]{3,2,1,0:T(8,128)(2,1)}, u32[]{:S(2)}, u32[]{:S(2)}) collective-permute-start(bf16[4,16,16,256]{3,2,1,0:T(8,128)(2,1)} %get-tuple-element.13), channel_id=1, source_target_pairs={{0,48},{64,112},{128,176},{192,240},{16,0},{80,64},{144,128},{208,... | collective-permute-start | bytes 1572872 | tf_op jit(solution)/shard_map/ppermute | solution.py:71
  93.1 79.0 %collective-permute-start.1 = (bf16[4,16,16,256]{3,2,1,0:T(8,128)(2,1)S(1)}, bf16[4,16,16,256]{3,2,1,0:T(8,128)(2,1)}, u32[]{:S(2)}, u32[]{:S(2)}) collective-permute-start(bf16[4,16,16,256]{3,2,1,0:T(8,128)(2,1)S(1)} %get-tuple-element.14), channel_id=1, source_target_pairs={{0,32},{64,96},{128,160},{192,224},{16,48},{80,112},{144,176},{208... | collective-permute-start | bytes 1572872 | tf_op jit(solution)/shard_map/ppermute | solution.py:71
  159.5 0.8 copy-start.9
  174.5 39.7 %collective-permute-start.3 = (bf16[16,16,256]{2,1,0:T(8,128)(2,1)}, bf16[16,16,256]{2,1,0:T(8,128)(2,1)S(1)}, u32[]{:S(2)}, u32[]{:S(2)}) collective-permute-start(bf16[16,16,256]{2,1,0:T(8,128)(2,1)} %get-tuple-element.15), channel_id=1, source_target_pairs={{0,64},{64,128},{128,192},{192,0},{16,80},{80,144},{144,208},{208,... | collective-permute-start | bytes 393224 | tf_op jit(solution)/shard_map/ppermute | solution.py:81
  175.9 38.4 %collective-permute-start.5 = (bf16[16,16,256]{2,1,0:T(8,128)(2,1)}, bf16[16,16,256]{2,1,0:T(8,128)(2,1)S(1)}, u32[]{:S(2)}, u32[]{:S(2)}) collective-permute-start(bf16[16,16,256]{2,1,0:T(8,128)(2,1)} %get-tuple-element.16), channel_id=1, source_target_pairs={{0,192},{64,0},{128,64},{192,128},{16,208},{80,16},{144,80},{208,1... | collective-permute-start | bytes 393224 | tf_op jit(solution)/shard_map/ppermute | solution.py:81
  177.3 36.9 %collective-permute-start.4 = (bf16[16,16,256]{2,1,0:T(8,128)(2,1)}, bf16[16,16,256]{2,1,0:T(8,128)(2,1)}, u32[]{:S(2)}, u32[]{:S(2)}) collective-permute-start(bf16[16,16,256]{2,1,0:T(8,128)(2,1)} %get-tuple-element.17), channel_id=1, source_target_pairs={{0,128},{64,192},{128,0},{192,64},{16,144},{80,208},{144,16},{208,... | collective-permute-start | bytes 393224 | tf_op jit(solution)/shard_map/ppermute | solution.py:81
  179.0 4.1 %copy-start.6 = (bf16[1,4096,256]{2,1,0:T(8,128)(2,1)S(1)}, bf16[1,4096,256]{2,1,0:T(8,128)(2,1)}, u32[]{:S(2)}) copy-start(bf16[1,4096,256]{2,1,0:T(8,128)(2,1)} %param.9) | copy-start | bytes 6291460
  186.6 1.9 copy-start.3
  186.7 29.3 %copy-start.8 = (bf16[256,256]{1,0:T(8,128)(2,1)S(1)}, bf16[256,256]{1,0:T(8,128)(2,1)}, u32[]{:S(2)}) copy-start(bf16[256,256]{1,0:T(8,128)(2,1)} %param.12) | copy-start | bytes 393220
  189.4 40.2 %all-to-all-start.2 = ((f32[256,1,256]{2,1,0:T(1,128)}), f32[256,1,256]{2,1,0:T(1,128)S(1)}, u32[]{:S(2)}, u32[]{:S(2)}) async-start(f32[256,1,256]{2,1,0:T(1,128)} %broadcast_in_dim.14), calls=%async_computation.2 | async-start | bytes 524288 | tf_op jit(solution)/shard_map/all_to_all | solution.py:110
  215.9 14.6 %copy-start.1 = (bf16[256,256]{1,0:T(8,128)(2,1)S(1)}, bf16[256,256]{1,0:T(8,128)(2,1)}, u32[]{:S(2)}) copy-start(bf16[256,256]{1,0:T(8,128)(2,1)} %param.14) | copy-start | bytes 393220
